TPU v7x, 32 devices: a whole 2x2x4 slice. The times are simulated.
32 devices in a mesh: narrow: 4 (over y, core), wide: 8 (over z, x).
Axes of the slice: x: 2, y: 2, z: 4, core: 2. Of those that a mesh axis runs over, the one named last changes fastest.
Arguments:
- hidden_in: bfloat16 [256, 16384], P('narrow', 'wide'), may hold values from -6 to 6
- w_query: bfloat16 [16384, 8, 2048], P('wide', 'narrow'), may hold values from -0.046875 to 0.046875
- w_keyval: bfloat16 [16384, 8, 256], P('wide', 'narrow'), may hold values from -0.046875 to 0.046875
- w_out: bfloat16 [16384, 16384], P('narrow', 'wide'), may hold values from -0.125 to 0.125
- key_cache: bfloat16 [256, 8, 1024, 128], P('wide', 'narrow'), may hold values from -1300 to 1300
- value_cache: bfloat16 [256, 8, 1024, 128], P('wide', 'narrow'), may hold values from -6 to 6
- lengths: int32 [256], P('wide'), may hold values from 2 to 1024, as said below
Outputs:
- hidden_out: bfloat16 [256, 16384], P('narrow', 'wide')
Inputs may be any that keep to these rules, and one draw needn't show every extreme that they name: `lengths`: each row holds at least 2 cached tokens; some row holds exactly 1024.
All inputs are finite; a program needn't handle non-finite values.
Results may differ from a plain program's by a relative error of at most 0.019.
The roundings to bfloat16 on the way count: a program that leaves them out, or rounds other values in their place, can miss the bound.
Values may be sent and summed in bfloat16 or wider, within the bound.
No kernel may reach another device: no remote copies, remote signals or barrier semaphores. Data moves between devices by JAX's collectives and lax.ppermute only.
A program may use at most 192 MiB of HBM per device.

v0:
```python
import jax
import jax.numpy as jnp
from jax import lax
from jax.sharding import PartitionSpec as P

STEPS = 2


rope_base = 500000.0


def rope(values, position):
    half = values.shape[-1] // 2
    freq = rope_base ** (-2.0 * jnp.arange(half, dtype=jnp.float32) / values.shape[-1])
    angle = position.astype(jnp.float32)[:, None] * freq[None, :]
    shape = (angle.shape[0],) + (1,) * (values.ndim - 2) + (half,)
    cosine = jnp.cos(angle).reshape(shape)
    sine = jnp.sin(angle).reshape(shape)
    first = values[..., :half]
    second = values[..., half:]
    return jnp.concatenate(
        (first * cosine - second * sine, second * cosine + first * sine), axis=-1
    )


def collect(current):
    return lax.all_gather(current, "narrow", axis=0, tiled=True)


def settle(partial_value):
    return lax.psum_scatter(partial_value, "narrow", scatter_dimension=0, tiled=True)


def attend_step(every, step, w_both, w_out, key_cache, value_cache, lengths, new_keys, new_vals):
    local_rows = key_cache.shape[0]
    groups = key_cache.shape[1]
    slots = key_cache.shape[2]
    head_dim = key_cache.shape[3]
    per_group = w_both.shape[2] // head_dim - 2
    proj = lax.psum_scatter(
        jnp.einsum("rd,dgc->rgc", every, w_both, preferred_element_type=jnp.float32),
        "wide",
        scatter_dimension=0,
        tiled=True,
    )
    position = lengths + step
    query = rope(
        proj[:, :, : per_group * head_dim].reshape(local_rows, groups, per_group, head_dim),
        position,
    ).astype(jnp.bfloat16)
    new_keys.append(
        rope(proj[:, :, per_group * head_dim : (per_group + 1) * head_dim], position).astype(
            jnp.bfloat16
        )
    )
    new_vals.append(proj[:, :, (per_group + 1) * head_dim :].astype(jnp.bfloat16))
    keys_now = jnp.stack(new_keys, axis=2)
    vals_now = jnp.stack(new_vals, axis=2)
    scale = 1.0 / head_dim**0.5
    live = (jnp.arange(slots, dtype=jnp.int32)[None, :] < lengths[:, None])[:, None, None, :]
    cached = (
        jnp.einsum("rgjd,rgcd->rgjc", query, key_cache, preferred_element_type=jnp.float32) * scale
    )
    cached = jnp.where(live, cached, -1e30)
    fresh = (
        jnp.einsum("rgjd,rgsd->rgjs", query, keys_now, preferred_element_type=jnp.float32) * scale
    )
    top = jnp.maximum(jnp.max(cached, axis=-1), jnp.max(fresh, axis=-1))
    e_cached = jnp.where(live, jnp.exp(cached - top[..., None]), 0.0)
    e_fresh = jnp.exp(fresh - top[..., None])
    total = jnp.sum(e_cached, axis=-1) + jnp.sum(e_fresh, axis=-1)
    p_cached = (e_cached / total[..., None]).astype(jnp.bfloat16)
    p_fresh = (e_fresh / total[..., None]).astype(jnp.bfloat16)
    out = jnp.einsum("rgjc,rgcd->rgjd", p_cached, value_cache, preferred_element_type=jnp.float32)
    out = out + jnp.einsum("rgjs,rgsd->rgjd", p_fresh, vals_now, preferred_element_type=jnp.float32)
    attended = out.astype(jnp.bfloat16).reshape(local_rows, groups * per_group * head_dim)
    return jnp.dot(
        lax.all_gather(attended, "wide", axis=0, tiled=True),
        w_out,
        preferred_element_type=jnp.float32,
    )


def on_device(hidden_in, w_query, w_keyval, w_out, key_cache, value_cache, lengths):
    w_both = jnp.concatenate((w_query, w_keyval), axis=2)
    new_keys = []
    new_vals = []
    result = hidden_in
    for step in range(STEPS):
        partial_value = attend_step(
            collect(result),
            step,
            w_both,
            w_out,
            key_cache,
            value_cache,
            lengths,
            new_keys,
            new_vals,
        )
        result = (result.astype(jnp.float32) + settle(partial_value)).astype(jnp.bfloat16)
    return result


def solution(mesh):
    placed = (
        P("narrow", "wide"),
        P("wide", "narrow", None),
        P("wide", "narrow", None),
        P("narrow", "wide"),
        P("wide", "narrow", None, None),
        P("wide", "narrow", None, None),
        P("wide"),
    )
    return jax.shard_map(
        on_device, mesh=mesh, in_specs=placed, out_specs=P("narrow", "wide"), check_vma=False
    )
```

profile of v0, /device:TPU:0, one launch (start us, length us, event | category | flops | bytes accessed | tf_op | source)
XLA Modules:
  0.0 699.7 jit_solution(11210913646420502382)
XLA Ops:
  6.5 0.7 all-gather.5.cloned.1.call-update
  7.3 4.7 copy.51
  12.0 41.0 %copy.50 = bf16[2048,2,2048]{0,2,1:T(8,128)(2,1)} copy(bf16[2048,2,2048]{2,1,0:T(2,128)(2,1)} %param.8) | data formatting | bytes 33554432 | tf_op args[1]
  53.0 10.3 %fusion.2 = f32[256,2,2304]{0,2,1:T(8,128)} fusion(bf16[2048,2,256]{0,2,1:T(8,128)(2,1)S(1)} %copy.51, bf16[2048,2,2048]{0,2,1:T(8,128)(2,1)} %copy.50, bf16[256,2048]{1,0:T(8,128)(2,1)} %all-gather.5.cloned.1.call-done), kind=kOutput, calls=%fused_computation.3 | convolution fusion | flops 4869586944 | bytes 24641536 | tf_op jit(solution)/shard_map/rd,dgc->rgc/dot_general | solution.py:41
  63.4 8.1 %copy.52 = f32[256,2,2304]{2,1,0:T(2,128)} copy(f32[256,2,2304]{0,2,1:T(8,128)} %fusion.2) | data formatting | bytes 9437184 | tf_op jit(solution)/shard_map/rd,dgc->rgc/dot_general | solution.py:41
  71.6 0.6 copy-done.5
  72.2 0.6 dynamic-slice
  73.4 0.1 iota_compare_fusion
  73.5 0.2 multiply_cosine_fusion
  73.7 170.3 %all-reduce.5.cloned.1.call-done = f32[256,2,2304]{2,1,0:T(2,128)} async-done(((f32[256,2,2304]{2,1,0:T(2,128)}), f32[256,2,2304]{2,1,0:T(2,128)}) %all-reduce.5.cloned.1.call-update) | async-done | bytes 4718608
  244.0 1.0 subtract_convert_fusion.3
  245.1 1.3 constant_dynamic-slice_fusion.3
  246.4 1.1 constant_dynamic-slice_fusion.1
  247.5 0.4 reshape.315
  247.9 0.2 subtract_convert_fusion.1
  248.2 0.1 maximum_bitcast_fusion
  248.3 0.3 fusion.27
  248.6 12.2 %fusion.3 = (f32[32,2,16]{2,1,0:T(2,128)S(1)}, f32[32,2,16,1024]{3,2,1,0:T(8,128)}) fusion(pred[32,1024]{1,0:T(8,128)(4,1)S(1)} %iota_compare_fusion, bf16[32,2,1024,128]{3,2,1,0:T(8,128)(2,1)} %param.11, bf16[32,2,16,64]{3,2,1,0:T(8,128)(2,1)S(1)} %get-tuple-element.12, bf16[32,2,16,64]{3,2,1,0:T(8,128)(2,1)S(1)} %get-tuple-element.11), kind=kOutput, calls=%fused_computation.10 | convolution fusion | flops 272104448 | bytes 21270528 | tf_op jit(solution)/shard_map/rgjd,rgcd->rgjc/dot_general | solution.py:62
  260.9 3.8 fusion.5
  264.7 7.5 %fusion.22 = bf16[32,2,16,128]{3,2,1,0:T(8,128)(2,1)S(1)} fusion(bf16[32,2,1024,128]{3,2,1,0:T(8,128)(2,1)} %param.12, f32[32,2,16,1024]{3,2,1,0:T(8,128)S(1)} %copy-done.1, f32[32,2,16]{2,1,0:T(2,128)S(1)} %get-tuple-element.14, f32[32,2,16]{2,1,0:T(2,128)S(1)} %multiply_maximum_fusion, pred[32,1024]{1,0:T(8,128)(4,1)S(1)} %iota_compare_fusion, ...), kind=kOutput, calls=%fused_computation.30 | convolution fusion | flops 275120128 | bytes 21311488 | tf_op jit(solution)/shard_map/rgjc,rgcd->rgjd/dot_general | solution.py:74
  272.2 0.8 copy.91
  273.1 0.2 reduce-scatter.3.cloned.1.call-start
  273.3 48.2 %all-gather.7.cloned.1.call-done = bf16[256,4096]{1,0:T(8,128)(2,1)} async-done(((bf16[32,4096]{1,0:T(8,128)(2,1)}), bf16[256,4096]{1,0:T(8,128)(2,1)}) %all-gather.7.cloned.1.call-update) | async-done | bytes 2097168 | tf_op jit(solution)/shard_map/all_gather | solution.py:78
  321.5 12.2 %fusion.58 = f32[256,2048]{1,0:T(8,128)} fusion(bf16[256,4096]{1,0:T(8,128)(2,1)} %all-gather.7.cloned.1.call-done, bf16[4096,2048]{1,0:T(8,128)(2,1)} %param.10), kind=kOutput, calls=%fused_computation.101 | convolution fusion | flops 4294967296 | bytes 20971520 | tf_op jit(solution)/shard_map/dot_general | solution.py:77
  333.8 30.0 %reduce-scatter.3.cloned.1.call-done = f32[64,2048]{1,0:T(8,128)} async-done(((f32[256,2048]{1,0:T(8,128)}), f32[64,2048]{1,0:T(8,128)}) %reduce-scatter.3.cloned.1.call-update) | async-done | bytes 524304 | tf_op jit(solution)/shard_map/reduce_scatter | solution.py:31
  363.8 1.8 add_convert_fusion.2
  365.7 16.8 %all-gather.9.cloned.1.call-done = bf16[256,2048]{1,0:T(8,128)(2,1)} async-done(((bf16[64,2048]{1,0:T(8,128)(2,1)}), bf16[256,2048]{1,0:T(8,128)(2,1)}) %all-gather.9.cloned.1.call-update) | async-done | bytes 1048592 | tf_op jit(solution)/shard_map/all_gather | solution.py:27
  382.5 10.3 %fusion = f32[256,2,2304]{2,0,1:T(8,128)} fusion(bf16[2048,2,256]{0,2,1:T(8,128)(2,1)S(1)} %copy.51, bf16[2048,2,2048]{0,2,1:T(8,128)(2,1)} %copy.50, bf16[256,2048]{1,0:T(8,128)(2,1)} %all-gather.9.cloned.1.call-done), kind=kOutput, calls=%fused_computation.1 | convolution fusion | flops 4869586944 | bytes 24641536 | tf_op jit(solution)/shard_map/rd,dgc->rgc/dot_general | solution.py:41
  392.8 8.1 %copy.58 = f32[256,2,2304]{2,1,0:T(2,128)} copy(f32[256,2,2304]{2,0,1:T(8,128)} %fusion) | data formatting | bytes 9437184 | tf_op jit(solution)/shard_map/rd,dgc->rgc/dot_general | solution.py:41
  401.0 0.3 all-gather.11.cloned.1.call-start
  401.3 169.5 %all-reduce.7.cloned.1.call-done = f32[256,2,2304]{2,1,0:T(2,128)} async-done(((f32[256,2,2304]{2,1,0:T(2,128)}), f32[256,2,2304]{2,1,0:T(2,128)}) %all-reduce.7.cloned.1.call-update) | async-done | bytes 4718608
  570.8 1.0 fusion.39
  571.9 1.3 constant_dynamic-slice_fusion.2
  573.2 1.1 constant_dynamic-slice_fusion
  574.3 0.4 reshape.317
  574.7 0.2 subtract_convert_fusion
  575.0 12.3 %fusion.4 = (f32[32,2,16]{2,1,0:T(2,128)S(1)}, f32[32,2,16,1024]{3,2,1,0:T(8,128)}) fusion(pred[32,1024]{1,0:T(8,128)(4,1)S(1)} %iota_compare_fusion, bf16[32,2,1024,128]{3,2,1,0:T(8,128)(2,1)} %param.11, bf16[32,2,16,64]{3,2,1,0:T(8,128)(2,1)S(1)} %get-tuple-element.10, bf16[32,2,16,64]{3,2,1,0:T(8,128)(2,1)S(1)} %get-tuple-element.9), kind=kOutput, calls=%fused_computation.11 | convolution fusion | flops 272104448 | bytes 21270528 | tf_op jit(solution)/shard_map/rgjd,rgcd->rgjc/dot_general | solution.py:62
  587.2 0.1 maximum_maximum_fusion
  587.3 0.4 fusion.57
  587.7 0.1 fusion.29
  587.9 3.9 fusion.6
  591.8 7.3 %fusion.8 = f32[32,2,16,128]{3,2,1,0:T(8,128)S(1)} fusion(bf16[32,2,1024,128]{3,2,1,0:T(8,128)(2,1)} %param.12, f32[32,2,16,1024]{3,2,1,0:T(8,128)S(1)} %copy-done, f32[32,2,16]{2,1,0:T(2,128)S(1)} %add.59, f32[32,2,16]{2,1,0:T(2,128)S(1)} %max.13, pred[32,1024]{1,0:T(8,128)(4,1)S(1)} %iota_compare_fusion), kind=kOutput, calls=%fused_computation.15 | convolution fusion | flops 274726912 | bytes 21536768 | tf_op jit(solution)/shard_map/rgjc,rgcd->rgjd/dot_general | solution.py:74
  599.2 0.3 fusion.23
  599.5 0.8 copy.90
  600.3 48.4 %all-gather.11.cloned.1.call-done = bf16[256,4096]{1,0:T(8,128)(2,1)} async-done(((bf16[32,4096]{1,0:T(8,128)(2,1)}), bf16[256,4096]{1,0:T(8,128)(2,1)}) %all-gather.11.cloned.1.call-update) | async-done | bytes 2097168 | tf_op jit(solution)/shard_map/all_gather | solution.py:78
  648.7 12.2 %fusion.59 = f32[256,2048]{1,0:T(8,128)} fusion(bf16[256,4096]{1,0:T(8,128)(2,1)} %all-gather.11.cloned.1.call-done, bf16[4096,2048]{1,0:T(8,128)(2,1)} %param.10), kind=kOutput, calls=%fused_computation.102 | convolution fusion | flops 4294967296 | bytes 20971520 | tf_op jit(solution)/shard_map/dot_general | solution.py:77
  661.0 30.1 %reduce-scatter.5.cloned.1.call-done = f32[64,2048]{1,0:T(8,128)} async-done(((f32[256,2048]{1,0:T(8,128)}), f32[64,2048]{1,0:T(8,128)}) %reduce-scatter.5.cloned.1.call-update) | async-done | bytes 524304 | tf_op jit(solution)/shard_map/reduce_scatter | solution.py:31
  691.0 1.8 add_convert_fusion
  (44 shorter events, 0.6 us)
Async XLA Ops:
  6.5 46.5 %all-gather.5.cloned.1.call-start = ((), (), s32[]{:S(2)}) async-start(), calls=%async_computation.2 | async-start | bytes 1310720 | tf_op jit(solution)/shard_map/all_gather | solution.py:27
  7.3 236.8 %all-reduce.5.cloned.1.call-start = ((), (), s32[]{:S(2)}) async-start(), calls=%async_computation.8 | async-start | bytes 9437184
  71.5 0.7 copy-start.5
  71.5 1.9 copy-start.4
  71.5 250.0 %all-gather.7.cloned.1.call-start = ((), (), s32[]{:S(2)}) async-start(), calls=%async_computation.3 | async-start | bytes 2359296 | tf_op jit(solution)/shard_map/all_gather | solution.py:78
  260.8 3.9 copy-start.1
  273.0 90.8 %copy-start.3 = (bf16[64,2048]{1,0:T(8,128)(2,1)S(1)}, bf16[64,2048]{1,0:T(8,128)(2,1)}, u32[]{:S(2)}) copy-start(bf16[64,2048]{1,0:T(8,128)(2,1)} %param.7) | copy-start | bytes 786436
  273.1 90.8 %reduce-scatter.3.cloned.1.call-start = ((), (), s32[]{:S(2)}) async-start(), calls=%async_computation.4 | async-start | bytes 2621440 | tf_op jit(solution)/shard_map/reduce_scatter | solution.py:31
  333.7 48.8 %all-gather.9.cloned.1.call-start = ((), (), s32[]{:S(2)}) async-start(), calls=%async_computation.5 | async-start | bytes 1310720 | tf_op jit(solution)/shard_map/all_gather | solution.py:27
  365.6 205.1 %all-reduce.7.cloned.1.call-start = ((), (), s32[]{:S(2)}) async-start(), calls=%async_computation.9 | async-start | bytes 9437184
  401.0 247.8 %all-gather.11.cloned.1.call-start = ((), (), s32[]{:S(2)}) async-start(), calls=%async_computation.6 | async-start | bytes 2359296 | tf_op jit(solution)/shard_map/all_gather | solution.py:78
  587.2 4.6 copy-start
  600.3 90.8 %copy-start.2 = (bf16[64,2048]{1,0:T(8,128)(2,1)S(1)}, bf16[64,2048]{1,0:T(8,128)(2,1)}, u32[]{:S(2)}) copy-start(bf16[64,2048]{1,0:T(8,128)(2,1)} %add_convert_fusion.2) | copy-start | bytes 786436
  600.3 90.8 %reduce-scatter.5.cloned.1.call-start = ((), (), s32[]{:S(2)}) async-start(), calls=%async_computation.7 | async-start | bytes 2621440 | tf_op jit(solution)/shard_map/reduce_scatter | solution.py:31
Sparse Core Ops, SparseCore 0:
  8.9 19.4 all-gather.4
  71.6 172.3 all-reduce.4
  273.2 48.2 all-gather.6
  333.9 29.9 reduce-scatter.2
  365.8 16.6 all-gather.8
  401.1 169.6 all-reduce.6
  600.4 48.2 all-gather.10
  661.1 29.9 reduce-scatter.4
where the time goes:
time: 702 us; the launch traced here: 700 us
  waiting for transfers between devices  514 us (73%)
  matrix products  85.4 us (12%)
  local copies, waits for them, and re-layouts  70.4 us (10%)
  other arithmetic  14.5 us (2%)
  between operations  14.5 us (2%)
    unnamed x10, waiting for transfers between devices  341 us
    all_gather x2, waiting for transfers between devices, attend_step(): lax.all_gather(attended, 'wide', axis=0, tiled=True)  96.6 us
    reduce_scatter x2, waiting for transfers between devices, settle(): lax.psum_scatter(partial_value, 'narrow', scatter_dimension=0, tiled=True)  60.1 us
    unnamed x20, local copies, waits for them, and re-layouts  51 us
    dot_general x2, matrix products, attend_step(): jnp.einsum('rgjd,rgcd->rgjc', query, key_cache, preferred_element_type=jn...  24.5 us
    dot_general x2, matrix products, attend_step(): jnp.dot(lax.all_gather(attended, 'wide', axis=0, tiled=True), w_out, pref...  24.4 us
    dot_general x2, matrix products, attend_step(): jnp.einsum('rd,dgc->rgc', every, w_both, preferred_element_type=jnp.float32)  20.7 us
    all_gather x2, waiting for transfers between devices, collect(): return lax.all_gather(current, 'narrow', axis=0, tiled=True)  16.8 us
  transfers between devices with their start and end apart: 8, of which 7 were waited for; matrix products, arithmetic and copies ran while one was open for 7% of the time, Pallas kernels for 0%

commit v1 on v0

--- a/solution.py
+++ b/solution.py
@@ -23,37 +23,25 @@
     )
 
 
-def collect(current):
-    return lax.all_gather(current, "narrow", axis=0, tiled=True)
-
-
-def settle(partial_value):
-    return lax.psum_scatter(partial_value, "narrow", scatter_dimension=0, tiled=True)
-
-
-def attend_step(every, step, w_both, w_out, key_cache, value_cache, lengths, new_keys, new_vals):
+def attend_step(every, step, w_q2, w_kv2, w_out, key_cache, value_cache, lengths, new_keys, new_vals):
     local_rows = key_cache.shape[0]
     groups = key_cache.shape[1]
     slots = key_cache.shape[2]
     head_dim = key_cache.shape[3]
-    per_group = w_both.shape[2] // head_dim - 2
+    qcols = w_q2.shape[1]
+    per_group = qcols // (groups * head_dim)
+    part_q = jnp.dot(every, w_q2, preferred_element_type=jnp.float32)
+    part_kv = jnp.dot(every, w_kv2, preferred_element_type=jnp.float32)
     proj = lax.psum_scatter(
-        jnp.einsum("rd,dgc->rgc", every, w_both, preferred_element_type=jnp.float32),
-        "wide",
-        scatter_dimension=0,
-        tiled=True,
+        jnp.concatenate((part_q, part_kv), axis=1), "wide", scatter_dimension=0, tiled=True
     )
     position = lengths + step
     query = rope(
-        proj[:, :, : per_group * head_dim].reshape(local_rows, groups, per_group, head_dim),
-        position,
+        proj[:, :qcols].reshape(local_rows, groups, per_group, head_dim), position
     ).astype(jnp.bfloat16)
-    new_keys.append(
-        rope(proj[:, :, per_group * head_dim : (per_group + 1) * head_dim], position).astype(
-            jnp.bfloat16
-        )
-    )
-    new_vals.append(proj[:, :, (per_group + 1) * head_dim :].astype(jnp.bfloat16))
+    kv = proj[:, qcols:].reshape(local_rows, groups, 2 * head_dim)
+    new_keys.append(rope(kv[:, :, :head_dim], position).astype(jnp.bfloat16))
+    new_vals.append(kv[:, :, head_dim:].astype(jnp.bfloat16))
     keys_now = jnp.stack(new_keys, axis=2)
     vals_now = jnp.stack(new_vals, axis=2)
     scale = 1.0 / head_dim**0.5
@@ -82,15 +70,17 @@
 
 
 def on_device(hidden_in, w_query, w_keyval, w_out, key_cache, value_cache, lengths):
-    w_both = jnp.concatenate((w_query, w_keyval), axis=2)
+    w_q2 = w_query.reshape(w_query.shape[0], -1)
+    w_kv2 = w_keyval.reshape(w_keyval.shape[0], -1)
     new_keys = []
     new_vals = []
     result = hidden_in
     for step in range(STEPS):
         partial_value = attend_step(
-            collect(result),
+            lax.all_gather(result, "narrow", axis=0, tiled=True),
             step,
-            w_both,
+            w_q2,
+            w_kv2,
             w_out,
             key_cache,
             value_cache,
@@ -98,7 +88,8 @@
             new_keys,
             new_vals,
         )
-        result = (result.astype(jnp.float32) + settle(partial_value)).astype(jnp.bfloat16)
+        update = lax.psum_scatter(partial_value, "narrow", scatter_dimension=0, tiled=True)
+        result = (result.astype(jnp.float32) + update).astype(jnp.bfloat16)
     return result
 
 

time: 702 us -> 513 us (0.73)
  waiting for transfers between devices: 514 us -> 369 us
  local copies, waits for them, and re-layouts: 70.4 us -> 24.7 us
    unnamed x10 -> x8, waiting for transfers between devices: 341 us -> 0.82 us
    reduce_scatter x2 -> x4, waiting for transfers between devices: 60.1 us -> 250 us  [the longest x2 190 us: attend_step(): lax.psum_scatter(jnp.concatenate((part_q, part_kv), axis=1), 'wide', scat...]
    unnamed x20 -> x25, local copies, waits for them, and re-layouts: 51 us -> 22.6 us
    dot_general x2 -> x0, local copies, waits for them, and re-layouts: 16.3 us -> none  [attend_step(): jnp.einsum('rd,dgc->rgc', every, w_both, preferred_element_type=jnp.float32)]
    dot_general x2 -> x4, matrix products: 20.7 us -> 22.4 us  [the longest x2 21 us: attend_step(): part_q = jnp.dot(every, w_q2, preferred_element_type=jnp.float32)]
  transfers between devices with their start and end apart: 8 -> 8, of which waited for: 7 -> 8; matrix products, arithmetic and copies ran while one was open for 7% -> 4% of each run, Pallas kernels for 0% -> 0%
where the time goes in v1:
time: 513 us
  waiting for transfers between devices  369 us (72%)
  matrix products  87.3 us (17%)
  local copies, waits for them, and re-layouts  24.7 us (5%)
  other arithmetic  17.5 us (3%)
  between operations  13.9 us (3%)
    reduce_scatter x2, waiting for transfers between devices, attend_step(): lax.psum_scatter(jnp.concatenate((part_q, part_kv), axis=1), 'wide', scat...  190 us
    all_gather x2, waiting for transfers between devices, attend_step(): lax.all_gather(attended, 'wide', axis=0, tiled=True)  98.1 us
    reduce_scatter x2, waiting for transfers between devices, on_device(): lax.psum_scatter(partial_value, 'narrow', scatter_dimension=0, tiled=True)  60.1 us
    dot_general x2, matrix products, attend_step(): jnp.einsum('rgjd,rgcd->rgjc', query, key_cache, preferred_element_type=jn...  24.5 us
    dot_general x2, matrix products, attend_step(): jnp.dot(lax.all_gather(attended, 'wide', axis=0, tiled=True), w_out, pref...  24.4 us
    unnamed x25, local copies, waits for them, and re-layouts  22.6 us
    dot_general x2, matrix products, attend_step(): part_q = jnp.dot(every, w_q2, preferred_element_type=jnp.float32)  21 us
    all_gather x2, waiting for transfers between devices, on_device(): lax.all_gather(result, 'narrow', axis=0, tiled=True)  19.9 us
  transfers between devices with their start and end apart: 8, of which 8 were waited for; matrix products, arithmetic and copies ran while one was open for 4% of the time, Pallas kernels for 0%

profile of v1, /device:TPU:0, one launch (start us, length us, event | category | flops | bytes accessed | tf_op | source)
XLA Modules:
  0.0 512.6 jit_solution(17955221334297827772)
XLA Ops:
  6.5 0.7 all-gather.5.cloned.1.call-update
  7.3 17.5 %copy.59 = bf16[256,8,2,2048]{3,1,2,0:T(8,128)(2,1)} copy(bf16[256,8,2,2048]{3,2,1,0:T(2,128)(2,1)} %bitcast.57) | data formatting | bytes 33554432
  24.8 0.5 copy.60
  25.3 3.1 all-gather.5.cloned.1.call-done
  28.4 10.5 %fusion.59 = f32[256,4096]{1,0:T(8,128)S(1)} fusion(bf16[256,2048]{1,0:T(8,128)(2,1)} %all-gather.5.cloned.1.call-done, bf16[2048,4096]{1,0:T(8,128)(2,1)} %bitcast.58), kind=kOutput, calls=%fused_computation.100 | convolution fusion | flops 4294967296 | bytes 22020096 | tf_op jit(solution)/shard_map/dot_general | solution.py:33
  38.9 0.7 fusion.60
  39.6 2.5 pad_maximum_fusion
  42.2 0.6 copy-done.5
  42.8 0.1 iota_compare_fusion
  42.9 0.2 multiply_cosine_fusion
  43.1 94.6 %reduce-scatter.5.cloned.1.call-done = f32[32,4608]{1,0:T(8,128)} async-done(((f32[256,4608]{1,0:T(8,128)}), f32[32,4608]{1,0:T(8,128)}) %reduce-scatter.5.cloned.1.call-update) | async-done | bytes 589840 | tf_op jit(solution)/shard_map/reduce_scatter | solution.py:35
  137.7 0.8 slice.67
  138.6 0.1 fusion.57
  138.7 1.1 slice_bitcast_fusion.1
  139.8 0.1 copy.61
  139.9 0.2 subtract_convert_fusion.1
  140.1 0.1 maximum_bitcast_fusion
  140.2 0.3 fusion.22
  140.5 12.2 %fusion = (f32[32,2,16]{2,1,0:T(2,128)S(1)}, f32[32,2,16,1024]{3,2,1,0:T(8,128)}) fusion(pred[32,1024]{1,0:T(8,128)(4,1)S(1)} %iota_compare_fusion, bf16[32,2,1024,128]{3,2,1,0:T(8,128)(2,1)} %param.11, bf16[32,2,16,64]{3,2,1,0:T(8,128)(2,1)S(1)} %get-tuple-element.8, bf16[32,2,16,64]{3,2,1,0:T(8,128)(2,1)S(1)} %get-tuple-element.7), kind=kOutput, calls=%fused_computation.8 | convolution fusion | flops 272104448 | bytes 21270528 | tf_op jit(solution)/shard_map/rgjd,rgcd->rgjc/dot_general | solution.py:50
  152.8 3.8 fusion.2
  156.7 7.5 %fusion.19 = bf16[32,2,16,128]{3,2,1,0:T(8,128)(2,1)S(1)} fusion(bf16[32,2,1024,128]{3,2,1,0:T(8,128)(2,1)} %param.12, f32[32,2,16,1024]{3,2,1,0:T(8,128)S(1)} %copy-done.1, f32[32,2,16]{2,1,0:T(2,128)S(1)} %get-tuple-element.12, f32[32,2,16]{2,1,0:T(2,128)S(1)} %multiply_maximum_fusion, pred[32,1024]{1,0:T(8,128)(4,1)S(1)} %iota_compare_fusion, ...), kind=kOutput, calls=%fused_computation.28 | convolution fusion | flops 275120128 | bytes 21311488 | tf_op jit(solution)/shard_map/rgjc,rgcd->rgjd/dot_general | solution.py:62
  164.2 0.8 copy.94
  165.1 0.2 reduce-scatter.7.cloned.1.call-start
  165.3 49.0 %all-gather.7.cloned.1.call-done = bf16[256,4096]{1,0:T(8,128)(2,1)} async-done(((bf16[32,4096]{1,0:T(8,128)(2,1)}), bf16[256,4096]{1,0:T(8,128)(2,1)}) %all-gather.7.cloned.1.call-update) | async-done | bytes 2097168 | tf_op jit(solution)/shard_map/all_gather | solution.py:66
  214.3 12.2 %fusion.61 = f32[256,2048]{1,0:T(8,128)} fusion(bf16[256,4096]{1,0:T(8,128)(2,1)} %all-gather.7.cloned.1.call-done, bf16[4096,2048]{1,0:T(8,128)(2,1)} %param.10), kind=kOutput, calls=%fused_computation.102 | convolution fusion | flops 4294967296 | bytes 20971520 | tf_op jit(solution)/shard_map/dot_general | solution.py:65
  226.6 30.0 %reduce-scatter.7.cloned.1.call-done = f32[64,2048]{1,0:T(8,128)} async-done(((f32[256,2048]{1,0:T(8,128)}), f32[64,2048]{1,0:T(8,128)}) %reduce-scatter.7.cloned.1.call-update) | async-done | bytes 524304 | tf_op jit(solution)/shard_map/reduce_scatter | solution.py:91
  256.6 1.8 add_convert_fusion.2
  258.5 16.8 %all-gather.9.cloned.1.call-done = bf16[256,2048]{1,0:T(8,128)(2,1)} async-done(((bf16[64,2048]{1,0:T(8,128)(2,1)}), bf16[256,2048]{1,0:T(8,128)(2,1)}) %all-gather.9.cloned.1.call-update) | async-done | bytes 1048592 | tf_op jit(solution)/shard_map/all_gather | solution.py:80
  275.3 10.5 %fusion.62 = f32[256,4096]{1,0:T(8,128)S(1)} fusion(bf16[256,2048]{1,0:T(8,128)(2,1)} %all-gather.9.cloned.1.call-done, bf16[2048,4096]{1,0:T(8,128)(2,1)} %bitcast.59), kind=kOutput, calls=%fused_computation.103 | convolution fusion | flops 4294967296 | bytes 22020096 | tf_op jit(solution)/shard_map/dot_general | solution.py:33
  285.8 0.7 fusion.63
  286.5 2.5 pad_maximum_fusion.1
  289.2 95.3 %reduce-scatter.9.cloned.1.call-done = f32[32,4608]{1,0:T(8,128)} async-done(((f32[256,4608]{1,0:T(8,128)}), f32[32,4608]{1,0:T(8,128)}) %reduce-scatter.9.cloned.1.call-update) | async-done | bytes 589840 | tf_op jit(solution)/shard_map/reduce_scatter | solution.py:35
  384.5 0.8 slice.74
  385.4 0.1 fusion.56
  385.6 1.1 slice_bitcast_fusion
  386.7 0.1 copy.63
  386.8 0.2 subtract_convert_fusion
  387.0 12.2 %fusion.1 = (f32[32,2,16]{2,1,0:T(2,128)S(1)}, f32[32,2,16,1024]{3,2,1,0:T(8,128)}) fusion(pred[32,1024]{1,0:T(8,128)(4,1)S(1)} %iota_compare_fusion, bf16[32,2,1024,128]{3,2,1,0:T(8,128)(2,1)} %param.11, bf16[32,2,16,64]{3,2,1,0:T(8,128)(2,1)S(1)} %get-tuple-element.6, bf16[32,2,16,64]{3,2,1,0:T(8,128)(2,1)S(1)} %get-tuple-element.5), kind=kOutput, calls=%fused_computation.9 | convolution fusion | flops 272104448 | bytes 21270528 | tf_op jit(solution)/shard_map/rgjd,rgcd->rgjc/dot_general | solution.py:50
  399.3 0.5 fusion.58
  399.8 0.1 fusion.24
  400.0 4.0 fusion.3
  404.0 7.3 %fusion.5 = f32[32,2,16,128]{3,2,1,0:T(8,128)S(1)} fusion(bf16[32,2,1024,128]{3,2,1,0:T(8,128)(2,1)} %param.12, f32[32,2,16,1024]{3,2,1,0:T(8,128)S(1)} %copy-done, f32[32,2,16]{2,1,0:T(2,128)S(1)} %add.59, f32[32,2,16]{2,1,0:T(2,128)S(1)} %max.13, pred[32,1024]{1,0:T(8,128)(4,1)S(1)} %iota_compare_fusion), kind=kOutput, calls=%fused_computation.13 | convolution fusion | flops 274726912 | bytes 21536768 | tf_op jit(solution)/shard_map/rgjc,rgcd->rgjd/dot_general | solution.py:62
  411.3 0.3 fusion.20
  411.6 0.8 copy.93
  412.5 49.1 %all-gather.11.cloned.1.call-done = bf16[256,4096]{1,0:T(8,128)(2,1)} async-done(((bf16[32,4096]{1,0:T(8,128)(2,1)}), bf16[256,4096]{1,0:T(8,128)(2,1)}) %all-gather.11.cloned.1.call-update) | async-done | bytes 2097168 | tf_op jit(solution)/shard_map/all_gather | solution.py:66
  461.7 12.2 %fusion.64 = f32[256,2048]{1,0:T(8,128)} fusion(bf16[256,4096]{1,0:T(8,128)(2,1)} %all-gather.11.cloned.1.call-done, bf16[4096,2048]{1,0:T(8,128)(2,1)} %param.10), kind=kOutput, calls=%fused_computation.105 | convolution fusion | flops 4294967296 | bytes 20971520 | tf_op jit(solution)/shard_map/dot_general | solution.py:65
  473.9 30.1 %reduce-scatter.11.cloned.1.call-done = f32[64,2048]{1,0:T(8,128)} async-done(((f32[256,2048]{1,0:T(8,128)}), f32[64,2048]{1,0:T(8,128)}) %reduce-scatter.11.cloned.1.call-update) | async-done | bytes 524304 | tf_op jit(solution)/shard_map/reduce_scatter | solution.py:91
  504.0 1.8 add_convert_fusion
  (50 shorter events, 0.9 us)
Async XLA Ops:
  6.5 21.8 %all-gather.5.cloned.1.call-start = ((), (), s32[]{:S(2)}) async-start(), calls=%async_computation.4 | async-start | bytes 1310720 | tf_op jit(solution)/shard_map/all_gather | solution.py:80
  7.3 130.4 %reduce-scatter.5.cloned.1.call-start = ((), (), s32[]{:S(2)}) async-start(), calls=%async_computation.5 | async-start | bytes 5308416 | tf_op jit(solution)/shard_map/reduce_scatter | solution.py:35
  7.3 17.5 %copy-start.3 = (bf16[2048,2,256]{2,1,0:T(2,128)(2,1)S(1)}, bf16[2048,2,256]{2,1,0:T(2,128)(2,1)}, u32[]{:S(2)}) copy-start(bf16[2048,2,256]{2,1,0:T(2,128)(2,1)} %param.9) | copy-start | bytes 6291460
  28.4 10.5 %copy-start.6 = (bf16[256,2048]{1,0:T(8,128)(2,1)S(1)}, bf16[256,2048]{1,0:T(8,128)(2,1)}, u32[]{:S(2)}) copy-start(bf16[256,2048]{1,0:T(8,128)(2,1)} %all-gather.5.cloned.1.call-done) | copy-start | bytes 3145732
  42.1 0.7 copy-start.5
  42.2 172.1 %all-gather.7.cloned.1.call-start = ((), (), s32[]{:S(2)}) async-start(), calls=%async_computation.6 | async-start | bytes 2359296 | tf_op jit(solution)/shard_map/all_gather | solution.py:66
  152.8 3.9 copy-start.1
  165.0 91.6 %copy-start.4 = (bf16[64,2048]{1,0:T(8,128)(2,1)S(1)}, bf16[64,2048]{1,0:T(8,128)(2,1)}, u32[]{:S(2)}) copy-start(bf16[64,2048]{1,0:T(8,128)(2,1)} %param.7) | copy-start | bytes 786436
  165.1 91.5 %reduce-scatter.7.cloned.1.call-start = ((), (), s32[]{:S(2)}) async-start(), calls=%async_computation.7 | async-start | bytes 2621440 | tf_op jit(solution)/shard_map/reduce_scatter | solution.py:91
  226.5 48.8 %all-gather.9.cloned.1.call-start = ((), (), s32[]{:S(2)}) async-start(), calls=%async_computation.8 | async-start | bytes 1310720 | tf_op jit(solution)/shard_map/all_gather | solution.py:80
  258.4 126.1 %reduce-scatter.9.cloned.1.call-start = ((), (), s32[]{:S(2)}) async-start(), calls=%async_computation.9 | async-start | bytes 5308416 | tf_op jit(solution)/shard_map/reduce_scatter | solution.py:35
  275.3 10.5 %copy-start.7 = (bf16[256,2048]{1,0:T(8,128)(2,1)S(1)}, bf16[256,2048]{1,0:T(8,128)(2,1)}, u32[]{:S(2)}) copy-start(bf16[256,2048]{1,0:T(8,128)(2,1)} %all-gather.9.cloned.1.call-done) | copy-start | bytes 3145732
  289.1 172.6 %all-gather.11.cloned.1.call-start = ((), (), s32[]{:S(2)}) async-start(), calls=%async_computation.10 | async-start | bytes 2359296 | tf_op jit(solution)/shard_map/all_gather | solution.py:66
  399.3 4.7 copy-start
  412.5 91.5 %copy-start.2 = (bf16[64,2048]{1,0:T(8,128)(2,1)S(1)}, bf16[64,2048]{1,0:T(8,128)(2,1)}, u32[]{:S(2)}) copy-start(bf16[64,2048]{1,0:T(8,128)(2,1)} %add_convert_fusion.2) | copy-start | bytes 786436
  412.5 91.5 %reduce-scatter.11.cloned.1.call-start = ((), (), s32[]{:S(2)}) async-start(), calls=%async_computation.11 | async-start | bytes 2621440 | tf_op jit(solution)/shard_map/reduce_scatter | solution.py:91
Sparse Core Ops, SparseCore 0:
  8.9 19.4 all-gather.4
  42.3 95.3 reduce-scatter.4
  165.2 49.0 all-gather.6
  226.6 29.9 reduce-scatter.6
  258.5 16.6 all-gather.8
  289.2 95.2 reduce-scatter.8
  412.6 49.0 all-gather.10
  474.0 29.9 reduce-scatter.10

commit v2 on v1

--- a/solution.py
+++ b/solution.py
@@ -4,6 +4,7 @@
 from jax.sharding import PartitionSpec as P
 
 STEPS = 2
+CHUNKS = 2
 
 
 rope_base = 500000.0
@@ -23,18 +24,9 @@
     )
 
 
-def attend_step(every, step, w_q2, w_kv2, w_out, key_cache, value_cache, lengths, new_keys, new_vals):
-    local_rows = key_cache.shape[0]
-    groups = key_cache.shape[1]
-    slots = key_cache.shape[2]
-    head_dim = key_cache.shape[3]
-    qcols = w_q2.shape[1]
+def attend(proj, step, key_cache, value_cache, lengths, new_keys, new_vals, qcols):
+    local_rows, groups, slots, head_dim = key_cache.shape
     per_group = qcols // (groups * head_dim)
-    part_q = jnp.dot(every, w_q2, preferred_element_type=jnp.float32)
-    part_kv = jnp.dot(every, w_kv2, preferred_element_type=jnp.float32)
-    proj = lax.psum_scatter(
-        jnp.concatenate((part_q, part_kv), axis=1), "wide", scatter_dimension=0, tiled=True
-    )
     position = lengths + step
     query = rope(
         proj[:, :qcols].reshape(local_rows, groups, per_group, head_dim), position
@@ -61,36 +53,51 @@
     p_fresh = (e_fresh / total[..., None]).astype(jnp.bfloat16)
     out = jnp.einsum("rgjc,rgcd->rgjd", p_cached, value_cache, preferred_element_type=jnp.float32)
     out = out + jnp.einsum("rgjs,rgsd->rgjd", p_fresh, vals_now, preferred_element_type=jnp.float32)
-    attended = out.astype(jnp.bfloat16).reshape(local_rows, groups * per_group * head_dim)
-    return jnp.dot(
-        lax.all_gather(attended, "wide", axis=0, tiled=True),
-        w_out,
-        preferred_element_type=jnp.float32,
-    )
+    return out.astype(jnp.bfloat16).reshape(local_rows, groups * per_group * head_dim)
+
+
+def run_chunk(state, w_q2, w_kv2, w_out, key_cache, value_cache, lengths):
+    qcols = w_q2.shape[1]
+    new_keys = []
+    new_vals = []
+    for step in range(STEPS):
+        every = lax.all_gather(state, "narrow", axis=0, tiled=True)
+        part_q = jnp.dot(every, w_q2, preferred_element_type=jnp.float32)
+        part_kv = jnp.dot(every, w_kv2, preferred_element_type=jnp.float32)
+        proj = lax.psum_scatter(
+            jnp.concatenate((part_q, part_kv), axis=1), "wide", scatter_dimension=0, tiled=True
+        )
+        attended = attend(proj, step, key_cache, value_cache, lengths, new_keys, new_vals, qcols)
+        partial_value = jnp.dot(
+            lax.all_gather(attended, "wide", axis=0, tiled=True),
+            w_out,
+            preferred_element_type=jnp.float32,
+        )
+        update = lax.psum_scatter(partial_value, "narrow", scatter_dimension=0, tiled=True)
+        state = (state.astype(jnp.float32) + update).astype(jnp.bfloat16)
+    return state
 
 
 def on_device(hidden_in, w_query, w_keyval, w_out, key_cache, value_cache, lengths):
     w_q2 = w_query.reshape(w_query.shape[0], -1)
     w_kv2 = w_keyval.reshape(w_keyval.shape[0], -1)
-    new_keys = []
-    new_vals = []
-    result = hidden_in
-    for step in range(STEPS):
-        partial_value = attend_step(
-            lax.all_gather(result, "narrow", axis=0, tiled=True),
-            step,
-            w_q2,
-            w_kv2,
-            w_out,
-            key_cache,
-            value_cache,
-            lengths,
-            new_keys,
-            new_vals,
+    n_narrow = lax.axis_size("narrow")
+    n_wide = lax.axis_size("wide")
+    narrow_rows, cols = hidden_in.shape
+    cache_rows = key_cache.shape[0]
+    assert n_wide % n_narrow == 0 and cache_rows % CHUNKS == 0
+    per_narrow = n_wide // n_narrow
+    size = cache_rows // CHUNKS
+    blocks = hidden_in.reshape(per_narrow, CHUNKS, size, cols)
+    outs = []
+    for c in range(CHUNKS):
+        rows = slice(c * size, (c + 1) * size)
+        state = blocks[:, c].reshape(per_narrow * size, cols)
+        state = run_chunk(
+            state, w_q2, w_kv2, w_out, key_cache[rows], value_cache[rows], lengths[rows]
         )
-        update = lax.psum_scatter(partial_value, "narrow", scatter_dimension=0, tiled=True)
-        result = (result.astype(jnp.float32) + update).astype(jnp.bfloat16)
-    return result
+        outs.append(state.reshape(per_narrow, size, cols))
+    return jnp.stack(outs, axis=1).reshape(narrow_rows, cols)
 
 
 def solution(mesh):

time: 513 us -> 633 us (1.23); the launches traced: 513 us -> 626 us
  waiting for transfers between devices: 369 us -> 431 us
  blocking collectives: 0 us -> 29.5 us
  matrix products: 87.3 us -> 110 us
    reduce_scatter x4 -> x8, waiting for transfers between devices: 250 us -> 316 us  [the longest x4 247 us: run_chunk(): lax.psum_scatter(jnp.concatenate((part_q, part_kv), axis=1), 'wide', scat...]
    all_gather x0 -> x4, blocking collectives: none -> 29.5 us  [run_chunk(): every = lax.all_gather(state, 'narrow', axis=0, tiled=True)]
    dot_general x13 -> x26, matrix products: 87.3 us -> 110 us  [the longest x4 37.8 us: run_chunk(): jnp.dot(lax.all_gather(attended, 'wide', axis=0, tiled=True), w_out, pref...]
    unnamed x25 -> x26, local copies, waits for them, and re-layouts: 22.6 us -> 19.3 us
  transfers between devices with their start and end apart: 8 -> 12, of which waited for: 8 -> 12; matrix products, arithmetic and copies ran while one was open for 4% -> 16% of each run, Pallas kernels for 0% -> 0%
where the time goes in v2:
time: 633 us; the launch traced here: 626 us
  waiting for transfers between devices  431 us (68%)
  matrix products  110 us (17%)
  blocking collectives  29.5 us (5%)
  local copies, waits for them, and re-layouts  23.7 us (4%)
  other arithmetic  14.8 us (2%)
  between operations  14.6 us (2%)
    reduce_scatter x4, waiting for transfers between devices, run_chunk(): lax.psum_scatter(jnp.concatenate((part_q, part_kv), axis=1), 'wide', scat...  247 us
    all_gather x4, waiting for transfers between devices, run_chunk(): lax.all_gather(attended, 'wide', axis=0, tiled=True)  115 us
    reduce_scatter x4, waiting for transfers between devices, run_chunk(): lax.psum_scatter(partial_value, 'narrow', scatter_dimension=0, tiled=True)  68.9 us
    dot_general x4, matrix products, run_chunk(): jnp.dot(lax.all_gather(attended, 'wide', axis=0, tiled=True), w_out, pref...  37.8 us
    all_gather x4, blocking collectives, run_chunk(): every = lax.all_gather(state, 'narrow', axis=0, tiled=True)  29.5 us
    dot_general x4, matrix products, run_chunk(): part_q = jnp.dot(every, w_q2, preferred_element_type=jnp.float32)  27.5 us
    dot_general x4, matrix products, attend(): jnp.einsum('rgjd,rgcd->rgjc', query, key_cache, preferred_element_type=jn...  23.2 us
    unnamed x26, local copies, waits for them, and re-layouts  19.3 us
  transfers between devices with their start and end apart: 12, of which 12 were waited for; matrix products, arithmetic and copies ran while one was open for 16% of the time, Pallas kernels for 0%

profile of v2, /device:TPU:0, one launch (start us, length us, event | category | flops | bytes accessed | tf_op | source)
XLA Modules:
  0.0 625.6 jit_solution(4232706851031313489)
XLA Ops:
  6.5 12.3 %copy.130 = bf16[256,8,2,2048]{3,1,2,0:T(8,128)(2,1)S(1)} copy(bf16[256,8,2,2048]{3,2,1,0:T(2,128)(2,1)} %bitcast.122) | data formatting | bytes 33554432
  18.9 8.6 %all_gather.24 = bf16[128,2048]{1,0:T(8,128)(2,1)S(1)} all-gather(bf16[32,2048]{1,0:T(8,128)(2,1)S(1)} %bitcast.129), channel_id=1, replica_groups=mesh['narrow'=4,'wide'=8] {'narrow'}, dimensions={0}, use_global_device_ids=true | all-gather | bytes 655360 | tf_op jit(solution)/shard_map/all_gather | solution.py:64
  28.1 2.4 fusion.135
  31.0 1.6 pad_maximum_fusion
  32.6 7.3 %all_gather.28 = bf16[128,2048]{1,0:T(8,128)(2,1)S(1)} all-gather(bf16[32,2048]{1,0:T(8,128)(2,1)S(1)} %bitcast.128), channel_id=1, replica_groups=mesh['narrow'=4,'wide'=8] {'narrow'}, dimensions={0}, use_global_device_ids=true | all-gather | bytes 655360 | tf_op jit(solution)/shard_map/all_gather | solution.py:64
  40.4 8.2 %fusion.141 = f32[128,4096]{1,0:T(8,128)S(1)} fusion(bf16[128,2048]{1,0:T(8,128)(2,1)S(1)} %all_gather.28, bf16[2048,4096]{1,0:T(8,128)(2,1)} %bitcast.115), kind=kOutput, calls=%fused_computation.217 | convolution fusion | flops 2147483648 | bytes 19398656 | tf_op jit(solution)/shard_map/dot_general | solution.py:65
  48.6 1.6 pad_maximum_fusion.2
  51.2 51.4 %reduce-scatter.9.cloned.1.call-done = f32[16,4608]{1,0:T(8,128)} async-done(((f32[128,4608]{1,0:T(8,128)}), f32[16,4608]{1,0:T(8,128)}) %reduce-scatter.9.cloned.1.call-update) | async-done | bytes 294928 | tf_op jit(solution)/shard_map/reduce_scatter | solution.py:67
  103.5 70.6 %reduce-scatter.17.cloned.1.call-done = f32[16,4608]{1,0:T(8,128)} async-done(((f32[128,4608]{1,0:T(8,128)}), f32[16,4608]{1,0:T(8,128)}) %reduce-scatter.17.cloned.1.call-update) | async-done | bytes 294928 | tf_op jit(solution)/shard_map/reduce_scatter | solution.py:67
  175.0 1.0 slice_bitcast_fusion.3
  176.0 1.0 slice_bitcast_fusion.1
  177.6 5.8 fusion.16
  183.5 0.8 fusion.20
  184.3 4.9 fusion.35
  190.2 5.8 fusion.18
  196.2 0.8 fusion.22
  197.1 5.0 fusion.32
  202.8 26.6 %all-gather.5.cloned.1.call-done = bf16[128,4096]{1,0:T(8,128)(2,1)} async-done(((bf16[16,4096]{1,0:T(8,128)(2,1)}), bf16[128,4096]{1,0:T(8,128)(2,1)}) %all-gather.5.cloned.1.call-update) | async-done | bytes 1048592 | tf_op jit(solution)/shard_map/all_gather | solution.py:72
  229.4 9.5 %fusion.137 = f32[128,2048]{1,0:T(8,128)} fusion(bf16[128,4096]{1,0:T(8,128)(2,1)} %all-gather.5.cloned.1.call-done, bf16[4096,2048]{1,0:T(8,128)(2,1)} %param.10), kind=kOutput, calls=%fused_computation.213 | convolution fusion | flops 2147483648 | bytes 18874368 | tf_op jit(solution)/shard_map/dot_general | solution.py:71
  239.1 31.2 %all-gather.9.cloned.1.call-done = bf16[128,4096]{1,0:T(8,128)(2,1)} async-done(((bf16[16,4096]{1,0:T(8,128)(2,1)}), bf16[128,4096]{1,0:T(8,128)(2,1)}) %all-gather.9.cloned.1.call-update) | async-done | bytes 1048592 | tf_op jit(solution)/shard_map/all_gather | solution.py:72
  270.3 9.4 %fusion.143 = f32[128,2048]{1,0:T(8,128)} fusion(bf16[128,4096]{1,0:T(8,128)(2,1)} %all-gather.9.cloned.1.call-done, bf16[4096,2048]{1,0:T(8,128)(2,1)} %param.10), kind=kOutput, calls=%fused_computation.219 | convolution fusion | flops 2147483648 | bytes 18874368 | tf_op jit(solution)/shard_map/dot_general | solution.py:71
  279.8 16.5 %reduce-scatter.11.cloned.1.call-done = f32[32,2048]{1,0:T(8,128)} async-done(((f32[128,2048]{1,0:T(8,128)}), f32[32,2048]{1,0:T(8,128)}) %reduce-scatter.11.cloned.1.call-update) | async-done | bytes 262160 | tf_op jit(solution)/shard_map/reduce_scatter | solution.py:76
  296.4 1.0 add_convert_fusion.6
  297.3 6.8 %all_gather.26 = bf16[128,2048]{1,0:T(8,128)(2,1)S(1)} all-gather(bf16[32,2048]{1,0:T(8,128)(2,1)S(1)} %add_convert_fusion.6), channel_id=1, replica_groups=mesh['narrow'=4,'wide'=8] {'narrow'}, dimensions={0}, use_global_device_ids=true | all-gather | bytes 655360 | tf_op jit(solution)/shard_map/all_gather | solution.py:64
  304.6 8.5 %fusion.138 = f32[128,4096]{1,0:T(8,128)S(1)} fusion(bf16[128,2048]{1,0:T(8,128)(2,1)S(1)} %all_gather.26, bf16[2048,4096]{1,0:T(8,128)(2,1)} %bitcast.116), kind=kOutput, calls=%fused_computation.214 | convolution fusion | flops 2147483648 | bytes 19398656 | tf_op jit(solution)/shard_map/dot_general | solution.py:65
  313.1 1.6 pad_maximum_fusion.1
  314.8 9.1 %reduce-scatter.19.cloned.1.call-done = f32[32,2048]{1,0:T(8,128)} async-done(((f32[128,2048]{1,0:T(8,128)}), f32[32,2048]{1,0:T(8,128)}) %reduce-scatter.19.cloned.1.call-update) | async-done | bytes 262160 | tf_op jit(solution)/shard_map/reduce_scatter | solution.py:76
  323.8 1.0 add_convert_fusion.2
  324.8 6.8 %all_gather.30 = bf16[128,2048]{1,0:T(8,128)(2,1)S(1)} all-gather(bf16[32,2048]{1,0:T(8,128)(2,1)S(1)} %add_convert_fusion.2), channel_id=1, replica_groups=mesh['narrow'=4,'wide'=8] {'narrow'}, dimensions={0}, use_global_device_ids=true | all-gather | bytes 655360 | tf_op jit(solution)/shard_map/all_gather | solution.py:64
  332.0 8.4 %fusion.144 = f32[128,4096]{1,0:T(8,128)S(1)} fusion(bf16[128,2048]{1,0:T(8,128)(2,1)S(1)} %all_gather.30, bf16[2048,4096]{1,0:T(8,128)(2,1)} %bitcast.117), kind=kOutput, calls=%fused_computation.220 | convolution fusion | flops 2147483648 | bytes 19398656 | tf_op jit(solution)/shard_map/dot_general | solution.py:65
  340.4 1.6 pad_maximum_fusion.3
  342.4 53.9 %reduce-scatter.13.cloned.1.call-done = f32[16,4608]{1,0:T(8,128)} async-done(((f32[128,4608]{1,0:T(8,128)}), f32[16,4608]{1,0:T(8,128)}) %reduce-scatter.13.cloned.1.call-update) | async-done | bytes 294928 | tf_op jit(solution)/shard_map/reduce_scatter | solution.py:67
  397.3 70.7 %reduce-scatter.21.cloned.1.call-done = f32[16,4608]{1,0:T(8,128)} async-done(((f32[128,4608]{1,0:T(8,128)}), f32[16,4608]{1,0:T(8,128)}) %reduce-scatter.21.cloned.1.call-update) | async-done | bytes 294928 | tf_op jit(solution)/shard_map/reduce_scatter | solution.py:67
  469.0 1.0 slice_bitcast_fusion.2
  470.1 5.8 fusion.17
  476.4 0.8 fusion.21
  477.2 4.3 fusion.8
  482.8 5.8 fusion.19
  489.1 0.8 fusion.23
  489.9 4.3 fusion
  495.3 26.6 %all-gather.7.cloned.1.call-done = bf16[128,4096]{1,0:T(8,128)(2,1)} async-done(((bf16[16,4096]{1,0:T(8,128)(2,1)}), bf16[128,4096]{1,0:T(8,128)(2,1)}) %all-gather.7.cloned.1.call-update) | async-done | bytes 1048592 | tf_op jit(solution)/shard_map/all_gather | solution.py:72
  521.9 9.5 %fusion.140 = f32[128,2048]{1,0:T(8,128)} fusion(bf16[128,4096]{1,0:T(8,128)(2,1)} %all-gather.7.cloned.1.call-done, bf16[4096,2048]{1,0:T(8,128)(2,1)} %param.10), kind=kOutput, calls=%fused_computation.216 | convolution fusion | flops 2147483648 | bytes 18874368 | tf_op jit(solution)/shard_map/dot_general | solution.py:71
  531.7 31.1 %all-gather.11.cloned.1.call-done = bf16[128,4096]{1,0:T(8,128)(2,1)} async-done(((bf16[16,4096]{1,0:T(8,128)(2,1)}), bf16[128,4096]{1,0:T(8,128)(2,1)}) %all-gather.11.cloned.1.call-update) | async-done | bytes 1048592 | tf_op jit(solution)/shard_map/all_gather | solution.py:72
  562.8 9.4 %fusion.146 = f32[128,2048]{1,0:T(8,128)} fusion(bf16[128,4096]{1,0:T(8,128)(2,1)} %all-gather.11.cloned.1.call-done, bf16[4096,2048]{1,0:T(8,128)(2,1)} %param.10), kind=kOutput, calls=%fused_computation.222 | convolution fusion | flops 2147483648 | bytes 18874368 | tf_op jit(solution)/shard_map/dot_general | solution.py:71
  572.2 16.8 %reduce-scatter.15.cloned.1.call-done = f32[32,2048]{1,0:T(8,128)} async-done(((f32[128,2048]{1,0:T(8,128)}), f32[32,2048]{1,0:T(8,128)}) %reduce-scatter.15.cloned.1.call-update) | async-done | bytes 262160 | tf_op jit(solution)/shard_map/reduce_scatter | solution.py:76
  589.1 1.0 add_convert_fusion.4
  590.0 26.5 %reduce-scatter.23.cloned.1.call-done = f32[32,2048]{1,0:T(8,128)} async-done(((f32[128,2048]{1,0:T(8,128)}), f32[32,2048]{1,0:T(8,128)}) %reduce-scatter.23.cloned.1.call-update) | async-done | bytes 262160 | tf_op jit(solution)/shard_map/reduce_scatter | solution.py:76
  616.5 1.0 add_convert_fusion
  (113 shorter events, 14.9 us)
Async XLA Ops:
  6.5 96.1 %reduce-scatter.9.cloned.1.call-start = ((), (), s32[]{:S(2)}) async-start(), calls=%async_computation.8 | async-start | bytes 2654208 | tf_op jit(solution)/shard_map/reduce_scatter | solution.py:67
  6.5 12.4 %copy-start.3 = (bf16[64,2048]{1,0:T(8,128)(2,1)S(1)}, bf16[64,2048]{1,0:T(8,128)(2,1)}, u32[]{:S(2)}) copy-start(bf16[64,2048]{1,0:T(8,128)(2,1)} %param.7) | copy-start | bytes 786436
  6.5 21.1 %copy-start.1 = (bf16[2048,2,256]{2,1,0:T(2,128)(2,1)S(1)}, bf16[2048,2,256]{2,1,0:T(2,128)(2,1)}, u32[]{:S(2)}) copy-start(bf16[2048,2,256]{2,1,0:T(2,128)(2,1)} %param.9) | copy-start | bytes 6291460
  18.9 11.6 %copy-start = (bf16[256,8,2,2048]{3,1,2,0:T(8,128)(2,1)}, bf16[256,8,2,2048]{3,1,2,0:T(8,128)(2,1)S(1)}, u32[]{:S(2)}) copy-start(bf16[256,8,2,2048]{3,1,2,0:T(8,128)(2,1)S(1)} %copy.130) | copy-start | bytes 50331652
  32.6 141.5 %reduce-scatter.17.cloned.1.call-start = ((), (), s32[]{:S(2)}) async-start(), calls=%async_computation.14 | async-start | bytes 2654208 | tf_op jit(solution)/shard_map/reduce_scatter | solution.py:67
  50.2 0.7 copy-start.4
  50.2 179.2 %all-gather.5.cloned.1.call-start = ((), (), s32[]{:S(2)}) async-start(), calls=%async_computation.9 | async-start | bytes 1179648 | tf_op jit(solution)/shard_map/all_gather | solution.py:72
  190.0 80.3 %all-gather.9.cloned.1.call-start = ((), (), s32[]{:S(2)}) async-start(), calls=%async_computation.15 | async-start | bytes 1179648 | tf_op jit(solution)/shard_map/all_gather | solution.py:72
  202.8 93.6 %reduce-scatter.11.cloned.1.call-start = ((), (), s32[]{:S(2)}) async-start(), calls=%async_computation.10 | async-start | bytes 1310720 | tf_op jit(solution)/shard_map/reduce_scatter | solution.py:76
  238.9 84.9 %reduce-scatter.19.cloned.1.call-start = ((), (), s32[]{:S(2)}) async-start(), calls=%async_computation.16 | async-start | bytes 1310720 | tf_op jit(solution)/shard_map/reduce_scatter | solution.py:76
  279.8 116.6 %reduce-scatter.13.cloned.1.call-start = ((), (), s32[]{:S(2)}) async-start(), calls=%async_computation.11 | async-start | bytes 2654208 | tf_op jit(solution)/shard_map/reduce_scatter | solution.py:67
  314.7 153.3 %reduce-scatter.21.cloned.1.call-start = ((), (), s32[]{:S(2)}) async-start(), calls=%async_computation.17 | async-start | bytes 2654208 | tf_op jit(solution)/shard_map/reduce_scatter | solution.py:67
  342.0 179.9 %all-gather.7.cloned.1.call-start = ((), (), s32[]{:S(2)}) async-start(), calls=%async_computation.12 | async-start | bytes 1179648 | tf_op jit(solution)/shard_map/all_gather | solution.py:72
  477.2 5.4 copy-start.2
  482.5 80.3 %all-gather.11.cloned.1.call-start = ((), (), s32[]{:S(2)}) async-start(), calls=%async_computation.18 | async-start | bytes 1179648 | tf_op jit(solution)/shard_map/all_gather | solution.py:72
  495.2 93.8 %reduce-scatter.15.cloned.1.call-start = ((), (), s32[]{:S(2)}) async-start(), calls=%async_computation.13 | async-start | bytes 1310720 | tf_op jit(solution)/shard_map/reduce_scatter | solution.py:76
  531.3 85.2 %reduce-scatter.23.cloned.1.call-start = ((), (), s32[]{:S(2)}) async-start(), calls=%async_computation.19 | async-start | bytes 1310720 | tf_op jit(solution)/shard_map/reduce_scatter | solution.py:76
Sparse Core Ops, SparseCore 0:
  32.7 69.8 reduce-scatter.8
  106.1 67.9 reduce-scatter.16
  190.1 39.2 all-gather.4
  231.4 38.8 all-gather.8
  272.7 23.6 reduce-scatter.10
  298.9 24.8 reduce-scatter.18
  327.3 69.0 reduce-scatter.12
  399.9 68.0 reduce-scatter.20
  482.6 39.1 all-gather.6
  523.8 38.8 all-gather.10
  565.3 23.7 reduce-scatter.14
  591.6 24.8 reduce-scatter.22

commit v3 on v1

--- a/solution.py
+++ b/solution.py
@@ -1,3 +1,5 @@
+import functools
+
 import jax
 import jax.numpy as jnp
 from jax import lax
@@ -23,7 +25,55 @@
     )
 
 
-def attend_step(every, step, w_q2, w_kv2, w_out, key_cache, value_cache, lengths, new_keys, new_vals):
+def line_scatter(blocks, pos, length, pairs):
+    if length == 1:
+        return blocks[0]
+    right = None
+    left = None
+    for t in range(length - 1):
+        b_right = jnp.clip(pos + length - 1 - t, 0, length - 1)
+        b_left = jnp.clip(t + pos - length + 1, 0, length - 1)
+        send_right = lax.dynamic_index_in_dim(blocks, b_right, 0, keepdims=False)
+        send_left = lax.dynamic_index_in_dim(blocks, b_left, 0, keepdims=False)
+        if t > 0:
+            send_right = send_right + right
+            send_left = send_left + left
+        right = lax.ppermute(send_right, "wide", pairs(t, 1))
+        left = lax.ppermute(send_left, "wide", pairs(t, -1))
+    own = lax.dynamic_index_in_dim(blocks, pos, 0, keepdims=False)
+    return own + right + left
+
+
+def wide_scatter(value, n_x):
+    n_wide = lax.axis_size("wide")
+    n_z = n_wide // n_x
+    w = lax.axis_index("wide")
+    zpos = w // n_x
+    xpos = w % n_x
+
+    def x_pairs(t, d):
+        if d > 0:
+            return [(z * n_x + j, z * n_x + j + 1) for z in range(n_z) for j in range(min(t + 1, n_x - 1))]
+        return [(z * n_x + j, z * n_x + j - 1) for z in range(n_z) for j in range(max(1, n_x - 1 - t), n_x)]
+
+    def z_pairs(t, d):
+        if d > 0:
+            return [(j * n_x + x, (j + 1) * n_x + x) for x in range(n_x) for j in range(min(t + 1, n_z - 1))]
+        return [(j * n_x + x, (j - 1) * n_x + x) for x in range(n_x) for j in range(max(1, n_z - 1 - t), n_z)]
+
+    rows, cols = value.shape
+    size = rows // n_wide
+    half = cols // 2
+    first = value[:, :half].reshape(n_z, n_x, size, half)
+    second = value[:, half:].reshape(n_z, n_x, size, cols - half)
+    a = line_scatter(jnp.swapaxes(first, 0, 1), xpos, n_x, x_pairs)
+    a = line_scatter(a, zpos, n_z, z_pairs)
+    b = line_scatter(second, zpos, n_z, z_pairs)
+    b = line_scatter(b, xpos, n_x, x_pairs)
+    return jnp.concatenate((a, b), axis=1)
+
+
+def attend_step(every, step, w_q2, w_kv2, w_out, key_cache, value_cache, lengths, new_keys, new_vals, n_x):
     local_rows = key_cache.shape[0]
     groups = key_cache.shape[1]
     slots = key_cache.shape[2]
@@ -32,9 +82,7 @@
     per_group = qcols // (groups * head_dim)
     part_q = jnp.dot(every, w_q2, preferred_element_type=jnp.float32)
     part_kv = jnp.dot(every, w_kv2, preferred_element_type=jnp.float32)
-    proj = lax.psum_scatter(
-        jnp.concatenate((part_q, part_kv), axis=1), "wide", scatter_dimension=0, tiled=True
-    )
+    proj = wide_scatter(jnp.concatenate((part_q, part_kv), axis=1), n_x)
     position = lengths + step
     query = rope(
         proj[:, :qcols].reshape(local_rows, groups, per_group, head_dim), position
@@ -69,7 +117,7 @@
     )
 
 
-def on_device(hidden_in, w_query, w_keyval, w_out, key_cache, value_cache, lengths):
+def on_device(hidden_in, w_query, w_keyval, w_out, key_cache, value_cache, lengths, n_x=1):
     w_q2 = w_query.reshape(w_query.shape[0], -1)
     w_kv2 = w_keyval.reshape(w_keyval.shape[0], -1)
     new_keys = []
@@ -87,10 +135,20 @@
             lengths,
             new_keys,
             new_vals,
+            n_x,
         )
         update = lax.psum_scatter(partial_value, "narrow", scatter_dimension=0, tiled=True)
         result = (result.astype(jnp.float32) + update).astype(jnp.bfloat16)
     return result
+
+
+def x_size(mesh):
+    n_wide = mesh.shape["wide"]
+    coords = [getattr(d, "coords", None) for d in mesh.devices.flat]
+    if any(c is None for c in coords):
+        return 1
+    n_x = len({c[0] for c in coords})
+    return n_x if n_wide % n_x == 0 else 1
 
 
 def solution(mesh):
@@ -103,6 +161,7 @@
         P("wide", "narrow", None, None),
         P("wide"),
     )
+    n_x = x_size(mesh)
     return jax.shard_map(
-        on_device, mesh=mesh, in_specs=placed, out_specs=P("narrow", "wide"), check_vma=False
+        functools.partial(on_device, n_x=n_x), mesh=mesh, in_specs=placed, out_specs=P("narrow", "wide"), check_vma=False
     )

time: 513 us -> 523 us (1.019)
  starting transfers between devices: 0.47 us -> 94.1 us
  waiting for transfers between devices: 369 us -> 284 us
    reduce_scatter x2 -> x0, waiting for transfers between devices: 190 us -> none  [attend_step(): lax.psum_scatter(jnp.concatenate((part_q, part_kv), axis=1), 'wide', scat...]
    ppermute x0 -> x32, waiting for transfers between devices: none -> 98.1 us  [the longest x16 71.6 us: line_scatter(): right = lax.ppermute(send_right, 'wide', pairs(t, 1))]
    ppermute x0 -> x32, starting transfers between devices: none -> 93.7 us  [the longest x16 77.5 us: line_scatter(): right = lax.ppermute(send_right, 'wide', pairs(t, 1))]
    all_gather x2, waiting for transfers between devices: 98.1 us -> 105 us  [attend_step(): lax.all_gather(attended, 'wide', axis=0, tiled=True)]
    unnamed x25 -> x36, local copies, waits for them, and re-layouts: 22.6 us -> 21.3 us
  transfers between devices with their start and end apart: 8 -> 38, of which waited for: 8 -> 24; matrix products, arithmetic and copies ran while one was open for 4% -> 4% of each run, Pallas kernels for 0% -> 0%
where the time goes in v3:
time: 523 us; the launch traced here: 522 us
  waiting for transfers between devices  284 us (54%)
  starting transfers between devices  94.1 us (18%)
  matrix products  87.4 us (17%)
  local copies, waits for them, and re-layouts  23.8 us (5%)
  other arithmetic  18 us (3%)
  between operations  14.5 us (3%)
    all_gather x2, waiting for transfers between devices, attend_step(): lax.all_gather(attended, 'wide', axis=0, tiled=True)  105 us
    ppermute x16, starting transfers between devices, line_scatter(): right = lax.ppermute(send_right, 'wide', pairs(t, 1))  77.5 us
    ppermute x16, waiting for transfers between devices, line_scatter(): right = lax.ppermute(send_right, 'wide', pairs(t, 1))  71.6 us
    reduce_scatter x2, waiting for transfers between devices, on_device(): lax.psum_scatter(partial_value, 'narrow', scatter_dimension=0, tiled=True)  60.1 us
    ppermute x16, waiting for transfers between devices, line_scatter(): left = lax.ppermute(send_left, 'wide', pairs(t, -1))  26.5 us
    dot_general x2, matrix products, attend_step(): jnp.einsum('rgjd,rgcd->rgjc', query, key_cache, preferred_element_type=jn...  24.6 us
    dot_general x2, matrix products, attend_step(): jnp.dot(lax.all_gather(attended, 'wide', axis=0, tiled=True), w_out, pref...  24.5 us
    unnamed x36, local copies, waits for them, and re-layouts  21.3 us
  transfers between devices with their start and end apart: 38, of which 24 were waited for; matrix products, arithmetic and copies ran while one was open for 4% of the time, Pallas kernels for 0%

profile of v3, /device:TPU:0, one launch (start us, length us, event | category | flops | bytes accessed | tf_op | source)
XLA Modules:
  0.0 521.6 jit_solution(4881577559063676818)
XLA Ops:
  7.3 17.5 %copy.69 = bf16[256,8,2,2048]{3,1,2,0:T(8,128)(2,1)} copy(bf16[256,8,2,2048]{3,2,1,0:T(2,128)(2,1)} %bitcast.162) | data formatting | bytes 33554432
  25.3 3.0 all-gather.5.cloned.1.call-done
  28.4 10.5 %fusion.69 = f32[256,4096]{1,0:T(8,128)S(1)} fusion(bf16[256,2048]{1,0:T(8,128)(2,1)} %all-gather.5.cloned.1.call-done, bf16[2048,4096]{1,0:T(8,128)(2,1)} %bitcast.163), kind=kOutput, calls=%fused_computation.150 | convolution fusion | flops 4294967296 | bytes 22020096 | tf_op jit(solution)/shard_map/dot_general | solution.py:83
  41.4 1.7 dynamic-slice_bitcast_fusion.3
  43.1 3.4 collective-permute-start
  49.5 3.4 collective-permute-start.8
  53.6 18.7 %collective-permute-done = f32[4,32,2304]{2,1,0:T(8,128)S(1)} collective-permute-done((f32[4,32,2304]{2,1,0:T(8,128)}, f32[4,32,2304]{2,1,0:T(8,128)S(1)}, u32[]{:S(2)}, u32[]{:S(2)}) %collective-permute-start) | collective-permute-done | bytes 1179680 | tf_op jit(solution)/shard_map/ppermute | solution.py:41
  72.4 4.2 collective-permute-done.1
  76.5 1.8 fusion.22
  78.4 3.4 collective-permute-start.2
  83.9 5.3 %collective-permute-done.2 = f32[32,2304]{1,0:T(8,128)S(1)} collective-permute-done((f32[32,2304]{1,0:T(8,128)S(1)}, f32[32,2304]{1,0:T(8,128)S(1)}, u32[]{:S(2)}, u32[]{:S(2)}) %collective-permute-start.2) | collective-permute-done | bytes 294944 | tf_op jit(solution)/shard_map/ppermute | solution.py:41
  89.3 4.4 collective-permute-start.3
  93.7 8.2 %collective-permute-done.9 = f32[2,32,2304]{2,1,0:T(8,128)S(1)} collective-permute-done((f32[2,32,2304]{2,1,0:T(8,128)S(1)}, f32[2,32,2304]{2,1,0:T(8,128)S(1)}, u32[]{:S(2)}, u32[]{:S(2)}) %collective-permute-start.9) | collective-permute-done | bytes 589856 | tf_op jit(solution)/shard_map/ppermute | solution.py:41
  102.7 5.0 collective-permute-start.10
  110.3 16.3 %collective-permute-start.4 = (f32[32,2304]{1,0:T(8,128)S(1)}, f32[32,2304]{1,0:T(8,128)S(1)}, u32[]{:S(2)}, u32[]{:S(2)}) collective-permute-start(f32[32,2304]{1,0:T(8,128)S(1)} %get-tuple-element.25), channel_id=1, source_target_pairs={{0,2},{2,4},{4,6},{1,3},{3,5},{5,7},{8,10},{10,12},{12,14},{9,11},... | collective-permute-start | bytes 884744 | tf_op jit(solution)/shard_map/ppermute | solution.py:41
  128.1 4.4 collective-permute-done.13
  134.1 1.5 collective-permute-start.15
  135.9 2.5 collective-permute-done.14
  138.3 4.4 collective-permute-done.15
  143.8 12.3 %fusion = (f32[32,2,16]{2,1,0:T(2,128)S(1)}, f32[32,2,16,1024]{3,2,1,0:T(8,128)}) fusion(pred[32,1024]{1,0:T(8,128)(4,1)S(1)} %copy-done.8, bf16[32,2,1024,128]{3,2,1,0:T(8,128)(2,1)} %param.11, bf16[32,2,16,64]{3,2,1,0:T(8,128)(2,1)S(1)} %get-tuple-element.36, bf16[32,2,16,64]{3,2,1,0:T(8,128)(2,1)S(1)} %get-tuple-element.35), kind=kOutput, calls=%fused_computation.6 | convolution fusion | flops 272104448 | bytes 21270528 | tf_op jit(solution)/shard_map/rgjd,rgcd->rgjc/dot_general | solution.py:98
  156.2 3.8 fusion.2
  160.0 7.5 %fusion.19 = bf16[32,2,16,128]{3,2,1,0:T(8,128)(2,1)S(1)} fusion(bf16[32,2,1024,128]{3,2,1,0:T(8,128)(2,1)} %param.12, f32[32,2,16,1024]{3,2,1,0:T(8,128)S(1)} %copy-done.1, f32[32,2,16]{2,1,0:T(2,128)S(1)} %get-tuple-element.40, f32[32,2,16]{2,1,0:T(2,128)S(1)} %multiply_maximum_fusion, pred[32,1024]{1,0:T(8,128)(4,1)S(1)} %copy-done.8, ...), kind=kOutput, calls=%fused_computation.28 | convolution fusion | flops 275120128 | bytes 21311488 | tf_op jit(solution)/shard_map/rgjc,rgcd->rgjd/dot_general | solution.py:110
  168.4 52.6 %all-gather.7.cloned.1.call-done = bf16[256,4096]{1,0:T(8,128)(2,1)} async-done(((bf16[32,4096]{1,0:T(8,128)(2,1)}), bf16[256,4096]{1,0:T(8,128)(2,1)}) %all-gather.7.cloned.1.call-update) | async-done | bytes 2097168 | tf_op jit(solution)/shard_map/all_gather | solution.py:114
  221.0 12.2 %fusion.71 = f32[256,2048]{1,0:T(8,128)} fusion(bf16[256,4096]{1,0:T(8,128)(2,1)} %all-gather.7.cloned.1.call-done, bf16[4096,2048]{1,0:T(8,128)(2,1)} %param.10), kind=kOutput, calls=%fused_computation.152 | convolution fusion | flops 4294967296 | bytes 20971520 | tf_op jit(solution)/shard_map/dot_general | solution.py:113
  233.3 30.0 %reduce-scatter.3.cloned.1.call-done = f32[64,2048]{1,0:T(8,128)} async-done(((f32[256,2048]{1,0:T(8,128)}), f32[64,2048]{1,0:T(8,128)}) %reduce-scatter.3.cloned.1.call-update) | async-done | bytes 524304 | tf_op jit(solution)/shard_map/reduce_scatter | solution.py:140
  263.4 1.8 add_convert_fusion.2
  265.5 16.6 %all-gather.9.cloned.1.call-done = bf16[256,2048]{1,0:T(8,128)(2,1)} async-done(((bf16[64,2048]{1,0:T(8,128)(2,1)}), bf16[256,2048]{1,0:T(8,128)(2,1)}) %all-gather.9.cloned.1.call-update) | async-done | bytes 1048592 | tf_op jit(solution)/shard_map/all_gather | solution.py:128
  282.1 10.5 %fusion.72 = f32[256,4096]{1,0:T(8,128)S(1)} fusion(bf16[256,2048]{1,0:T(8,128)(2,1)} %all-gather.9.cloned.1.call-done, bf16[2048,4096]{1,0:T(8,128)(2,1)} %bitcast.164), kind=kOutput, calls=%fused_computation.153 | convolution fusion | flops 4294967296 | bytes 22020096 | tf_op jit(solution)/shard_map/dot_general | solution.py:83
  293.9 3.4 collective-permute-start.16
  298.8 3.4 collective-permute-start.24
  303.0 19.9 %collective-permute-done.16 = f32[4,32,2304]{2,1,0:T(8,128)S(1)} collective-permute-done((f32[4,32,2304]{2,1,0:T(8,128)S(1)}, f32[4,32,2304]{2,1,0:T(8,128)S(1)}, u32[]{:S(2)}, u32[]{:S(2)}) %collective-permute-start.16) | collective-permute-done | bytes 1179680 | tf_op jit(solution)/shard_map/ppermute | solution.py:41
  322.9 4.2 collective-permute-done.17
  327.4 3.4 collective-permute-start.18
  332.9 5.3 %collective-permute-done.18 = f32[32,2304]{1,0:T(8,128)S(1)} collective-permute-done((f32[32,2304]{1,0:T(8,128)S(1)}, f32[32,2304]{1,0:T(8,128)S(1)}, u32[]{:S(2)}, u32[]{:S(2)}) %collective-permute-start.18) | collective-permute-done | bytes 294944 | tf_op jit(solution)/shard_map/ppermute | solution.py:41
  338.2 4.4 collective-permute-start.19
  342.7 8.2 %collective-permute-done.25 = f32[2,32,2304]{2,1,0:T(8,128)S(1)} collective-permute-done((f32[2,32,2304]{2,1,0:T(8,128)S(1)}, f32[2,32,2304]{2,1,0:T(8,128)S(1)}, u32[]{:S(2)}, u32[]{:S(2)}) %collective-permute-start.25) | collective-permute-done | bytes 589856 | tf_op jit(solution)/shard_map/ppermute | solution.py:41
  351.7 5.0 collective-permute-start.26
  359.3 16.3 %collective-permute-start.20 = (f32[32,2304]{1,0:T(8,128)S(1)}, f32[32,2304]{1,0:T(8,128)S(1)}, u32[]{:S(2)}, u32[]{:S(2)}) collective-permute-start(f32[32,2304]{1,0:T(8,128)S(1)} %get-tuple-element.21), channel_id=1, source_target_pairs={{0,2},{2,4},{4,6},{1,3},{3,5},{5,7},{8,10},{10,12},{12,14},{9,11},... | collective-permute-start | bytes 884744 | tf_op jit(solution)/shard_map/ppermute | solution.py:41
  377.0 4.5 collective-permute-done.29
  384.7 2.6 collective-permute-done.30
  387.3 4.4 collective-permute-done.31
  392.5 12.3 %fusion.1 = (f32[32,2,16]{2,1,0:T(2,128)S(1)}, f32[32,2,16,1024]{3,2,1,0:T(8,128)}) fusion(pred[32,1024]{1,0:T(8,128)(4,1)S(1)} %copy-done.8, bf16[32,2,1024,128]{3,2,1,0:T(8,128)(2,1)} %param.11, bf16[32,2,16,64]{3,2,1,0:T(8,128)(2,1)S(1)} %get-tuple-element.34, bf16[32,2,16,64]{3,2,1,0:T(8,128)(2,1)S(1)} %get-tuple-element.33), kind=kOutput, calls=%fused_computation.7 | convolution fusion | flops 272104448 | bytes 21270528 | tf_op jit(solution)/shard_map/rgjd,rgcd->rgjc/dot_general | solution.py:98
  405.5 4.0 fusion.3
  409.5 7.3 %fusion.5 = f32[32,2,16,128]{3,2,1,0:T(8,128)S(1)} fusion(bf16[32,2,1024,128]{3,2,1,0:T(8,128)(2,1)} %param.12, f32[32,2,16,1024]{3,2,1,0:T(8,128)S(1)} %copy-done, f32[32,2,16]{2,1,0:T(2,128)S(1)} %add.317, f32[32,2,16]{2,1,0:T(2,128)S(1)} %max.70, pred[32,1024]{1,0:T(8,128)(4,1)S(1)} %copy-done.8), kind=kOutput, calls=%fused_computation.13 | convolution fusion | flops 274726912 | bytes 21536768 | tf_op jit(solution)/shard_map/rgjc,rgcd->rgjd/dot_general | solution.py:110
  418.0 52.6 %all-gather.11.cloned.1.call-done = bf16[256,4096]{1,0:T(8,128)(2,1)} async-done(((bf16[32,4096]{1,0:T(8,128)(2,1)}), bf16[256,4096]{1,0:T(8,128)(2,1)}) %all-gather.11.cloned.1.call-update) | async-done | bytes 2097168 | tf_op jit(solution)/shard_map/all_gather | solution.py:114
  470.6 12.3 %fusion.74 = f32[256,2048]{1,0:T(8,128)} fusion(bf16[256,4096]{1,0:T(8,128)(2,1)} %all-gather.11.cloned.1.call-done, bf16[4096,2048]{1,0:T(8,128)(2,1)} %param.10), kind=kOutput, calls=%fused_computation.155 | convolution fusion | flops 4294967296 | bytes 20971520 | tf_op jit(solution)/shard_map/dot_general | solution.py:113
  482.9 30.1 %reduce-scatter.5.cloned.1.call-done = f32[64,2048]{1,0:T(8,128)} async-done(((f32[256,2048]{1,0:T(8,128)}), f32[64,2048]{1,0:T(8,128)}) %reduce-scatter.5.cloned.1.call-update) | async-done | bytes 524304 | tf_op jit(solution)/shard_map/reduce_scatter | solution.py:140
  513.0 1.8 add_convert_fusion
  (145 shorter events, 34.8 us)
Async XLA Ops:
  6.5 21.8 %all-gather.5.cloned.1.call-start = ((), (), s32[]{:S(2)}) async-start(), calls=%async_computation.2 | async-start | bytes 1310720 | tf_op jit(solution)/shard_map/all_gather | solution.py:128
  7.3 213.8 %all-gather.7.cloned.1.call-start = ((), (), s32[]{:S(2)}) async-start(), calls=%async_computation.3 | async-start | bytes 2359296 | tf_op jit(solution)/shard_map/all_gather | solution.py:114
  7.3 17.5 %copy-start.4 = (bf16[2048,2,256]{2,1,0:T(2,128)(2,1)S(1)}, bf16[2048,2,256]{2,1,0:T(2,128)(2,1)}, u32[]{:S(2)}) copy-start(bf16[2048,2,256]{2,1,0:T(2,128)(2,1)} %param.9) | copy-start | bytes 6291460
  25.3 13.6 %copy-start.5 = (bf16[256,8,2,256]{3,1,2,0:T(8,128)(2,1)}, bf16[256,8,2,256]{3,1,2,0:T(8,128)(2,1)S(1)}, u32[]{:S(2)}) copy-start(bf16[256,8,2,256]{3,1,2,0:T(8,128)(2,1)S(1)} %copy.70) | copy-start | bytes 6291460
  28.4 10.5 %copy-start.13 = (bf16[256,2048]{1,0:T(8,128)(2,1)S(1)}, bf16[256,2048]{1,0:T(8,128)(2,1)}, u32[]{:S(2)}) copy-start(bf16[256,2048]{1,0:T(8,128)(2,1)} %all-gather.5.cloned.1.call-done) | copy-start | bytes 3145732
  43.1 29.3 %collective-permute-start = (f32[4,32,2304]{2,1,0:T(8,128)}, f32[4,32,2304]{2,1,0:T(8,128)S(1)}, u32[]{:S(2)}, u32[]{:S(2)}) collective-permute-start(f32[4,32,2304]{2,1,0:T(8,128)} %get-tuple-element.15), channel_id=1, source_target_pairs={{0,1},{2,3},{4,5},{6,7},{8,9},{10,11},{12,13},{14,15},{16,17},{18,... | collective-permute-start | bytes 3538952 | tf_op jit(solution)/shard_map/ppermute | solution.py:41
  46.5 30.0 %collective-permute-start.1 = (f32[4,32,2304]{2,1,0:T(8,128)}, f32[4,32,2304]{2,1,0:T(8,128)}, u32[]{:S(2)}, u32[]{:S(2)}) collective-permute-start(f32[4,32,2304]{2,1,0:T(8,128)} %get-tuple-element.16), channel_id=1, source_target_pairs={{1,0},{3,2},{5,4},{7,6},{9,8},{11,10},{13,12},{15,14},{17,16},{19,... | collective-permute-start | bytes 3538952 | tf_op jit(solution)/shard_map/ppermute | solution.py:42
  49.5 32.3 %collective-permute-start.8 = (f32[2,32,2304]{2,1,0:T(8,128)S(1)}, f32[2,32,2304]{2,1,0:T(8,128)S(1)}, u32[]{:S(2)}, u32[]{:S(2)}) collective-permute-start(f32[2,32,2304]{2,1,0:T(8,128)S(1)} %get-tuple-element.19), channel_id=1, source_target_pairs={{0,2},{1,3},{8,10},{9,11},{16,18},{17,19},{24,26},{25,27}} | collective-permute-start | bytes 1769480 | tf_op jit(solution)/shard_map/ppermute | solution.py:41
  52.9 40.8 %collective-permute-start.11 = (f32[2,32,2304]{2,1,0:T(8,128)S(1)}, f32[2,32,2304]{2,1,0:T(8,128)S(1)}, u32[]{:S(2)}, u32[]{:S(2)}) collective-permute-start(f32[2,32,2304]{2,1,0:T(8,128)S(1)} %get-tuple-element.20), channel_id=1, source_target_pairs={{6,4},{7,5},{14,12},{15,13},{22,20},{23,21},{30,28},{31,29}} | collective-permute-start | bytes 1769480 | tf_op jit(solution)/shard_map/ppermute | solution.py:42
  78.4 10.8 %collective-permute-start.2 = (f32[32,2304]{1,0:T(8,128)S(1)}, f32[32,2304]{1,0:T(8,128)S(1)}, u32[]{:S(2)}, u32[]{:S(2)}) collective-permute-start(f32[32,2304]{1,0:T(8,128)S(1)} %get-tuple-element.27), channel_id=1, source_target_pairs={{0,2},{1,3},{8,10},{9,11},{16,18},{17,19},{24,26},{25,27}} | collective-permute-start | bytes 884744 | tf_op jit(solution)/shard_map/ppermute | solution.py:41
  81.9 20.0 %collective-permute-start.9 = (f32[2,32,2304]{2,1,0:T(8,128)S(1)}, f32[2,32,2304]{2,1,0:T(8,128)S(1)}, u32[]{:S(2)}, u32[]{:S(2)}) collective-permute-start(f32[2,32,2304]{2,1,0:T(8,128)S(1)} %bitcast_add_fusion.9), channel_id=1, source_target_pairs={{0,2},{2,4},{1,3},{3,5},{8,10},{10,12},{9,11},{11,13},{16,18},{18,... | collective-permute-start | bytes 1769480 | tf_op jit(solution)/shard_map/ppermute | solution.py:41
  83.2 24.5 %collective-permute-start.5 = (f32[32,2304]{1,0:T(8,128)S(1)}, f32[32,2304]{1,0:T(8,128)S(1)}, u32[]{:S(2)}, u32[]{:S(2)}) collective-permute-start(f32[32,2304]{1,0:T(8,128)S(1)} %get-tuple-element.28), channel_id=1, source_target_pairs={{6,4},{7,5},{14,12},{15,13},{22,20},{23,21},{30,28},{31,29}} | collective-permute-start | bytes 884744 | tf_op jit(solution)/shard_map/ppermute | solution.py:42
  89.3 18.9 %collective-permute-start.3 = (f32[32,2304]{1,0:T(8,128)S(1)}, f32[32,2304]{1,0:T(8,128)S(1)}, u32[]{:S(2)}, u32[]{:S(2)}) collective-permute-start(f32[32,2304]{1,0:T(8,128)S(1)} %bitcast_add_fusion.21), channel_id=1, source_target_pairs={{0,2},{2,4},{1,3},{3,5},{8,10},{10,12},{9,11},{11,13},{16,18},{18,... | collective-permute-start | bytes 884744 | tf_op jit(solution)/shard_map/ppermute | solution.py:41
  102.0 6.9 %collective-permute-start.12 = (f32[2,32,2304]{2,1,0:T(8,128)S(1)}, f32[2,32,2304]{2,1,0:T(8,128)S(1)}, u32[]{:S(2)}, u32[]{:S(2)}) collective-permute-start(f32[2,32,2304]{2,1,0:T(8,128)S(1)} %get-tuple-element.18), channel_id=1, source_target_pairs={{4,2},{6,4},{5,3},{7,5},{12,10},{14,12},{13,11},{15,13},{20,18},{2... | collective-permute-start | bytes 1769480 | tf_op jit(solution)/shard_map/ppermute | solution.py:42
  102.7 25.4 %collective-permute-start.10 = (f32[2,32,2304]{2,1,0:T(8,128)S(1)}, f32[2,32,2304]{2,1,0:T(8,128)S(1)}, u32[]{:S(2)}, u32[]{:S(2)}) collective-permute-start(f32[2,32,2304]{2,1,0:T(8,128)S(1)} %get-tuple-element.17), channel_id=1, source_target_pairs={{0,2},{2,4},{4,6},{1,3},{3,5},{5,7},{8,10},{10,12},{12,14},{9,11},... | collective-permute-start | bytes 1769480 | tf_op jit(solution)/shard_map/ppermute | solution.py:41
  108.3 18.3 %collective-permute-start.6 = (f32[32,2304]{1,0:T(8,128)S(1)}, f32[32,2304]{1,0:T(8,128)S(1)}, u32[]{:S(2)}, u32[]{:S(2)}) collective-permute-start(f32[32,2304]{1,0:T(8,128)S(1)} %get-tuple-element.26), channel_id=1, source_target_pairs={{4,2},{6,4},{5,3},{7,5},{12,10},{14,12},{13,11},{15,13},{20,18},{2... | collective-permute-start | bytes 884744 | tf_op jit(solution)/shard_map/ppermute | solution.py:42
  109.0 23.5 %collective-permute-start.13 = (f32[2,32,2304]{2,1,0:T(8,128)S(1)}, f32[2,32,2304]{2,1,0:T(8,128)S(1)}, u32[]{:S(2)}, u32[]{:S(2)}) collective-permute-start(f32[2,32,2304]{2,1,0:T(8,128)S(1)} %bitcast_add_fusion.8), channel_id=1, source_target_pairs={{2,0},{4,2},{6,4},{3,1},{5,3},{7,5},{10,8},{12,10},{14,12},{11,9},... | collective-permute-start | bytes 1769480 | tf_op jit(solution)/shard_map/ppermute | solution.py:42
  110.3 25.3 %collective-permute-start.4 = (f32[32,2304]{1,0:T(8,128)S(1)}, f32[32,2304]{1,0:T(8,128)S(1)}, u32[]{:S(2)}, u32[]{:S(2)}) collective-permute-start(f32[32,2304]{1,0:T(8,128)S(1)} %get-tuple-element.25), channel_id=1, source_target_pairs={{0,2},{2,4},{4,6},{1,3},{3,5},{5,7},{8,10},{10,12},{12,14},{9,11},... | collective-permute-start | bytes 884744 | tf_op jit(solution)/shard_map/ppermute | solution.py:41
  126.7 16.4 %copy-start.10 = (f32[32,64]{1,0:T(8,128)S(1)}, f32[32,64]{1,0:T(8,128)}, u32[]{:S(2)}) copy-start(f32[32,64]{1,0:T(8,128)} %get-tuple-element.49) | copy-start | bytes 24580
  126.7 16.4 %copy-start.11 = (f32[32,64]{1,0:T(8,128)S(1)}, f32[32,64]{1,0:T(8,128)}, u32[]{:S(2)}) copy-start(f32[32,64]{1,0:T(8,128)} %get-tuple-element.50) | copy-start | bytes 24580
  126.7 9.1 %collective-permute-start.7 = (f32[32,2304]{1,0:T(8,128)S(1)}, f32[32,2304]{1,0:T(8,128)S(1)}, u32[]{:S(2)}, u32[]{:S(2)}) collective-permute-start(f32[32,2304]{1,0:T(8,128)S(1)} %bitcast_add_fusion.20), channel_id=1, source_target_pairs={{2,0},{4,2},{6,4},{3,1},{5,3},{7,5},{10,8},{12,10},{14,12},{11,9},... | collective-permute-start | bytes 884744 | tf_op jit(solution)/shard_map/ppermute | solution.py:42
  132.6 11.2 %copy-start.8 = (pred[32,1024]{1,0:T(8,128)(4,1)S(1)}, pred[32,1024]{1,0:T(8,128)(4,1)}, u32[]{:S(2)}) copy-start(pred[32,1024]{1,0:T(8,128)(4,1)} %iota_compare_fusion) | copy-start | bytes 98308
  132.7 5.7 %collective-permute-start.14 = (f32[32,2304]{1,0:T(8,128)S(1)}, f32[32,2304]{1,0:T(8,128)S(1)}, u32[]{:S(2)}, u32[]{:S(2)}) collective-permute-start(f32[32,2304]{1,0:T(8,128)S(1)} %get-tuple-element.31), channel_id=1, source_target_pairs={{0,1},{2,3},{4,5},{6,7},{8,9},{10,11},{12,13},{14,15},{16,17},{18,... | collective-permute-start | bytes 884744 | tf_op jit(solution)/shard_map/ppermute | solution.py:41
  134.1 8.6 %collective-permute-start.15 = (f32[32,2304]{1,0:T(8,128)S(1)}, f32[32,2304]{1,0:T(8,128)S(1)}, u32[]{:S(2)}, u32[]{:S(2)}) collective-permute-start(f32[32,2304]{1,0:T(8,128)S(1)} %get-tuple-element.32), channel_id=1, source_target_pairs={{1,0},{3,2},{5,4},{7,6},{9,8},{11,10},{13,12},{15,14},{17,16},{19,... | collective-permute-start | bytes 884744 | tf_op jit(solution)/shard_map/ppermute | solution.py:42
  168.3 95.1 %copy-start.7 = (bf16[64,2048]{1,0:T(8,128)(2,1)S(1)}, bf16[64,2048]{1,0:T(8,128)(2,1)}, u32[]{:S(2)}) copy-start(bf16[64,2048]{1,0:T(8,128)(2,1)} %param.7) | copy-start | bytes 786436
  168.3 95.1 %reduce-scatter.3.cloned.1.call-start = ((), (), s32[]{:S(2)}) async-start(), calls=%async_computation.4 | async-start | bytes 2621440 | tf_op jit(solution)/shard_map/reduce_scatter | solution.py:140
  233.3 48.8 %all-gather.9.cloned.1.call-start = ((), (), s32[]{:S(2)}) async-start(), calls=%async_computation.5 | async-start | bytes 1310720 | tf_op jit(solution)/shard_map/all_gather | solution.py:128
  265.2 27.4 %copy-start.6 = (bf16[256,8,2,256]{3,1,2,0:T(8,128)(2,1)S(1)}, bf16[256,8,2,256]{3,1,2,0:T(8,128)(2,1)}, u32[]{:S(2)}) copy-start(bf16[256,8,2,256]{3,1,2,0:T(8,128)(2,1)} %copy-done.5) | copy-start | bytes 6291460
  265.2 205.4 %all-gather.11.cloned.1.call-start = ((), (), s32[]{:S(2)}) async-start(), calls=%async_computation.6 | async-start | bytes 2359296 | tf_op jit(solution)/shard_map/all_gather | solution.py:114
  293.9 29.0 %collective-permute-start.16 = (f32[4,32,2304]{2,1,0:T(8,128)S(1)}, f32[4,32,2304]{2,1,0:T(8,128)S(1)}, u32[]{:S(2)}, u32[]{:S(2)}) collective-permute-start(f32[4,32,2304]{2,1,0:T(8,128)S(1)} %get-tuple-element.9), channel_id=1, source_target_pairs={{0,1},{2,3},{4,5},{6,7},{8,9},{10,11},{12,13},{14,15},{16,17},{18,... | collective-permute-start | bytes 3538952 | tf_op jit(solution)/shard_map/ppermute | solution.py:41
  297.3 29.7 %collective-permute-start.17 = (f32[4,32,2304]{2,1,0:T(8,128)S(1)}, f32[4,32,2304]{2,1,0:T(8,128)S(1)}, u32[]{:S(2)}, u32[]{:S(2)}) collective-permute-start(f32[4,32,2304]{2,1,0:T(8,128)S(1)} %get-tuple-element.10), channel_id=1, source_target_pairs={{1,0},{3,2},{5,4},{7,6},{9,8},{11,10},{13,12},{15,14},{17,16},{19,... | collective-permute-start | bytes 3538952 | tf_op jit(solution)/shard_map/ppermute | solution.py:42
  298.8 32.0 %collective-permute-start.24 = (f32[2,32,2304]{2,1,0:T(8,128)S(1)}, f32[2,32,2304]{2,1,0:T(8,128)S(1)}, u32[]{:S(2)}, u32[]{:S(2)}) collective-permute-start(f32[2,32,2304]{2,1,0:T(8,128)S(1)} %get-tuple-element.13), channel_id=1, source_target_pairs={{0,2},{1,3},{8,10},{9,11},{16,18},{17,19},{24,26},{25,27}} | collective-permute-start | bytes 1769480 | tf_op jit(solution)/shard_map/ppermute | solution.py:41
  302.3 40.4 %collective-permute-start.27 = (f32[2,32,2304]{2,1,0:T(8,128)S(1)}, f32[2,32,2304]{2,1,0:T(8,128)S(1)}, u32[]{:S(2)}, u32[]{:S(2)}) collective-permute-start(f32[2,32,2304]{2,1,0:T(8,128)S(1)} %get-tuple-element.14), channel_id=1, source_target_pairs={{6,4},{7,5},{14,12},{15,13},{22,20},{23,21},{30,28},{31,29}} | collective-permute-start | bytes 1769480 | tf_op jit(solution)/shard_map/ppermute | solution.py:42
  327.4 10.8 %collective-permute-start.18 = (f32[32,2304]{1,0:T(8,128)S(1)}, f32[32,2304]{1,0:T(8,128)S(1)}, u32[]{:S(2)}, u32[]{:S(2)}) collective-permute-start(f32[32,2304]{1,0:T(8,128)S(1)} %get-tuple-element.23), channel_id=1, source_target_pairs={{0,2},{1,3},{8,10},{9,11},{16,18},{17,19},{24,26},{25,27}} | collective-permute-start | bytes 884744 | tf_op jit(solution)/shard_map/ppermute | solution.py:41
  330.9 20.0 %collective-permute-start.25 = (f32[2,32,2304]{2,1,0:T(8,128)S(1)}, f32[2,32,2304]{2,1,0:T(8,128)S(1)}, u32[]{:S(2)}, u32[]{:S(2)}) collective-permute-start(f32[2,32,2304]{2,1,0:T(8,128)S(1)} %bitcast_add_fusion.4), channel_id=1, source_target_pairs={{0,2},{2,4},{1,3},{3,5},{8,10},{10,12},{9,11},{11,13},{16,18},{18,... | collective-permute-start | bytes 1769480 | tf_op jit(solution)/shard_map/ppermute | solution.py:41
  332.2 24.5 %collective-permute-start.21 = (f32[32,2304]{1,0:T(8,128)S(1)}, f32[32,2304]{1,0:T(8,128)S(1)}, u32[]{:S(2)}, u32[]{:S(2)}) collective-permute-start(f32[32,2304]{1,0:T(8,128)S(1)} %get-tuple-element.24), channel_id=1, source_target_pairs={{6,4},{7,5},{14,12},{15,13},{22,20},{23,21},{30,28},{31,29}} | collective-permute-start | bytes 884744 | tf_op jit(solution)/shard_map/ppermute | solution.py:42
  338.2 18.9 %collective-permute-start.19 = (f32[32,2304]{1,0:T(8,128)S(1)}, f32[32,2304]{1,0:T(8,128)S(1)}, u32[]{:S(2)}, u32[]{:S(2)}) collective-permute-start(f32[32,2304]{1,0:T(8,128)S(1)} %bitcast_add_fusion.15), channel_id=1, source_target_pairs={{0,2},{2,4},{1,3},{3,5},{8,10},{10,12},{9,11},{11,13},{16,18},{18,... | collective-permute-start | bytes 884744 | tf_op jit(solution)/shard_map/ppermute | solution.py:41
  351.0 6.9 %collective-permute-start.28 = (f32[2,32,2304]{2,1,0:T(8,128)S(1)}, f32[2,32,2304]{2,1,0:T(8,128)S(1)}, u32[]{:S(2)}, u32[]{:S(2)}) collective-permute-start(f32[2,32,2304]{2,1,0:T(8,128)S(1)} %get-tuple-element.12), channel_id=1, source_target_pairs={{4,2},{6,4},{5,3},{7,5},{12,10},{14,12},{13,11},{15,13},{20,18},{2... | collective-permute-start | bytes 1769480 | tf_op jit(solution)/shard_map/ppermute | solution.py:42
  351.7 25.2 %collective-permute-start.26 = (f32[2,32,2304]{2,1,0:T(8,128)S(1)}, f32[2,32,2304]{2,1,0:T(8,128)S(1)}, u32[]{:S(2)}, u32[]{:S(2)}) collective-permute-start(f32[2,32,2304]{2,1,0:T(8,128)S(1)} %get-tuple-element.11), channel_id=1, source_target_pairs={{0,2},{2,4},{4,6},{1,3},{3,5},{5,7},{8,10},{10,12},{12,14},{9,11},... | collective-permute-start | bytes 1769480 | tf_op jit(solution)/shard_map/ppermute | solution.py:41
  357.2 18.4 %collective-permute-start.22 = (f32[32,2304]{1,0:T(8,128)S(1)}, f32[32,2304]{1,0:T(8,128)S(1)}, u32[]{:S(2)}, u32[]{:S(2)}) collective-permute-start(f32[32,2304]{1,0:T(8,128)S(1)} %get-tuple-element.22), channel_id=1, source_target_pairs={{4,2},{6,4},{5,3},{7,5},{12,10},{14,12},{13,11},{15,13},{20,18},{2... | collective-permute-start | bytes 884744 | tf_op jit(solution)/shard_map/ppermute | solution.py:42
  358.0 23.5 %collective-permute-start.29 = (f32[2,32,2304]{2,1,0:T(8,128)S(1)}, f32[2,32,2304]{2,1,0:T(8,128)S(1)}, u32[]{:S(2)}, u32[]{:S(2)}) collective-permute-start(f32[2,32,2304]{2,1,0:T(8,128)S(1)} %bitcast_add_fusion.3), channel_id=1, source_target_pairs={{2,0},{4,2},{6,4},{3,1},{5,3},{7,5},{10,8},{12,10},{14,12},{11,9},... | collective-permute-start | bytes 1769480 | tf_op jit(solution)/shard_map/ppermute | solution.py:42
  359.3 25.1 %collective-permute-start.20 = (f32[32,2304]{1,0:T(8,128)S(1)}, f32[32,2304]{1,0:T(8,128)S(1)}, u32[]{:S(2)}, u32[]{:S(2)}) collective-permute-start(f32[32,2304]{1,0:T(8,128)S(1)} %get-tuple-element.21), channel_id=1, source_target_pairs={{0,2},{2,4},{4,6},{1,3},{3,5},{5,7},{8,10},{10,12},{12,14},{9,11},... | collective-permute-start | bytes 884744 | tf_op jit(solution)/shard_map/ppermute | solution.py:41
  375.6 16.4 %copy-start.9 = (f32[32,64]{1,0:T(8,128)S(1)}, f32[32,64]{1,0:T(8,128)}, u32[]{:S(2)}) copy-start(f32[32,64]{1,0:T(8,128)} %get-tuple-element.46) | copy-start | bytes 24580
  375.6 9.0 %collective-permute-start.23 = (f32[32,2304]{1,0:T(8,128)S(1)}, f32[32,2304]{1,0:T(8,128)S(1)}, u32[]{:S(2)}, u32[]{:S(2)}) collective-permute-start(f32[32,2304]{1,0:T(8,128)S(1)} %bitcast_add_fusion.14), channel_id=1, source_target_pairs={{2,0},{4,2},{6,4},{3,1},{5,3},{7,5},{10,8},{12,10},{14,12},{11,9},... | collective-permute-start | bytes 884744 | tf_op jit(solution)/shard_map/ppermute | solution.py:42
  381.7 5.7 %collective-permute-start.30 = (f32[32,2304]{1,0:T(8,128)S(1)}, f32[32,2304]{1,0:T(8,128)S(1)}, u32[]{:S(2)}, u32[]{:S(2)}) collective-permute-start(f32[32,2304]{1,0:T(8,128)S(1)} %get-tuple-element.29), channel_id=1, source_target_pairs={{0,1},{2,3},{4,5},{6,7},{8,9},{10,11},{12,13},{14,15},{16,17},{18,... | collective-permute-start | bytes 884744 | tf_op jit(solution)/shard_map/ppermute | solution.py:41
  383.1 8.6 %collective-permute-start.31 = (f32[32,2304]{1,0:T(8,128)S(1)}, f32[32,2304]{1,0:T(8,128)S(1)}, u32[]{:S(2)}, u32[]{:S(2)}) collective-permute-start(f32[32,2304]{1,0:T(8,128)S(1)} %get-tuple-element.30), channel_id=1, source_target_pairs={{1,0},{3,2},{5,4},{7,6},{9,8},{11,10},{13,12},{15,14},{17,16},{19,... | collective-permute-start | bytes 884744 | tf_op jit(solution)/shard_map/ppermute | solution.py:42
  417.9 95.0 %copy-start.3 = (bf16[64,2048]{1,0:T(8,128)(2,1)S(1)}, bf16[64,2048]{1,0:T(8,128)(2,1)}, u32[]{:S(2)}) copy-start(bf16[64,2048]{1,0:T(8,128)(2,1)} %add_convert_fusion.2) | copy-start | bytes 786436
  418.0 95.0 %reduce-scatter.5.cloned.1.call-start = ((), (), s32[]{:S(2)}) async-start(), calls=%async_computation.7 | async-start | bytes 2621440 | tf_op jit(solution)/shard_map/reduce_scatter | solution.py:140
  (5 other events, 28.4 us)
Sparse Core Ops, SparseCore 0:
  8.9 19.4 all-gather.4
  168.4 52.5 all-gather.6
  233.4 29.9 reduce-scatter.2
  265.3 16.6 all-gather.8
  418.1 52.5 all-gather.10
  483.0 29.9 reduce-scatter.4

commit v4 on v1

--- a/solution.py
+++ b/solution.py
@@ -74,10 +74,10 @@
     w_kv2 = w_keyval.reshape(w_keyval.shape[0], -1)
     new_keys = []
     new_vals = []
-    result = hidden_in
+    every = lax.all_gather(hidden_in, "narrow", axis=0, tiled=True)
     for step in range(STEPS):
         partial_value = attend_step(
-            lax.all_gather(result, "narrow", axis=0, tiled=True),
+            every,
             step,
             w_q2,
             w_kv2,
@@ -88,9 +88,10 @@
             new_keys,
             new_vals,
         )
-        update = lax.psum_scatter(partial_value, "narrow", scatter_dimension=0, tiled=True)
-        result = (result.astype(jnp.float32) + update).astype(jnp.bfloat16)
-    return result
+        update = lax.psum(partial_value, "narrow")
+        every = (every.astype(jnp.float32) + update).astype(jnp.bfloat16)
+    own = hidden_in.shape[0]
+    return lax.dynamic_slice_in_dim(every, lax.axis_index("narrow") * own, own, 0)
 
 
 def solution(mesh):

time: 513 us -> 534 us (1.041)
  waiting for transfers between devices: 369 us -> 392 us
    psum x0 -> x2, waiting for transfers between devices: none -> 100 us  [on_device(): update = lax.psum(partial_value, 'narrow')]
    reduce_scatter x2 -> x0, waiting for transfers between devices: 60.1 us -> none  [on_device(): lax.psum_scatter(partial_value, 'narrow', scatter_dimension=0, tiled=True)]
    all_gather x2 -> x1, waiting for transfers between devices: 19.9 us -> 3.07 us  [on_device(): every = lax.all_gather(hidden_in, 'narrow', axis=0, tiled=True)]
    unnamed x25 -> x19, local copies, waits for them, and re-layouts: 22.6 us -> 22.5 us
  transfers between devices with their start and end apart: 8 -> 7, of which waited for: 8 -> 7; matrix products, arithmetic and copies ran while one was open for 4% -> 3% of each run, Pallas kernels for 0% -> 0%
where the time goes in v4:
time: 534 us
  waiting for transfers between devices  392 us (73%)
  matrix products  84.9 us (16%)
  local copies, waits for them, and re-layouts  24.7 us (5%)
  other arithmetic  17.8 us (3%)
  between operations  13.8 us (3%)
    reduce_scatter x2, waiting for transfers between devices, attend_step(): lax.psum_scatter(jnp.concatenate((part_q, part_kv), axis=1), 'wide', scat...  190 us
    psum x2, waiting for transfers between devices, on_device(): update = lax.psum(partial_value, 'narrow')  100 us
    all_gather x2, waiting for transfers between devices, attend_step(): lax.all_gather(attended, 'wide', axis=0, tiled=True)  98.1 us
    dot_general x2, matrix products, attend_step(): jnp.einsum('rgjd,rgcd->rgjc', query, key_cache, preferred_element_type=jn...  24.5 us
    dot_general x2, matrix products, attend_step(): jnp.dot(lax.all_gather(attended, 'wide', axis=0, tiled=True), w_out, pref...  24.4 us
    unnamed x19, local copies, waits for them, and re-layouts  22.5 us
    dot_general x2, matrix products, attend_step(): part_q = jnp.dot(every, w_q2, preferred_element_type=jnp.float32)  18.6 us
    dot_general x2, matrix products, attend_step(): jnp.einsum('rgjc,rgcd->rgjd', p_cached, value_cache, preferred_element_ty...  14.8 us
  transfers between devices with their start and end apart: 7, of which 7 were waited for; matrix products, arithmetic and copies ran while one was open for 3% of the time, Pallas kernels for 0%

profile of v4, /device:TPU:0, one launch (start us, length us, event | category | flops | bytes accessed | tf_op | source)
XLA Modules:
  0.0 533.7 jit_solution(17887279063644982727)
XLA Ops:
  6.5 0.7 all-gather.4.cloned.1.call-update
  7.3 17.5 %copy.59 = bf16[256,8,2,2048]{3,1,2,0:T(8,128)(2,1)} copy(bf16[256,8,2,2048]{3,2,1,0:T(2,128)(2,1)} %bitcast.57) | data formatting | bytes 33554432
  24.8 0.5 copy.60
  25.3 3.1 all-gather.4.cloned.1.call-done
  28.4 10.5 %fusion.60 = f32[256,4096]{1,0:T(8,128)S(1)} fusion(bf16[256,2048]{1,0:T(8,128)(2,1)} %all-gather.4.cloned.1.call-done, bf16[2048,4096]{1,0:T(8,128)(2,1)} %bitcast.58), kind=kOutput, calls=%fused_computation.101 | convolution fusion | flops 4294967296 | bytes 22020096 | tf_op jit(solution)/shard_map/dot_general | solution.py:33
  38.9 0.7 fusion.61
  39.6 2.5 pad_maximum_fusion
  42.2 0.6 copy-done.4
  42.8 0.1 iota_compare_fusion
  42.9 0.2 multiply_cosine_fusion
  43.1 94.5 %reduce-scatter.3.cloned.1.call-done = f32[32,4608]{1,0:T(8,128)} async-done(((f32[256,4608]{1,0:T(8,128)}), f32[32,4608]{1,0:T(8,128)}) %reduce-scatter.3.cloned.1.call-update) | async-done | bytes 589840 | tf_op jit(solution)/shard_map/reduce_scatter | solution.py:35
  137.6 0.8 slice.67
  138.5 0.1 fusion.58
  138.6 1.1 slice_bitcast_fusion.1
  139.7 0.1 copy.61
  139.8 0.2 subtract_convert_fusion.1
  140.0 0.1 maximum_bitcast_fusion
  140.1 0.3 fusion.23
  140.4 12.2 %fusion = (f32[32,2,16]{2,1,0:T(2,128)S(1)}, f32[32,2,16,1024]{3,2,1,0:T(8,128)}) fusion(pred[32,1024]{1,0:T(8,128)(4,1)S(1)} %iota_compare_fusion, bf16[32,2,1024,128]{3,2,1,0:T(8,128)(2,1)} %param.11, bf16[32,2,16,64]{3,2,1,0:T(8,128)(2,1)S(1)} %get-tuple-element.8, bf16[32,2,16,64]{3,2,1,0:T(8,128)(2,1)S(1)} %get-tuple-element.7), kind=kOutput, calls=%fused_computation.8 | convolution fusion | flops 272104448 | bytes 21270528 | tf_op jit(solution)/shard_map/rgjd,rgcd->rgjc/dot_general | solution.py:50
  152.7 3.8 fusion.2
  156.5 0.1 fusion.42
  156.6 7.5 %fusion.19 = bf16[32,2,16,128]{3,2,1,0:T(8,128)(2,1)S(1)} fusion(bf16[32,2,1024,128]{3,2,1,0:T(8,128)(2,1)} %param.12, f32[32,2,16,1024]{3,2,1,0:T(8,128)S(1)} %copy-done.1, f32[32,2,16]{2,1,0:T(2,128)S(1)} %get-tuple-element.12, f32[32,2,16]{2,1,0:T(2,128)S(1)} %multiply_maximum_fusion, pred[32,1024]{1,0:T(8,128)(4,1)S(1)} %iota_compare_fusion, ...), kind=kOutput, calls=%fused_computation.29 | convolution fusion | flops 275120128 | bytes 21311488 | tf_op jit(solution)/shard_map/rgjc,rgcd->rgjd/dot_general | solution.py:62
  164.1 0.8 copy.94
  164.9 0.2 all-reduce.3.cloned.1.call-start
  165.2 49.0 %all-gather.6.cloned.1.call-done = bf16[256,4096]{1,0:T(8,128)(2,1)} async-done(((bf16[32,4096]{1,0:T(8,128)(2,1)}), bf16[256,4096]{1,0:T(8,128)(2,1)}) %all-gather.6.cloned.1.call-update) | async-done | bytes 2097168 | tf_op jit(solution)/shard_map/all_gather | solution.py:66
  214.1 12.2 %fusion.62 = f32[256,2048]{1,0:T(8,128)} fusion(bf16[256,4096]{1,0:T(8,128)(2,1)} %all-gather.6.cloned.1.call-done, bf16[4096,2048]{1,0:T(8,128)(2,1)} %param.10), kind=kOutput, calls=%fused_computation.103 | convolution fusion | flops 4294967296 | bytes 20971520 | tf_op jit(solution)/shard_map/dot_general | solution.py:65
  226.4 50.0 %all-reduce.3.cloned.1.call-done = f32[256,2048]{1,0:T(8,128)} async-done(((f32[256,2048]{1,0:T(8,128)}), f32[256,2048]{1,0:T(8,128)}) %all-reduce.3.cloned.1.call-update) | async-done | bytes 2097168 | tf_op jit(solution)/shard_map/psum | solution.py:91
  276.4 2.1 add_convert_fusion
  278.5 8.1 %fusion.63 = f32[256,4096]{1,0:T(8,128)S(1)} fusion(bf16[256,2048]{1,0:T(8,128)(2,1)S(1)} %add_convert_fusion, bf16[2048,4096]{1,0:T(8,128)(2,1)} %bitcast.59), kind=kOutput, calls=%fused_computation.104 | convolution fusion | flops 4294967296 | bytes 22020096 | tf_op jit(solution)/shard_map/dot_general | solution.py:33
  286.7 0.7 fusion.64
  287.4 2.5 pad_maximum_fusion.1
  290.1 95.5 %reduce-scatter.5.cloned.1.call-done = f32[32,4608]{1,0:T(8,128)} async-done(((f32[256,4608]{1,0:T(8,128)}), f32[32,4608]{1,0:T(8,128)}) %reduce-scatter.5.cloned.1.call-update) | async-done | bytes 589840 | tf_op jit(solution)/shard_map/reduce_scatter | solution.py:35
  385.6 0.8 slice.74
  386.4 0.1 fusion.57
  386.7 1.1 slice_bitcast_fusion
  387.7 0.1 copy.63
  387.8 0.2 subtract_convert_fusion
  388.1 12.2 %fusion.1 = (f32[32,2,16]{2,1,0:T(2,128)S(1)}, f32[32,2,16,1024]{3,2,1,0:T(8,128)}) fusion(pred[32,1024]{1,0:T(8,128)(4,1)S(1)} %iota_compare_fusion, bf16[32,2,1024,128]{3,2,1,0:T(8,128)(2,1)} %param.11, bf16[32,2,16,64]{3,2,1,0:T(8,128)(2,1)S(1)} %get-tuple-element.6, bf16[32,2,16,64]{3,2,1,0:T(8,128)(2,1)S(1)} %get-tuple-element.5), kind=kOutput, calls=%fused_computation.9 | convolution fusion | flops 272104448 | bytes 21270528 | tf_op jit(solution)/shard_map/rgjd,rgcd->rgjc/dot_general | solution.py:50
  400.3 0.5 fusion.59
  400.9 0.1 fusion.25
  401.0 4.0 fusion.3
  405.0 7.3 %fusion.5 = f32[32,2,16,128]{3,2,1,0:T(8,128)S(1)} fusion(bf16[32,2,1024,128]{3,2,1,0:T(8,128)(2,1)} %param.12, f32[32,2,16,1024]{3,2,1,0:T(8,128)S(1)} %copy-done, f32[32,2,16]{2,1,0:T(2,128)S(1)} %add.62, f32[32,2,16]{2,1,0:T(2,128)S(1)} %max.13, pred[32,1024]{1,0:T(8,128)(4,1)S(1)} %iota_compare_fusion), kind=kOutput, calls=%fused_computation.13 | convolution fusion | flops 274726912 | bytes 21536768 | tf_op jit(solution)/shard_map/rgjc,rgcd->rgjd/dot_general | solution.py:62
  412.4 0.3 fusion.20
  412.7 0.8 copy.93
  413.6 49.2 %all-gather.8.cloned.1.call-done = bf16[256,4096]{1,0:T(8,128)(2,1)} async-done(((bf16[32,4096]{1,0:T(8,128)(2,1)}), bf16[256,4096]{1,0:T(8,128)(2,1)}) %all-gather.8.cloned.1.call-update) | async-done | bytes 2097168 | tf_op jit(solution)/shard_map/all_gather | solution.py:66
  462.7 12.2 %fusion.65 = f32[256,2048]{1,0:T(8,128)} fusion(bf16[256,4096]{1,0:T(8,128)(2,1)} %all-gather.8.cloned.1.call-done, bf16[4096,2048]{1,0:T(8,128)(2,1)} %param.10), kind=kOutput, calls=%fused_computation.106 | convolution fusion | flops 4294967296 | bytes 20971520 | tf_op jit(solution)/shard_map/dot_general | solution.py:65
  475.0 50.0 %all-reduce.5.cloned.1.call-done = f32[256,2048]{1,0:T(8,128)} async-done(((f32[256,2048]{1,0:T(8,128)}), f32[256,2048]{1,0:T(8,128)}) %all-reduce.5.cloned.1.call-update) | async-done | bytes 2097168 | tf_op jit(solution)/shard_map/psum | solution.py:91
  525.0 1.8 fusion.21
  (41 shorter events, 0.8 us)
Async XLA Ops:
  6.5 21.8 %all-gather.4.cloned.1.call-start = ((), (), s32[]{:S(2)}) async-start(), calls=%async_computation.2 | async-start | bytes 1310720 | tf_op jit(solution)/shard_map/all_gather | solution.py:77
  7.3 130.3 %reduce-scatter.3.cloned.1.call-start = ((), (), s32[]{:S(2)}) async-start(), calls=%async_computation.3 | async-start | bytes 5308416 | tf_op jit(solution)/shard_map/reduce_scatter | solution.py:35
  7.3 17.5 %copy-start.2 = (bf16[2048,2,256]{2,1,0:T(2,128)(2,1)S(1)}, bf16[2048,2,256]{2,1,0:T(2,128)(2,1)}, u32[]{:S(2)}) copy-start(bf16[2048,2,256]{2,1,0:T(2,128)(2,1)} %param.9) | copy-start | bytes 6291460
  28.4 10.5 %copy-start.3 = (bf16[256,2048]{1,0:T(8,128)(2,1)S(1)}, bf16[256,2048]{1,0:T(8,128)(2,1)}, u32[]{:S(2)}) copy-start(bf16[256,2048]{1,0:T(8,128)(2,1)} %all-gather.4.cloned.1.call-done) | copy-start | bytes 3145732
  42.2 0.7 copy-start.4
  42.2 171.9 %all-gather.6.cloned.1.call-start = ((), (), s32[]{:S(2)}) async-start(), calls=%async_computation.4 | async-start | bytes 2359296 | tf_op jit(solution)/shard_map/all_gather | solution.py:66
  152.7 3.9 copy-start.1
  164.9 111.5 %all-reduce.3.cloned.1.call-start = ((), (), s32[]{:S(2)}) async-start(), calls=%async_computation.5 | async-start | bytes 4194304 | tf_op jit(solution)/shard_map/psum | solution.py:91
  226.4 159.2 %reduce-scatter.5.cloned.1.call-start = ((), (), s32[]{:S(2)}) async-start(), calls=%async_computation.6 | async-start | bytes 5308416 | tf_op jit(solution)/shard_map/reduce_scatter | solution.py:35
  289.9 172.8 %all-gather.8.cloned.1.call-start = ((), (), s32[]{:S(2)}) async-start(), calls=%async_computation.7 | async-start | bytes 2359296 | tf_op jit(solution)/shard_map/all_gather | solution.py:66
  400.3 4.7 copy-start
  413.5 111.5 %all-reduce.5.cloned.1.call-start = ((), (), s32[]{:S(2)}) async-start(), calls=%async_computation.8 | async-start | bytes 4194304 | tf_op jit(solution)/shard_map/psum | solution.py:91
Sparse Core Ops, SparseCore 0:
  8.9 19.4 all-gather.3
  42.3 95.2 reduce-scatter.2
  165.0 49.0 all-gather.5
  226.5 49.8 all-reduce.2
  290.1 95.4 reduce-scatter.4
  413.6 49.0 all-gather.7
  475.1 49.8 all-reduce.4

commit v5 on v3

--- a/solution.py
+++ b/solution.py
@@ -64,12 +64,10 @@
     rows, cols = value.shape
     size = rows // n_wide
     half = cols // 2
-    first = value[:, :half].reshape(n_z, n_x, size, half)
+    a = lax.psum_scatter(value[:, :half], "wide", scatter_dimension=0, tiled=True)
     second = value[:, half:].reshape(n_z, n_x, size, cols - half)
-    a = line_scatter(jnp.swapaxes(first, 0, 1), xpos, n_x, x_pairs)
-    a = line_scatter(a, zpos, n_z, z_pairs)
-    b = line_scatter(second, zpos, n_z, z_pairs)
-    b = line_scatter(b, xpos, n_x, x_pairs)
+    b = line_scatter(jnp.swapaxes(second, 0, 1), xpos, n_x, x_pairs)
+    b = line_scatter(b, zpos, n_z, z_pairs)
     return jnp.concatenate((a, b), axis=1)
 
 

time: 523 us -> 515 us (0.985)
  starting transfers between devices: 94.1 us -> 41.4 us
  waiting for transfers between devices: 284 us -> 324 us
    ppermute x16 -> x8, starting transfers between devices: 77.5 us -> 32.5 us  [line_scatter(): right = lax.ppermute(send_right, 'wide', pairs(t, 1))]
    reduce_scatter x0 -> x2, waiting for transfers between devices: none -> 26.1 us  [wide_scatter(): lax.psum_scatter(value[:, :half], 'wide', scatter_dimension=0, tiled=True)]
    ppermute x16 -> x8, waiting for transfers between devices: 71.6 us -> 97.1 us  [line_scatter(): right = lax.ppermute(send_right, 'wide', pairs(t, 1))]
    all_gather x2, waiting for transfers between devices: 105 us -> 96.2 us  [attend_step(): lax.all_gather(attended, 'wide', axis=0, tiled=True)]
    ppermute x16 -> x8, starting transfers between devices: 16.2 us -> 8.07 us  [line_scatter(): left = lax.ppermute(send_left, 'wide', pairs(t, -1))]
    ppermute x16 -> x8, waiting for transfers between devices: 26.5 us -> 23.5 us  [line_scatter(): left = lax.ppermute(send_left, 'wide', pairs(t, -1))]
    unnamed x36 -> x45, local copies, waits for them, and re-layouts: 21.3 us -> 21 us
  transfers between devices with their start and end apart: 38 -> 24, of which waited for: 24 -> 19; matrix products, arithmetic and copies ran while one was open for 4% -> 4% of each run, Pallas kernels for 0% -> 0%
where the time goes in v5:
time: 515 us; the launch traced here: 514 us
  waiting for transfers between devices  324 us (63%)
  matrix products  87.3 us (17%)
  starting transfers between devices  41.4 us (8%)
  local copies, waits for them, and re-layouts  25 us (5%)
  other arithmetic  22.7 us (4%)
  between operations  14.3 us (3%)
    ppermute x8, waiting for transfers between devices, line_scatter(): right = lax.ppermute(send_right, 'wide', pairs(t, 1))  97.1 us
    all_gather x2, waiting for transfers between devices, attend_step(): lax.all_gather(attended, 'wide', axis=0, tiled=True)  96.2 us
    reduce_scatter x2, waiting for transfers between devices, on_device(): lax.psum_scatter(partial_value, 'narrow', scatter_dimension=0, tiled=True)  60.1 us
    ppermute x8, starting transfers between devices, line_scatter(): right = lax.ppermute(send_right, 'wide', pairs(t, 1))  32.5 us
    reduce_scatter x2, waiting for transfers between devices, wide_scatter(): lax.psum_scatter(value[:, :half], 'wide', scatter_dimension=0, tiled=True)  26.1 us
    dot_general x2, matrix products, attend_step(): jnp.einsum('rgjd,rgcd->rgjc', query, key_cache, preferred_element_type=jn...  24.6 us
    dot_general x2, matrix products, attend_step(): jnp.dot(lax.all_gather(attended, 'wide', axis=0, tiled=True), w_out, pref...  24.5 us
    ppermute x8, waiting for transfers between devices, line_scatter(): left = lax.ppermute(send_left, 'wide', pairs(t, -1))  23.5 us
  transfers between devices with their start and end apart: 24, of which 19 were waited for; matrix products, arithmetic and copies ran while one was open for 4% of the time, Pallas kernels for 0%

profile of v5, /device:TPU:0, one launch (start us, length us, event | category | flops | bytes accessed | tf_op | source)
XLA Modules:
  0.0 514.2 jit_solution(17743957071190790821)
XLA Ops:
  7.3 17.5 %copy.59 = bf16[256,8,2,2048]{3,1,2,0:T(8,128)(2,1)} copy(bf16[256,8,2,2048]{3,2,1,0:T(2,128)(2,1)} %bitcast.107) | data formatting | bytes 33554432
  25.3 3.0 all-gather.5.cloned.1.call-done
  28.4 10.4 %fusion.67 = f32[256,4096]{1,0:T(8,128)S(1)} fusion(bf16[256,2048]{1,0:T(8,128)(2,1)} %all-gather.5.cloned.1.call-done, bf16[2048,4096]{1,0:T(8,128)(2,1)} %bitcast.108), kind=kOutput, calls=%fused_computation.128 | convolution fusion | flops 4294967296 | bytes 22020096 | tf_op jit(solution)/shard_map/dot_general | solution.py:81
  39.6 1.8 fusion.63
  41.3 1.7 dynamic-slice_bitcast_fusion.3
  43.1 3.4 collective-permute-start
  46.5 1.3 collective-permute-start.1
  47.9 24.5 %collective-permute-done = f32[4,32,2304]{2,1,0:T(8,128)S(1)} collective-permute-done((f32[4,32,2304]{2,1,0:T(8,128)}, f32[4,32,2304]{2,1,0:T(8,128)S(1)}, u32[]{:S(2)}, u32[]{:S(2)}) %collective-permute-start) | collective-permute-done | bytes 1179680 | tf_op jit(solution)/shard_map/ppermute | solution.py:41
  73.5 3.1 collective-permute-done.1
  76.6 1.8 fusion.22
  78.4 3.4 collective-permute-start.2
  82.6 8.7 %collective-permute-done.2 = f32[32,2304]{1,0:T(8,128)S(1)} collective-permute-done((f32[32,2304]{1,0:T(8,128)S(1)}, f32[32,2304]{1,0:T(8,128)S(1)}, u32[]{:S(2)}, u32[]{:S(2)}) %collective-permute-start.2) | collective-permute-done | bytes 294944 | tf_op jit(solution)/shard_map/ppermute | solution.py:41
  91.4 4.4 collective-permute-start.3
  95.8 11.7 %collective-permute-done.3 = f32[32,2304]{1,0:T(8,128)S(1)} collective-permute-done((f32[32,2304]{1,0:T(8,128)S(1)}, f32[32,2304]{1,0:T(8,128)S(1)}, u32[]{:S(2)}, u32[]{:S(2)}) %collective-permute-start.3) | collective-permute-done | bytes 294944 | tf_op jit(solution)/shard_map/ppermute | solution.py:41
  108.4 5.0 collective-permute-start.4
  113.5 1.5 collective-permute-start.7
  115.7 3.2 collective-permute-done.4
  118.9 7.4 %collective-permute-done.7 = f32[32,2304]{1,0:T(8,128)S(1)} collective-permute-done((f32[32,2304]{1,0:T(8,128)S(1)}, f32[32,2304]{1,0:T(8,128)S(1)}, u32[]{:S(2)}, u32[]{:S(2)}) %collective-permute-start.7) | collective-permute-done | bytes 294944 | tf_op jit(solution)/shard_map/ppermute | solution.py:42
  127.3 26.1 %reduce-scatter.5.cloned.1.call-done = f32[32,2304]{1,0:T(8,128)} async-done(((f32[256,2304]{1,0:T(8,128)}), f32[32,2304]{1,0:T(8,128)}) %reduce-scatter.5.cloned.1.call-update) | async-done | bytes 294928 | tf_op jit(solution)/shard_map/reduce_scatter | solution.py:67
  155.1 12.4 %fusion = (f32[32,2,16]{2,1,0:T(2,128)S(1)}, f32[32,2,16,1024]{3,2,1,0:T(8,128)}) fusion(pred[32,1024]{1,0:T(8,128)(4,1)S(1)} %iota_compare_fusion, bf16[32,2,1024,128]{3,2,1,0:T(8,128)(2,1)} %param.11, bf16[32,2,16,64]{3,2,1,0:T(8,128)(2,1)S(1)} %get-tuple-element.24, bf16[32,2,16,64]{3,2,1,0:T(8,128)(2,1)S(1)} %get-tuple-element.23), kind=kOutput, calls=%fused_computation.6 | convolution fusion | flops 272104448 | bytes 21270528 | tf_op jit(solution)/shard_map/rgjd,rgcd->rgjc/dot_general | solution.py:96
  167.5 3.8 fusion.2
  171.3 7.5 %fusion.19 = bf16[32,2,16,128]{3,2,1,0:T(8,128)(2,1)S(1)} fusion(bf16[32,2,1024,128]{3,2,1,0:T(8,128)(2,1)} %param.12, f32[32,2,16,1024]{3,2,1,0:T(8,128)S(1)} %copy-done.1, f32[32,2,16]{2,1,0:T(2,128)S(1)} %get-tuple-element.28, f32[32,2,16]{2,1,0:T(2,128)S(1)} %multiply_maximum_fusion, pred[32,1024]{1,0:T(8,128)(4,1)S(1)} %iota_compare_fusion, ...), kind=kOutput, calls=%fused_computation.28 | convolution fusion | flops 275120128 | bytes 21311488 | tf_op jit(solution)/shard_map/rgjc,rgcd->rgjd/dot_general | solution.py:108
  179.7 48.5 %all-gather.7.cloned.1.call-done = bf16[256,4096]{1,0:T(8,128)(2,1)} async-done(((bf16[32,4096]{1,0:T(8,128)(2,1)}), bf16[256,4096]{1,0:T(8,128)(2,1)}) %all-gather.7.cloned.1.call-update) | async-done | bytes 2097168 | tf_op jit(solution)/shard_map/all_gather | solution.py:112
  228.2 12.2 %fusion.69 = f32[256,2048]{1,0:T(8,128)} fusion(bf16[256,4096]{1,0:T(8,128)(2,1)} %all-gather.7.cloned.1.call-done, bf16[4096,2048]{1,0:T(8,128)(2,1)} %param.10), kind=kOutput, calls=%fused_computation.130 | convolution fusion | flops 4294967296 | bytes 20971520 | tf_op jit(solution)/shard_map/dot_general | solution.py:111
  240.5 30.0 %reduce-scatter.7.cloned.1.call-done = f32[64,2048]{1,0:T(8,128)} async-done(((f32[256,2048]{1,0:T(8,128)}), f32[64,2048]{1,0:T(8,128)}) %reduce-scatter.7.cloned.1.call-update) | async-done | bytes 524304 | tf_op jit(solution)/shard_map/reduce_scatter | solution.py:138
  270.5 1.8 add_convert_fusion.2
  272.6 16.6 %all-gather.9.cloned.1.call-done = bf16[256,2048]{1,0:T(8,128)(2,1)} async-done(((bf16[64,2048]{1,0:T(8,128)(2,1)}), bf16[256,2048]{1,0:T(8,128)(2,1)}) %all-gather.9.cloned.1.call-update) | async-done | bytes 1048592 | tf_op jit(solution)/shard_map/all_gather | solution.py:126
  289.2 10.5 %fusion.70 = f32[256,4096]{1,0:T(8,128)S(1)} fusion(bf16[256,2048]{1,0:T(8,128)(2,1)} %all-gather.9.cloned.1.call-done, bf16[2048,4096]{1,0:T(8,128)(2,1)} %bitcast.109), kind=kOutput, calls=%fused_computation.131 | convolution fusion | flops 4294967296 | bytes 22020096 | tf_op jit(solution)/shard_map/dot_general | solution.py:81
  300.4 1.7 fusion.62
  302.1 1.7 dynamic-slice_bitcast_fusion.1
  303.8 3.4 collective-permute-start.8
  308.7 30.8 %collective-permute-done.8 = f32[4,32,2304]{2,1,0:T(8,128)S(1)} collective-permute-done((f32[4,32,2304]{2,1,0:T(8,128)}, f32[4,32,2304]{2,1,0:T(8,128)S(1)}, u32[]{:S(2)}, u32[]{:S(2)}) %collective-permute-start.8) | collective-permute-done | bytes 1179680 | tf_op jit(solution)/shard_map/ppermute | solution.py:41
  339.4 4.2 collective-permute-done.9
  343.6 1.4 fusion.21
  345.1 3.4 collective-permute-start.10
  349.2 4.8 collective-permute-done.10
  354.1 4.4 collective-permute-start.11
  358.5 4.6 collective-permute-done.11
  363.8 5.0 collective-permute-start.12
  370.3 8.8 %collective-permute-done.12 = f32[32,2304]{1,0:T(8,128)S(1)} collective-permute-done((f32[32,2304]{1,0:T(8,128)S(1)}, f32[32,2304]{1,0:T(8,128)S(1)}, u32[]{:S(2)}, u32[]{:S(2)}) %collective-permute-start.12) | collective-permute-done | bytes 294944 | tf_op jit(solution)/shard_map/ppermute | solution.py:41
  379.2 8.8 %collective-permute-done.15 = f32[32,2304]{1,0:T(8,128)S(1)} collective-permute-done((f32[32,2304]{1,0:T(8,128)S(1)}, f32[32,2304]{1,0:T(8,128)S(1)}, u32[]{:S(2)}, u32[]{:S(2)}) %collective-permute-start.15) | collective-permute-done | bytes 294944 | tf_op jit(solution)/shard_map/ppermute | solution.py:42
  389.8 12.2 %fusion.1 = (f32[32,2,16]{2,1,0:T(2,128)S(1)}, f32[32,2,16,1024]{3,2,1,0:T(8,128)}) fusion(pred[32,1024]{1,0:T(8,128)(4,1)S(1)} %copy-done.9, bf16[32,2,1024,128]{3,2,1,0:T(8,128)(2,1)} %param.11, bf16[32,2,16,64]{3,2,1,0:T(8,128)(2,1)S(1)} %get-tuple-element.22, bf16[32,2,16,64]{3,2,1,0:T(8,128)(2,1)S(1)} %get-tuple-element.21), kind=kOutput, calls=%fused_computation.7 | convolution fusion | flops 272104448 | bytes 21270528 | tf_op jit(solution)/shard_map/rgjd,rgcd->rgjc/dot_general | solution.py:96
  402.7 3.9 fusion.3
  406.7 7.3 %fusion.5 = f32[32,2,16,128]{3,2,1,0:T(8,128)S(1)} fusion(bf16[32,2,1024,128]{3,2,1,0:T(8,128)(2,1)} %param.12, f32[32,2,16,1024]{3,2,1,0:T(8,128)S(1)} %copy-done, f32[32,2,16]{2,1,0:T(2,128)S(1)} %add.215, f32[32,2,16]{2,1,0:T(2,128)S(1)} %max.54, pred[32,1024]{1,0:T(8,128)(4,1)S(1)} %copy-done.9), kind=kOutput, calls=%fused_computation.13 | convolution fusion | flops 274726912 | bytes 21536768 | tf_op jit(solution)/shard_map/rgjc,rgcd->rgjd/dot_general | solution.py:108
  415.5 47.8 %all-gather.11.cloned.1.call-done = bf16[256,4096]{1,0:T(8,128)(2,1)} async-done(((bf16[32,4096]{1,0:T(8,128)(2,1)}), bf16[256,4096]{1,0:T(8,128)(2,1)}) %all-gather.11.cloned.1.call-update) | async-done | bytes 2097168 | tf_op jit(solution)/shard_map/all_gather | solution.py:112
  463.3 12.2 %fusion.72 = f32[256,2048]{1,0:T(8,128)} fusion(bf16[256,4096]{1,0:T(8,128)(2,1)} %all-gather.11.cloned.1.call-done, bf16[4096,2048]{1,0:T(8,128)(2,1)} %param.10), kind=kOutput, calls=%fused_computation.133 | convolution fusion | flops 4294967296 | bytes 20971520 | tf_op jit(solution)/shard_map/dot_general | solution.py:111
  475.5 30.1 %reduce-scatter.11.cloned.1.call-done = f32[64,2048]{1,0:T(8,128)} async-done(((f32[256,2048]{1,0:T(8,128)}), f32[64,2048]{1,0:T(8,128)}) %reduce-scatter.11.cloned.1.call-update) | async-done | bytes 524304 | tf_op jit(solution)/shard_map/reduce_scatter | solution.py:138
  505.6 1.8 add_convert_fusion
  (118 shorter events, 18.3 us)
Async XLA Ops:
  6.5 21.8 %all-gather.5.cloned.1.call-start = ((), (), s32[]{:S(2)}) async-start(), calls=%async_computation.4 | async-start | bytes 1310720 | tf_op jit(solution)/shard_map/all_gather | solution.py:126
  7.3 146.1 %reduce-scatter.5.cloned.1.call-start = ((), (), s32[]{:S(2)}) async-start(), calls=%async_computation.5 | async-start | bytes 2654208 | tf_op jit(solution)/shard_map/reduce_scatter | solution.py:67
  7.3 17.5 %copy-start.3 = (bf16[2048,2,256]{2,1,0:T(2,128)(2,1)S(1)}, bf16[2048,2,256]{2,1,0:T(2,128)(2,1)}, u32[]{:S(2)}) copy-start(bf16[2048,2,256]{2,1,0:T(2,128)(2,1)} %param.9) | copy-start | bytes 6291460
  25.3 13.5 %copy-start.4 = (bf16[256,8,2,256]{3,1,2,0:T(8,128)(2,1)}, bf16[256,8,2,256]{3,1,2,0:T(8,128)(2,1)S(1)}, u32[]{:S(2)}) copy-start(bf16[256,8,2,256]{3,1,2,0:T(8,128)(2,1)S(1)} %copy.60) | copy-start | bytes 6291460
  28.4 10.5 %copy-start.17 = (bf16[256,2048]{1,0:T(8,128)(2,1)S(1)}, bf16[256,2048]{1,0:T(8,128)(2,1)}, u32[]{:S(2)}) copy-start(bf16[256,2048]{1,0:T(8,128)(2,1)} %all-gather.5.cloned.1.call-done) | copy-start | bytes 3145732
  43.1 29.3 %collective-permute-start = (f32[4,32,2304]{2,1,0:T(8,128)}, f32[4,32,2304]{2,1,0:T(8,128)S(1)}, u32[]{:S(2)}, u32[]{:S(2)}) collective-permute-start(f32[4,32,2304]{2,1,0:T(8,128)} %get-tuple-element.11), channel_id=1, source_target_pairs={{0,1},{2,3},{4,5},{6,7},{8,9},{10,11},{12,13},{14,15},{16,17},{18,... | collective-permute-start | bytes 3538952 | tf_op jit(solution)/shard_map/ppermute | solution.py:41
  46.5 30.0 %collective-permute-start.1 = (f32[4,32,2304]{2,1,0:T(8,128)}, f32[4,32,2304]{2,1,0:T(8,128)}, u32[]{:S(2)}, u32[]{:S(2)}) collective-permute-start(f32[4,32,2304]{2,1,0:T(8,128)} %get-tuple-element.12), channel_id=1, source_target_pairs={{1,0},{3,2},{5,4},{7,6},{9,8},{11,10},{13,12},{15,14},{17,16},{19,... | collective-permute-start | bytes 3538952 | tf_op jit(solution)/shard_map/ppermute | solution.py:42
  72.4 1.1 copy-start.6
  78.4 29.9 %copy-start.16 = (s32[32]{0:T(128)S(1)}, s32[32]{0:T(128)}, u32[]{:S(2)}) copy-start(s32[32]{0:T(128)} %param.13) | copy-start | bytes 388
  78.4 12.9 %collective-permute-start.2 = (f32[32,2304]{1,0:T(8,128)S(1)}, f32[32,2304]{1,0:T(8,128)S(1)}, u32[]{:S(2)}, u32[]{:S(2)}) collective-permute-start(f32[32,2304]{1,0:T(8,128)S(1)} %get-tuple-element.19), channel_id=1, source_target_pairs={{0,2},{1,3},{8,10},{9,11},{16,18},{17,19},{24,26},{25,27}} | collective-permute-start | bytes 884744 | tf_op jit(solution)/shard_map/ppermute | solution.py:41
  81.9 146.3 %all-gather.7.cloned.1.call-start = ((), (), s32[]{:S(2)}) async-start(), calls=%async_computation.6 | async-start | bytes 2359296 | tf_op jit(solution)/shard_map/all_gather | solution.py:112
  81.9 13.9 %collective-permute-start.5 = (f32[32,2304]{1,0:T(8,128)S(1)}, f32[32,2304]{1,0:T(8,128)S(1)}, u32[]{:S(2)}, u32[]{:S(2)}) collective-permute-start(f32[32,2304]{1,0:T(8,128)S(1)} %get-tuple-element.20), channel_id=1, source_target_pairs={{6,4},{7,5},{14,12},{15,13},{22,20},{23,21},{30,28},{31,29}} | collective-permute-start | bytes 884744 | tf_op jit(solution)/shard_map/ppermute | solution.py:42
  91.4 16.1 %collective-permute-start.3 = (f32[32,2304]{1,0:T(8,128)S(1)}, f32[32,2304]{1,0:T(8,128)S(1)}, u32[]{:S(2)}, u32[]{:S(2)}) collective-permute-start(f32[32,2304]{1,0:T(8,128)S(1)} %bitcast_add_fusion.9), channel_id=1, source_target_pairs={{0,2},{2,4},{1,3},{3,5},{8,10},{10,12},{9,11},{11,13},{16,18},{18,... | collective-permute-start | bytes 884744 | tf_op jit(solution)/shard_map/ppermute | solution.py:41
  107.6 5.9 %collective-permute-start.6 = (f32[32,2304]{1,0:T(8,128)S(1)}, f32[32,2304]{1,0:T(8,128)S(1)}, u32[]{:S(2)}, u32[]{:S(2)}) collective-permute-start(f32[32,2304]{1,0:T(8,128)S(1)} %get-tuple-element.18), channel_id=1, source_target_pairs={{4,2},{6,4},{5,3},{7,5},{12,10},{14,12},{13,11},{15,13},{20,18},{2... | collective-permute-start | bytes 884744 | tf_op jit(solution)/shard_map/ppermute | solution.py:42
  108.4 62.9 %copy-start.8 = (pred[32,1024]{1,0:T(8,128)(4,1)}, pred[32,1024]{1,0:T(8,128)(4,1)S(1)}, u32[]{:S(2)}) copy-start(pred[32,1024]{1,0:T(8,128)(4,1)S(1)} %iota_compare_fusion) | copy-start | bytes 98308
  108.4 10.5 %collective-permute-start.4 = (f32[32,2304]{1,0:T(8,128)S(1)}, f32[32,2304]{1,0:T(8,128)S(1)}, u32[]{:S(2)}, u32[]{:S(2)}) collective-permute-start(f32[32,2304]{1,0:T(8,128)S(1)} %get-tuple-element.17), channel_id=1, source_target_pairs={{0,2},{2,4},{4,6},{1,3},{3,5},{5,7},{8,10},{10,12},{12,14},{9,11},... | collective-permute-start | bytes 884744 | tf_op jit(solution)/shard_map/ppermute | solution.py:41
  113.5 12.8 %collective-permute-start.7 = (f32[32,2304]{1,0:T(8,128)S(1)}, f32[32,2304]{1,0:T(8,128)S(1)}, u32[]{:S(2)}, u32[]{:S(2)}) collective-permute-start(f32[32,2304]{1,0:T(8,128)S(1)} %bitcast_add_fusion.8), channel_id=1, source_target_pairs={{2,0},{4,2},{6,4},{3,1},{5,3},{7,5},{10,8},{12,10},{14,12},{11,9},... | collective-permute-start | bytes 884744 | tf_op jit(solution)/shard_map/ppermute | solution.py:42
  127.2 27.3 %copy-start.11 = (bf16[32,2,64]{2,0,1:T(8,128)(2,1)}, bf16[32,2,64]{2,0,1:T(8,128)(2,1)S(1)}, u32[]{:S(2)}) copy-start(bf16[32,2,64]{2,0,1:T(8,128)(2,1)S(1)} %get-tuple-element.30) | copy-start | bytes 24580
  127.2 27.3 %copy-start.13 = (bf16[32,2,64]{2,0,1:T(8,128)(2,1)}, bf16[32,2,64]{2,0,1:T(8,128)(2,1)S(1)}, u32[]{:S(2)}) copy-start(bf16[32,2,64]{2,0,1:T(8,128)(2,1)S(1)} %get-tuple-element.29) | copy-start | bytes 24580
  167.4 3.9 copy-start.1
  179.6 90.9 %copy-start.7 = (bf16[64,2048]{1,0:T(8,128)(2,1)S(1)}, bf16[64,2048]{1,0:T(8,128)(2,1)}, u32[]{:S(2)}) copy-start(bf16[64,2048]{1,0:T(8,128)(2,1)} %param.7) | copy-start | bytes 786436
  179.7 90.9 %reduce-scatter.7.cloned.1.call-start = ((), (), s32[]{:S(2)}) async-start(), calls=%async_computation.7 | async-start | bytes 2621440 | tf_op jit(solution)/shard_map/reduce_scatter | solution.py:138
  240.4 48.8 %all-gather.9.cloned.1.call-start = ((), (), s32[]{:S(2)}) async-start(), calls=%async_computation.8 | async-start | bytes 1310720 | tf_op jit(solution)/shard_map/all_gather | solution.py:126
  272.3 27.3 %copy-start.5 = (bf16[256,8,2,256]{3,1,2,0:T(8,128)(2,1)S(1)}, bf16[256,8,2,256]{3,1,2,0:T(8,128)(2,1)}, u32[]{:S(2)}) copy-start(bf16[256,8,2,256]{3,1,2,0:T(8,128)(2,1)} %copy-done.4) | copy-start | bytes 6291460
  272.4 116.1 %reduce-scatter.9.cloned.1.call-start = ((), (), s32[]{:S(2)}) async-start(), calls=%async_computation.9 | async-start | bytes 2654208 | tf_op jit(solution)/shard_map/reduce_scatter | solution.py:67
  289.2 10.5 %copy-start.18 = (bf16[256,2048]{1,0:T(8,128)(2,1)S(1)}, bf16[256,2048]{1,0:T(8,128)(2,1)}, u32[]{:S(2)}) copy-start(bf16[256,2048]{1,0:T(8,128)(2,1)} %all-gather.9.cloned.1.call-done) | copy-start | bytes 3145732
  303.8 35.6 %collective-permute-start.8 = (f32[4,32,2304]{2,1,0:T(8,128)}, f32[4,32,2304]{2,1,0:T(8,128)S(1)}, u32[]{:S(2)}, u32[]{:S(2)}) collective-permute-start(f32[4,32,2304]{2,1,0:T(8,128)} %get-tuple-element.9), channel_id=1, source_target_pairs={{0,1},{2,3},{4,5},{6,7},{8,9},{10,11},{12,13},{14,15},{16,17},{18,... | collective-permute-start | bytes 3538952 | tf_op jit(solution)/shard_map/ppermute | solution.py:41
  307.2 36.4 %collective-permute-start.9 = (f32[4,32,2304]{2,1,0:T(8,128)}, f32[4,32,2304]{2,1,0:T(8,128)}, u32[]{:S(2)}, u32[]{:S(2)}) collective-permute-start(f32[4,32,2304]{2,1,0:T(8,128)} %get-tuple-element.10), channel_id=1, source_target_pairs={{1,0},{3,2},{5,4},{7,6},{9,8},{11,10},{13,12},{15,14},{17,16},{19,... | collective-permute-start | bytes 3538952 | tf_op jit(solution)/shard_map/ppermute | solution.py:42
  308.6 154.7 %all-gather.11.cloned.1.call-start = ((), (), s32[]{:S(2)}) async-start(), calls=%async_computation.10 | async-start | bytes 2359296 | tf_op jit(solution)/shard_map/all_gather | solution.py:112
  308.6 61.6 %copy-start.14 = (bf16[32,2,64]{2,0,1:T(8,128)(2,1)S(1)}, bf16[32,2,64]{2,0,1:T(8,128)(2,1)}, u32[]{:S(2)}) copy-start(bf16[32,2,64]{2,0,1:T(8,128)(2,1)} %copy-done.13) | copy-start | bytes 24580
  308.6 61.6 %copy-start.12 = (bf16[32,2,64]{2,0,1:T(8,128)(2,1)S(1)}, bf16[32,2,64]{2,0,1:T(8,128)(2,1)}, u32[]{:S(2)}) copy-start(bf16[32,2,64]{2,0,1:T(8,128)(2,1)} %copy-done.11) | copy-start | bytes 24580
  308.6 61.6 %copy-start.15 = (bf16[32,2,1,128]{3,0,2,1:T(8,128)(2,1)S(1)}, bf16[32,2,1,128]{3,0,2,1:T(8,128)(2,1)}, u32[]{:S(2)}) copy-start(bf16[32,2,1,128]{3,0,2,1:T(8,128)(2,1)} %get-tuple-element.35) | copy-start | bytes 49156
  345.1 43.2 %copy-start.10 = (f32[32,64]{1,0:T(8,128)S(1)}, f32[32,64]{1,0:T(8,128)}, u32[]{:S(2)}) copy-start(f32[32,64]{1,0:T(8,128)} %get-tuple-element.38) | copy-start | bytes 24580
  345.1 8.9 %collective-permute-start.10 = (f32[32,2304]{1,0:T(8,128)S(1)}, f32[32,2304]{1,0:T(8,128)S(1)}, u32[]{:S(2)}, u32[]{:S(2)}) collective-permute-start(f32[32,2304]{1,0:T(8,128)S(1)} %get-tuple-element.15), channel_id=1, source_target_pairs={{0,2},{1,3},{8,10},{9,11},{16,18},{17,19},{24,26},{25,27}} | collective-permute-start | bytes 884744 | tf_op jit(solution)/shard_map/ppermute | solution.py:41
  348.5 10.0 %collective-permute-start.13 = (f32[32,2304]{1,0:T(8,128)S(1)}, f32[32,2304]{1,0:T(8,128)S(1)}, u32[]{:S(2)}, u32[]{:S(2)}) collective-permute-start(f32[32,2304]{1,0:T(8,128)S(1)} %get-tuple-element.16), channel_id=1, source_target_pairs={{6,4},{7,5},{14,12},{15,13},{22,20},{23,21},{30,28},{31,29}} | collective-permute-start | bytes 884744 | tf_op jit(solution)/shard_map/ppermute | solution.py:42
  354.1 35.7 %copy-start.9 = (pred[32,1024]{1,0:T(8,128)(4,1)S(1)}, pred[32,1024]{1,0:T(8,128)(4,1)}, u32[]{:S(2)}) copy-start(pred[32,1024]{1,0:T(8,128)(4,1)} %copy-done.8) | copy-start | bytes 98308
  354.1 9.0 %collective-permute-start.11 = (f32[32,2304]{1,0:T(8,128)S(1)}, f32[32,2304]{1,0:T(8,128)S(1)}, u32[]{:S(2)}, u32[]{:S(2)}) collective-permute-start(f32[32,2304]{1,0:T(8,128)S(1)} %bitcast_add_fusion.4), channel_id=1, source_target_pairs={{0,2},{2,4},{1,3},{3,5},{8,10},{10,12},{9,11},{11,13},{16,18},{18,... | collective-permute-start | bytes 884744 | tf_op jit(solution)/shard_map/ppermute | solution.py:41
  363.1 5.7 %collective-permute-start.14 = (f32[32,2304]{1,0:T(8,128)S(1)}, f32[32,2304]{1,0:T(8,128)S(1)}, u32[]{:S(2)}, u32[]{:S(2)}) collective-permute-start(f32[32,2304]{1,0:T(8,128)S(1)} %get-tuple-element.14), channel_id=1, source_target_pairs={{4,2},{6,4},{5,3},{7,5},{12,10},{14,12},{13,11},{15,13},{20,18},{2... | collective-permute-start | bytes 884744 | tf_op jit(solution)/shard_map/ppermute | solution.py:42
  363.8 15.4 %collective-permute-start.12 = (f32[32,2304]{1,0:T(8,128)S(1)}, f32[32,2304]{1,0:T(8,128)S(1)}, u32[]{:S(2)}, u32[]{:S(2)}) collective-permute-start(f32[32,2304]{1,0:T(8,128)S(1)} %get-tuple-element.13), channel_id=1, source_target_pairs={{0,2},{2,4},{4,6},{1,3},{3,5},{5,7},{8,10},{10,12},{12,14},{9,11},... | collective-permute-start | bytes 884744 | tf_op jit(solution)/shard_map/ppermute | solution.py:41
  368.9 19.1 %collective-permute-start.15 = (f32[32,2304]{1,0:T(8,128)S(1)}, f32[32,2304]{1,0:T(8,128)S(1)}, u32[]{:S(2)}, u32[]{:S(2)}) collective-permute-start(f32[32,2304]{1,0:T(8,128)S(1)} %bitcast_add_fusion.3), channel_id=1, source_target_pairs={{2,0},{4,2},{6,4},{3,1},{5,3},{7,5},{10,8},{12,10},{14,12},{11,9},... | collective-permute-start | bytes 884744 | tf_op jit(solution)/shard_map/ppermute | solution.py:42
  402.0 4.7 copy-start
  415.2 90.4 %copy-start.2 = (bf16[64,2048]{1,0:T(8,128)(2,1)S(1)}, bf16[64,2048]{1,0:T(8,128)(2,1)}, u32[]{:S(2)}) copy-start(bf16[64,2048]{1,0:T(8,128)(2,1)} %add_convert_fusion.2) | copy-start | bytes 786436
  415.2 90.4 %reduce-scatter.11.cloned.1.call-start = ((), (), s32[]{:S(2)}) async-start(), calls=%async_computation.11 | async-start | bytes 2621440 | tf_op jit(solution)/shard_map/reduce_scatter | solution.py:138
Sparse Core Ops, SparseCore 0:
  8.9 19.4 all-gather.4
  82.0 71.3 reduce-scatter.4
  179.8 48.3 all-gather.6
  240.6 29.9 reduce-scatter.6
  272.5 16.6 all-gather.8
  308.7 77.6 reduce-scatter.8
  415.3 47.9 all-gather.10
  475.6 29.9 reduce-scatter.10

commit v6 on v1

--- a/solution.py
+++ b/solution.py
@@ -1,6 +1,8 @@
 import jax
 import jax.numpy as jnp
 from jax import lax
+from jax.experimental import pallas as pl
+from jax.experimental.pallas import tpu as pltpu
 from jax.sharding import PartitionSpec as P
 
 STEPS = 2
@@ -21,6 +23,67 @@
     return jnp.concatenate(
         (first * cosine - second * sine, second * cosine + first * sine), axis=-1
     )
+
+
+def attention_kernel(len_ref, q_ref, k_ref, v_ref, kn_ref, vn_ref, o_ref):
+    groups, per_group, head_dim = q_ref.shape[1:]
+    slots = k_ref.shape[2]
+    fresh_count = kn_ref.shape[2]
+    scale = 1.0 / head_dim**0.5
+    length = len_ref[pl.program_id(0)]
+    live = lax.broadcasted_iota(jnp.int32, (per_group, slots), 1) < length
+    for g in range(groups):
+        q = q_ref[0, g]
+        cached = lax.dot_general(
+            q, k_ref[0, g], (((1,), (1,)), ((), ())), preferred_element_type=jnp.float32
+        ) * scale
+        cached = jnp.where(live, cached, -1e30)
+        qf = q.astype(jnp.float32)
+        kn = kn_ref[0, g].astype(jnp.float32)
+        vn = vn_ref[0, g].astype(jnp.float32)
+        fresh = [
+            jnp.sum(qf * kn[s : s + 1, :], axis=-1, keepdims=True) * scale
+            for s in range(fresh_count)
+        ]
+        top = jnp.max(cached, axis=-1, keepdims=True)
+        for f in fresh:
+            top = jnp.maximum(top, f)
+        e_cached = jnp.where(live, jnp.exp(cached - top), 0.0)
+        e_fresh = [jnp.exp(f - top) for f in fresh]
+        total = jnp.sum(e_cached, axis=-1, keepdims=True)
+        for e in e_fresh:
+            total = total + e
+        p_cached = (e_cached / total).astype(jnp.bfloat16)
+        out = jnp.dot(p_cached, v_ref[0, g], preferred_element_type=jnp.float32)
+        fresh_out = None
+        for s, e in enumerate(e_fresh):
+            p = (e / total).astype(jnp.bfloat16).astype(jnp.float32)
+            term = p * vn[s : s + 1, :]
+            fresh_out = term if fresh_out is None else fresh_out + term
+        o_ref[0, g] = (out + fresh_out).astype(o_ref.dtype)
+
+
+def attention(query, key_cache, value_cache, keys_now, vals_now, lengths):
+    rows, groups, per_group, head_dim = query.shape
+    slots = key_cache.shape[2]
+    fresh_count = keys_now.shape[2]
+    row_map = lambda r, lens: (r, 0, 0, 0)
+    return pl.pallas_call(
+        attention_kernel,
+        out_shape=jax.ShapeDtypeStruct(query.shape, jnp.bfloat16),
+        grid_spec=pltpu.PrefetchScalarGridSpec(
+            num_scalar_prefetch=1,
+            grid=(rows,),
+            in_specs=[
+                pl.BlockSpec((1, groups, per_group, head_dim), row_map),
+                pl.BlockSpec((1, groups, slots, head_dim), row_map),
+                pl.BlockSpec((1, groups, slots, head_dim), row_map),
+                pl.BlockSpec((1, groups, fresh_count, head_dim), row_map),
+                pl.BlockSpec((1, groups, fresh_count, head_dim), row_map),
+            ],
+            out_specs=pl.BlockSpec((1, groups, per_group, head_dim), row_map),
+        ),
+    )(lengths, query, key_cache, value_cache, keys_now, vals_now)
 
 
 def attend_step(every, step, w_q2, w_kv2, w_out, key_cache, value_cache, lengths, new_keys, new_vals):
@@ -44,24 +107,9 @@
     new_vals.append(kv[:, :, head_dim:].astype(jnp.bfloat16))
     keys_now = jnp.stack(new_keys, axis=2)
     vals_now = jnp.stack(new_vals, axis=2)
-    scale = 1.0 / head_dim**0.5
-    live = (jnp.arange(slots, dtype=jnp.int32)[None, :] < lengths[:, None])[:, None, None, :]
-    cached = (
-        jnp.einsum("rgjd,rgcd->rgjc", query, key_cache, preferred_element_type=jnp.float32) * scale
+    attended = attention(query, key_cache, value_cache, keys_now, vals_now, lengths).reshape(
+        local_rows, groups * per_group * head_dim
     )
-    cached = jnp.where(live, cached, -1e30)
-    fresh = (
-        jnp.einsum("rgjd,rgsd->rgjs", query, keys_now, preferred_element_type=jnp.float32) * scale
-    )
-    top = jnp.maximum(jnp.max(cached, axis=-1), jnp.max(fresh, axis=-1))
-    e_cached = jnp.where(live, jnp.exp(cached - top[..., None]), 0.0)
-    e_fresh = jnp.exp(fresh - top[..., None])
-    total = jnp.sum(e_cached, axis=-1) + jnp.sum(e_fresh, axis=-1)
-    p_cached = (e_cached / total[..., None]).astype(jnp.bfloat16)
-    p_fresh = (e_fresh / total[..., None]).astype(jnp.bfloat16)
-    out = jnp.einsum("rgjc,rgcd->rgjd", p_cached, value_cache, preferred_element_type=jnp.float32)
-    out = out + jnp.einsum("rgjs,rgsd->rgjd", p_fresh, vals_now, preferred_element_type=jnp.float32)
-    attended = out.astype(jnp.bfloat16).reshape(local_rows, groups * per_group * head_dim)
     return jnp.dot(
         lax.all_gather(attended, "wide", axis=0, tiled=True),
         w_out,

time: 513 us -> 546 us (1.064)
  Pallas kernels: 0 us -> 73.5 us
  matrix products: 87.3 us -> 47 us
    pallas_call x0 -> x2, Pallas kernels: none -> 73.5 us  [attention(): pl.pallas_call(attention_kernel, out_shape=jax.ShapeDtypeStruct(query.sha...]
    dot_general x7 -> x0, matrix products: 40.4 us -> none  [the longest x2 24.5 us: attend_step(): jnp.einsum('rgjd,rgcd->rgjc', query, key_cache, preferred_element_type=jn...]
    reduce_sum x3 -> x0, other arithmetic: 7.85 us -> none  [attend_step(): total = jnp.sum(e_cached, axis=-1) + jnp.sum(e_fresh, axis=-1)]
    unnamed x25 -> x24, local copies, waits for them, and re-layouts: 22.6 us -> 24.5 us
  transfers between devices with their start and end apart: 8 -> 8, of which waited for: 8 -> 8; matrix products, arithmetic and copies ran while one was open for 4% -> 3% of each run, Pallas kernels for 0% -> 0%
where the time goes in v6:
time: 546 us; the launch traced here: 544 us
  waiting for transfers between devices  369 us (68%)
  Pallas kernels  73.5 us (13%)
  matrix products  47 us (9%)
  local copies, waits for them, and re-layouts  27.2 us (5%)
  between operations  13.7 us (3%)
  other arithmetic  12.7 us (2%)
    reduce_scatter x2, waiting for transfers between devices, attend_step(): lax.psum_scatter(jnp.concatenate((part_q, part_kv), axis=1), 'wide', scat...  190 us
    all_gather x2, waiting for transfers between devices, attend_step(): lax.all_gather(attended, 'wide', axis=0, tiled=True)  98.3 us
    pallas_call x2, Pallas kernels, attention(): pl.pallas_call(attention_kernel, out_shape=jax.ShapeDtypeStruct(query.sha...  73.5 us
    reduce_scatter x2, waiting for transfers between devices, on_device(): lax.psum_scatter(partial_value, 'narrow', scatter_dimension=0, tiled=True)  60.1 us
    unnamed x24, local copies, waits for them, and re-layouts  24.5 us
    dot_general x2, matrix products, attend_step(): jnp.dot(lax.all_gather(attended, 'wide', axis=0, tiled=True), w_out, pref...  24.4 us
    dot_general x2, matrix products, attend_step(): part_q = jnp.dot(every, w_q2, preferred_element_type=jnp.float32)  21.1 us
    all_gather x2, waiting for transfers between devices, on_device(): lax.all_gather(result, 'narrow', axis=0, tiled=True)  19.7 us
  transfers between devices with their start and end apart: 8, of which 8 were waited for; matrix products, arithmetic and copies ran while one was open for 3% of the time, Pallas kernels for 0%

profile of v6, /device:TPU:0, one launch (start us, length us, event | category | flops | bytes accessed | tf_op | source)
XLA Modules:
  0.0 543.6 jit_solution(10624880353921070032)
XLA Ops:
  6.5 0.7 all-gather.5.cloned.1.call-update
  7.3 17.5 %copy.53 = bf16[256,8,2,2048]{3,1,2,0:T(8,128)(2,1)} copy(bf16[256,8,2,2048]{3,2,1,0:T(2,128)(2,1)} %bitcast.52) | data formatting | bytes 33554432
  24.8 0.5 copy.54
  25.3 3.0 all-gather.5.cloned.1.call-done
  28.4 10.5 %fusion.8 = f32[256,4096]{1,0:T(8,128)S(1)} fusion(bf16[256,2048]{1,0:T(8,128)(2,1)} %all-gather.5.cloned.1.call-done, bf16[2048,4096]{1,0:T(8,128)(2,1)} %bitcast.53), kind=kOutput, calls=%fused_computation.37 | convolution fusion | flops 4294967296 | bytes 22020096 | tf_op jit(solution)/shard_map/dot_general | solution.py:96
  38.9 0.7 fusion.9
  39.7 2.6 pad_maximum_fusion
  42.2 0.0 all-gather.7.cloned.1.call-start
  42.3 0.6 copy-done.4
  42.9 0.2 multiply_cosine_fusion
  43.1 94.8 %reduce-scatter.5.cloned.1.call-done = f32[32,4608]{1,0:T(8,128)} async-done(((f32[256,4608]{1,0:T(8,128)}), f32[32,4608]{1,0:T(8,128)}) %reduce-scatter.5.cloned.1.call-update) | async-done | bytes 589840 | tf_op jit(solution)/shard_map/reduce_scatter | solution.py:98
  137.8 0.8 slice.67
  138.7 0.1 fusion.7
  138.9 1.1 slice_bitcast_fusion.1
  140.0 0.1 copy.55
  140.1 0.2 subtract_convert_fusion.1
  140.4 0.6 copy.37.vn_ref
  141.0 0.7 pad_maximum_fusion.4.kn_ref
  141.7 0.8 pad_maximum_fusion.2.q_ref
  142.6 36.7 %shard_map.73 = bf16[32,2,16,128]{3,2,1,0:T(8,128)(2,1)} custom-call(s32[32]{0:T(128)} %len_ref.3, bf16[32,2,16,128]{3,2,1,0:T(8,128)(2,1)} %pad_maximum_fusion.2.q_ref, bf16[32,2,1024,128]{3,2,1,0:T(8,128)(2,1)} %k_ref.3, bf16[32,2,1024,128]{3,2,1,0:T(8,128)(2,1)} %v_ref.3, bf16[32,2,1,128]{3,2,1,0:T(2,128)(2,1)} %pad_maximum_fusion.4.kn_ref, ...), custom_call_target="tpu_custom_call" | custom-call | tf_op jit(solution)/shard_map/pallas_call | solution.py:71
  179.3 1.8 copy.92
  181.1 0.0 reduce-scatter.7.cloned.1.call-start
  181.1 49.1 %all-gather.7.cloned.1.call-done = bf16[256,4096]{1,0:T(8,128)(2,1)} async-done(((bf16[32,4096]{1,0:T(8,128)(2,1)}), bf16[256,4096]{1,0:T(8,128)(2,1)}) %all-gather.7.cloned.1.call-update) | async-done | bytes 2097168 | tf_op jit(solution)/shard_map/all_gather | solution.py:114
  230.3 12.2 %fusion.10 = f32[256,2048]{1,0:T(8,128)} fusion(bf16[256,4096]{1,0:T(8,128)(2,1)} %all-gather.7.cloned.1.call-done, bf16[4096,2048]{1,0:T(8,128)(2,1)} %param.10), kind=kOutput, calls=%fused_computation.39 | convolution fusion | flops 4294967296 | bytes 20971520 | tf_op jit(solution)/shard_map/dot_general | solution.py:113
  242.5 0.0 all-gather.9.cloned.1.call-start
  242.6 30.0 %reduce-scatter.7.cloned.1.call-done = f32[64,2048]{1,0:T(8,128)} async-done(((f32[256,2048]{1,0:T(8,128)}), f32[64,2048]{1,0:T(8,128)}) %reduce-scatter.7.cloned.1.call-update) | async-done | bytes 524304 | tf_op jit(solution)/shard_map/reduce_scatter | solution.py:139
  272.6 1.8 add_convert_fusion.2
  274.4 0.2 reduce-scatter.9.cloned.1.call-start
  274.7 16.6 %all-gather.9.cloned.1.call-done = bf16[256,2048]{1,0:T(8,128)(2,1)} async-done(((bf16[64,2048]{1,0:T(8,128)(2,1)}), bf16[256,2048]{1,0:T(8,128)(2,1)}) %all-gather.9.cloned.1.call-update) | async-done | bytes 1048592 | tf_op jit(solution)/shard_map/all_gather | solution.py:128
  291.3 10.5 %fusion.11 = f32[256,4096]{1,0:T(8,128)S(1)} fusion(bf16[256,2048]{1,0:T(8,128)(2,1)} %all-gather.9.cloned.1.call-done, bf16[2048,4096]{1,0:T(8,128)(2,1)} %bitcast.54), kind=kOutput, calls=%fused_computation.40 | convolution fusion | flops 4294967296 | bytes 22020096 | tf_op jit(solution)/shard_map/dot_general | solution.py:96
  301.9 0.7 fusion.12
  302.6 2.6 pad_maximum_fusion.1
  305.2 0.0 all-gather.11.cloned.1.call-start
  305.2 95.4 %reduce-scatter.9.cloned.1.call-done = f32[32,4608]{1,0:T(8,128)} async-done(((f32[256,4608]{1,0:T(8,128)}), f32[32,4608]{1,0:T(8,128)}) %reduce-scatter.9.cloned.1.call-update) | async-done | bytes 589840 | tf_op jit(solution)/shard_map/reduce_scatter | solution.py:98
  400.6 0.8 slice.74
  401.5 0.1 fusion.6
  401.7 1.1 slice_bitcast_fusion
  402.8 0.1 copy.57
  402.9 0.2 subtract_convert_fusion
  403.2 0.9 pad_maximum_fusion.3.q_ref
  404.0 0.9 maximum_maximum_fusion
  404.9 36.8 %shard_map.74 = bf16[32,2,16,128]{3,2,1,0:T(8,128)(2,1)} custom-call(s32[32]{0:T(128)} %len_ref.3, bf16[32,2,16,128]{3,2,1,0:T(8,128)(2,1)} %pad_maximum_fusion.3.q_ref, bf16[32,2,1024,128]{3,2,1,0:T(8,128)(2,1)} %k_ref.3, bf16[32,2,1024,128]{3,2,1,0:T(8,128)(2,1)} %v_ref.3, bf16[32,2,2,128]{3,2,1,0:T(2,128)(2,1)} %get-tuple-element.25.kn_ref, ...), custom_call_target="tpu_custom_call" | custom-call | tf_op jit(solution)/shard_map/pallas_call | solution.py:71
  441.7 1.8 copy.91
  443.5 0.0 reduce-scatter.11.cloned.1.call-start
  443.5 49.1 %all-gather.11.cloned.1.call-done = bf16[256,4096]{1,0:T(8,128)(2,1)} async-done(((bf16[32,4096]{1,0:T(8,128)(2,1)}), bf16[256,4096]{1,0:T(8,128)(2,1)}) %all-gather.11.cloned.1.call-update) | async-done | bytes 2097168 | tf_op jit(solution)/shard_map/all_gather | solution.py:114
  492.7 12.2 %fusion.13 = f32[256,2048]{1,0:T(8,128)} fusion(bf16[256,4096]{1,0:T(8,128)(2,1)} %all-gather.11.cloned.1.call-done, bf16[4096,2048]{1,0:T(8,128)(2,1)} %param.10), kind=kOutput, calls=%fused_computation.42 | convolution fusion | flops 4294967296 | bytes 20971520 | tf_op jit(solution)/shard_map/dot_general | solution.py:113
  504.9 30.1 %reduce-scatter.11.cloned.1.call-done = f32[64,2048]{1,0:T(8,128)} async-done(((f32[256,2048]{1,0:T(8,128)}), f32[64,2048]{1,0:T(8,128)}) %reduce-scatter.11.cloned.1.call-update) | async-done | bytes 524304 | tf_op jit(solution)/shard_map/reduce_scatter | solution.py:139
  535.0 1.8 add_convert_fusion
  (37 shorter events, 0.5 us)
Async XLA Ops:
  6.5 21.8 %all-gather.5.cloned.1.call-start = ((), (), s32[]{:S(2)}) async-start(), calls=%async_computation.4 | async-start | bytes 1310720 | tf_op jit(solution)/shard_map/all_gather | solution.py:128
  7.3 130.6 %reduce-scatter.5.cloned.1.call-start = ((), (), s32[]{:S(2)}) async-start(), calls=%async_computation.5 | async-start | bytes 5308416 | tf_op jit(solution)/shard_map/reduce_scatter | solution.py:98
  7.3 17.5 %copy-start.1 = (bf16[2048,2,256]{2,1,0:T(2,128)(2,1)S(1)}, bf16[2048,2,256]{2,1,0:T(2,128)(2,1)}, u32[]{:S(2)}) copy-start(bf16[2048,2,256]{2,1,0:T(2,128)(2,1)} %param.9) | copy-start | bytes 6291460
  28.4 10.5 %copy-start.5 = (bf16[256,2048]{1,0:T(8,128)(2,1)S(1)}, bf16[256,2048]{1,0:T(8,128)(2,1)}, u32[]{:S(2)}) copy-start(bf16[256,2048]{1,0:T(8,128)(2,1)} %all-gather.5.cloned.1.call-done) | copy-start | bytes 3145732
  42.2 0.7 copy-start.4
  42.2 188.0 %all-gather.7.cloned.1.call-start = ((), (), s32[]{:S(2)}) async-start(), calls=%async_computation.6 | async-start | bytes 2359296 | tf_op jit(solution)/shard_map/all_gather | solution.py:114
  181.1 91.6 %copy-start.2 = (bf16[64,2048]{1,0:T(8,128)(2,1)S(1)}, bf16[64,2048]{1,0:T(8,128)(2,1)}, u32[]{:S(2)}) copy-start(bf16[64,2048]{1,0:T(8,128)(2,1)} %param.7) | copy-start | bytes 786436
  181.1 91.5 %reduce-scatter.7.cloned.1.call-start = ((), (), s32[]{:S(2)}) async-start(), calls=%async_computation.7 | async-start | bytes 2621440 | tf_op jit(solution)/shard_map/reduce_scatter | solution.py:139
  242.5 48.8 %all-gather.9.cloned.1.call-start = ((), (), s32[]{:S(2)}) async-start(), calls=%async_computation.8 | async-start | bytes 1310720 | tf_op jit(solution)/shard_map/all_gather | solution.py:128
  274.4 126.1 %reduce-scatter.9.cloned.1.call-start = ((), (), s32[]{:S(2)}) async-start(), calls=%async_computation.9 | async-start | bytes 5308416 | tf_op jit(solution)/shard_map/reduce_scatter | solution.py:98
  291.3 10.5 %copy-start.6 = (bf16[256,2048]{1,0:T(8,128)(2,1)S(1)}, bf16[256,2048]{1,0:T(8,128)(2,1)}, u32[]{:S(2)}) copy-start(bf16[256,2048]{1,0:T(8,128)(2,1)} %all-gather.9.cloned.1.call-done) | copy-start | bytes 3145732
  305.1 98.9 %copy-start.3 = (bf16[32,2,1,128]{3,2,1,0:T(2,128)(2,1)S(1)}, bf16[32,2,1,128]{3,2,1,0:T(2,128)(2,1)}, u32[]{:S(2)}) copy-start(bf16[32,2,1,128]{3,2,1,0:T(2,128)(2,1)} %copy.37.vn_ref) | copy-start | bytes 49156
  305.2 187.5 %all-gather.11.cloned.1.call-start = ((), (), s32[]{:S(2)}) async-start(), calls=%async_computation.10 | async-start | bytes 2359296 | tf_op jit(solution)/shard_map/all_gather | solution.py:114
  443.5 91.5 %copy-start = (bf16[64,2048]{1,0:T(8,128)(2,1)S(1)}, bf16[64,2048]{1,0:T(8,128)(2,1)}, u32[]{:S(2)}) copy-start(bf16[64,2048]{1,0:T(8,128)(2,1)} %add_convert_fusion.2) | copy-start | bytes 786436
  443.5 91.5 %reduce-scatter.11.cloned.1.call-start = ((), (), s32[]{:S(2)}) async-start(), calls=%async_computation.11 | async-start | bytes 2621440 | tf_op jit(solution)/shard_map/reduce_scatter | solution.py:139
Sparse Core Ops, SparseCore 0:
  8.9 19.4 all-gather.4
  42.4 95.4 reduce-scatter.4
  181.2 49.0 all-gather.6
  242.7 29.9 reduce-scatter.6
  274.6 16.6 all-gather.8
  305.3 95.2 reduce-scatter.8
  443.6 49.0 all-gather.10
  505.0 29.9 reduce-scatter.10

commit v7 on v6

--- a/solution.py
+++ b/solution.py
@@ -25,19 +25,32 @@
     )
 
 
-def attention_kernel(len_ref, q_ref, k_ref, v_ref, kn_ref, vn_ref, o_ref):
+def attention_kernel(len_ref, q_ref, k_ref, v_ref, kn_ref, vn_ref, o_ref, s_ref):
     groups, per_group, head_dim = q_ref.shape[1:]
-    slots = k_ref.shape[2]
+    block = s_ref.shape[2]
     fresh_count = kn_ref.shape[2]
     scale = 1.0 / head_dim**0.5
     length = len_ref[pl.program_id(0)]
-    live = lax.broadcasted_iota(jnp.int32, (per_group, slots), 1) < length
+    blocks = (length + block - 1) // block
     for g in range(groups):
         q = q_ref[0, g]
-        cached = lax.dot_general(
-            q, k_ref[0, g], (((1,), (1,)), ((), ())), preferred_element_type=jnp.float32
-        ) * scale
-        cached = jnp.where(live, cached, -1e30)
+
+        def scores(b, top):
+            at = pl.multiple_of(b * block, block)
+            cached = lax.dot_general(
+                q,
+                k_ref[0, g, pl.ds(at, block), :],
+                (((1,), (1,)), ((), ())),
+                preferred_element_type=jnp.float32,
+            ) * scale
+            live = lax.broadcasted_iota(jnp.int32, (per_group, block), 1) + at < length
+            cached = jnp.where(live, cached, -1e30)
+            s_ref[b] = cached
+            return jnp.maximum(top, jnp.max(cached, axis=-1, keepdims=True))
+
+        top = lax.fori_loop(
+            0, blocks, scores, jnp.full((per_group, 1), -jnp.inf, jnp.float32)
+        )
         qf = q.astype(jnp.float32)
         kn = kn_ref[0, g].astype(jnp.float32)
         vn = vn_ref[0, g].astype(jnp.float32)
@@ -45,22 +58,38 @@
             jnp.sum(qf * kn[s : s + 1, :], axis=-1, keepdims=True) * scale
             for s in range(fresh_count)
         ]
-        top = jnp.max(cached, axis=-1, keepdims=True)
         for f in fresh:
             top = jnp.maximum(top, f)
-        e_cached = jnp.where(live, jnp.exp(cached - top), 0.0)
+
+        def exps(b, total):
+            at = b * block
+            live = lax.broadcasted_iota(jnp.int32, (per_group, block), 1) + at < length
+            e = jnp.where(live, jnp.exp(s_ref[b] - top), 0.0)
+            s_ref[b] = e
+            return total + jnp.sum(e, axis=-1, keepdims=True)
+
+        total = lax.fori_loop(0, blocks, exps, jnp.zeros((per_group, 1), jnp.float32))
         e_fresh = [jnp.exp(f - top) for f in fresh]
-        total = jnp.sum(e_cached, axis=-1, keepdims=True)
         for e in e_fresh:
             total = total + e
-        p_cached = (e_cached / total).astype(jnp.bfloat16)
-        out = jnp.dot(p_cached, v_ref[0, g], preferred_element_type=jnp.float32)
-        fresh_out = None
+
+        def weighted(b, acc):
+            at = pl.multiple_of(b * block, block)
+            p = (s_ref[b] / total).astype(jnp.bfloat16)
+            return acc + jnp.dot(
+                p, v_ref[0, g, pl.ds(at, block), :], preferred_element_type=jnp.float32
+            )
+
+        out = lax.fori_loop(
+            0, blocks, weighted, jnp.zeros((per_group, head_dim), jnp.float32)
+        )
         for s, e in enumerate(e_fresh):
             p = (e / total).astype(jnp.bfloat16).astype(jnp.float32)
-            term = p * vn[s : s + 1, :]
-            fresh_out = term if fresh_out is None else fresh_out + term
-        o_ref[0, g] = (out + fresh_out).astype(o_ref.dtype)
+            out = out + p * vn[s : s + 1, :]
+        o_ref[0, g] = out.astype(o_ref.dtype)
+
+
+SLOT_BLOCK = 256
 
 
 def attention(query, key_cache, value_cache, keys_now, vals_now, lengths):
@@ -82,6 +111,9 @@
                 pl.BlockSpec((1, groups, fresh_count, head_dim), row_map),
             ],
             out_specs=pl.BlockSpec((1, groups, per_group, head_dim), row_map),
+            scratch_shapes=[
+                pltpu.VMEM((slots // SLOT_BLOCK, per_group, SLOT_BLOCK), jnp.float32)
+            ],
         ),
     )(lengths, query, key_cache, value_cache, keys_now, vals_now)
 

time: 546 us -> 653 us (1.20)
  Pallas kernels: 73.5 us -> 168 us
  waiting for transfers between devices: 369 us -> 384 us
    pallas_call x2, Pallas kernels: 73.5 us -> 168 us  [attention(): pl.pallas_call(attention_kernel, out_shape=jax.ShapeDtypeStruct(query.sha...]
    all_gather x2, waiting for transfers between devices: 98.3 us -> 113 us  [attend_step(): lax.all_gather(attended, 'wide', axis=0, tiled=True)]
where the time goes in v7:
time: 653 us
  waiting for transfers between devices  384 us (59%)
  Pallas kernels  168 us (26%)
  matrix products  47 us (7%)
  local copies, waits for them, and re-layouts  27.2 us (4%)
  between operations  13.7 us (2%)
  other arithmetic  12.7 us (2%)
    reduce_scatter x2, waiting for transfers between devices, attend_step(): lax.psum_scatter(jnp.concatenate((part_q, part_kv), axis=1), 'wide', scat...  190 us
    pallas_call x2, Pallas kernels, attention(): pl.pallas_call(attention_kernel, out_shape=jax.ShapeDtypeStruct(query.sha...  168 us
    all_gather x2, waiting for transfers between devices, attend_step(): lax.all_gather(attended, 'wide', axis=0, tiled=True)  113 us
    reduce_scatter x2, waiting for transfers between devices, on_device(): lax.psum_scatter(partial_value, 'narrow', scatter_dimension=0, tiled=True)  60.1 us
    unnamed x24, local copies, waits for them, and re-layouts  24.5 us
    dot_general x2, matrix products, attend_step(): jnp.dot(lax.all_gather(attended, 'wide', axis=0, tiled=True), w_out, pref...  24.4 us
    dot_general x2, matrix products, attend_step(): part_q = jnp.dot(every, w_q2, preferred_element_type=jnp.float32)  21.1 us
    all_gather x2, waiting for transfers between devices, on_device(): lax.all_gather(result, 'narrow', axis=0, tiled=True)  19.7 us
  transfers between devices with their start and end apart: 8, of which 8 were waited for; matrix products, arithmetic and copies ran while one was open for 3% of the time, Pallas kernels for 0%

profile of v7, /device:TPU:0, one launch (start us, length us, event | category | flops | bytes accessed | tf_op | source)
XLA Modules:
  0.0 652.6 jit_solution(13141357362313789413)
XLA Ops:
  6.5 0.7 all-gather.5.cloned.1.call-update
  7.3 17.5 %copy.53 = bf16[256,8,2,2048]{3,1,2,0:T(8,128)(2,1)} copy(bf16[256,8,2,2048]{3,2,1,0:T(2,128)(2,1)} %bitcast.52) | data formatting | bytes 33554432
  24.8 0.5 copy.54
  25.3 3.0 all-gather.5.cloned.1.call-done
  28.4 10.5 %fusion.8 = f32[256,4096]{1,0:T(8,128)S(1)} fusion(bf16[256,2048]{1,0:T(8,128)(2,1)} %all-gather.5.cloned.1.call-done, bf16[2048,4096]{1,0:T(8,128)(2,1)} %bitcast.53), kind=kOutput, calls=%fused_computation.37 | convolution fusion | flops 4294967296 | bytes 22020096 | tf_op jit(solution)/shard_map/dot_general | solution.py:128
  38.9 0.7 fusion.9
  39.7 2.6 pad_maximum_fusion
  42.2 0.0 all-gather.7.cloned.1.call-start
  42.3 0.6 copy-done.4
  42.9 0.2 multiply_cosine_fusion
  43.1 94.8 %reduce-scatter.5.cloned.1.call-done = f32[32,4608]{1,0:T(8,128)} async-done(((f32[256,4608]{1,0:T(8,128)}), f32[32,4608]{1,0:T(8,128)}) %reduce-scatter.5.cloned.1.call-update) | async-done | bytes 589840 | tf_op jit(solution)/shard_map/reduce_scatter | solution.py:130
  137.8 0.8 slice.67
  138.7 0.1 fusion.7
  138.9 1.1 slice_bitcast_fusion.1
  140.0 0.1 copy.55
  140.1 0.2 subtract_convert_fusion.1
  140.4 0.6 copy.37.vn_ref
  141.0 0.7 pad_maximum_fusion.4.kn_ref
  141.7 0.8 pad_maximum_fusion.2.q_ref
  142.6 83.8 %shard_map.73 = bf16[32,2,16,128]{3,2,1,0:T(8,128)(2,1)} custom-call(s32[32]{0:T(128)} %len_ref.3, bf16[32,2,16,128]{3,2,1,0:T(8,128)(2,1)} %pad_maximum_fusion.2.q_ref, bf16[32,2,1024,128]{3,2,1,0:T(8,128)(2,1)} %k_ref.3, bf16[32,2,1024,128]{3,2,1,0:T(8,128)(2,1)} %v_ref.3, bf16[32,2,1,128]{3,2,1,0:T(2,128)(2,1)} %pad_maximum_fusion.4.kn_ref, ...), custom_call_target="tpu_custom_call" | custom-call | tf_op jit(solution)/shard_map/pallas_call | solution.py:100
  226.4 1.8 copy.92
  228.2 0.0 reduce-scatter.7.cloned.1.call-start
  228.3 56.4 %all-gather.7.cloned.1.call-done = bf16[256,4096]{1,0:T(8,128)(2,1)} async-done(((bf16[32,4096]{1,0:T(8,128)(2,1)}), bf16[256,4096]{1,0:T(8,128)(2,1)}) %all-gather.7.cloned.1.call-update) | async-done | bytes 2097168 | tf_op jit(solution)/shard_map/all_gather | solution.py:146
  284.7 12.2 %fusion.10 = f32[256,2048]{1,0:T(8,128)} fusion(bf16[256,4096]{1,0:T(8,128)(2,1)} %all-gather.7.cloned.1.call-done, bf16[4096,2048]{1,0:T(8,128)(2,1)} %param.10), kind=kOutput, calls=%fused_computation.39 | convolution fusion | flops 4294967296 | bytes 20971520 | tf_op jit(solution)/shard_map/dot_general | solution.py:145
  297.0 0.0 all-gather.9.cloned.1.call-start
  297.0 30.0 %reduce-scatter.7.cloned.1.call-done = f32[64,2048]{1,0:T(8,128)} async-done(((f32[256,2048]{1,0:T(8,128)}), f32[64,2048]{1,0:T(8,128)}) %reduce-scatter.7.cloned.1.call-update) | async-done | bytes 524304 | tf_op jit(solution)/shard_map/reduce_scatter | solution.py:171
  327.1 1.8 add_convert_fusion.2
  328.9 0.2 reduce-scatter.9.cloned.1.call-start
  329.1 16.6 %all-gather.9.cloned.1.call-done = bf16[256,2048]{1,0:T(8,128)(2,1)} async-done(((bf16[64,2048]{1,0:T(8,128)(2,1)}), bf16[256,2048]{1,0:T(8,128)(2,1)}) %all-gather.9.cloned.1.call-update) | async-done | bytes 1048592 | tf_op jit(solution)/shard_map/all_gather | solution.py:160
  345.7 10.5 %fusion.11 = f32[256,4096]{1,0:T(8,128)S(1)} fusion(bf16[256,2048]{1,0:T(8,128)(2,1)} %all-gather.9.cloned.1.call-done, bf16[2048,4096]{1,0:T(8,128)(2,1)} %bitcast.54), kind=kOutput, calls=%fused_computation.40 | convolution fusion | flops 4294967296 | bytes 22020096 | tf_op jit(solution)/shard_map/dot_general | solution.py:128
  356.3 0.7 fusion.12
  357.0 2.6 pad_maximum_fusion.1
  359.6 0.0 all-gather.11.cloned.1.call-start
  359.6 95.4 %reduce-scatter.9.cloned.1.call-done = f32[32,4608]{1,0:T(8,128)} async-done(((f32[256,4608]{1,0:T(8,128)}), f32[32,4608]{1,0:T(8,128)}) %reduce-scatter.9.cloned.1.call-update) | async-done | bytes 589840 | tf_op jit(solution)/shard_map/reduce_scatter | solution.py:130
  455.0 0.8 slice.74
  455.9 0.1 fusion.6
  456.2 1.1 slice_bitcast_fusion
  457.3 0.1 copy.57
  457.4 0.2 subtract_convert_fusion
  457.6 0.9 pad_maximum_fusion.3.q_ref
  458.5 0.9 maximum_maximum_fusion
  459.4 84.1 %shard_map.74 = bf16[32,2,16,128]{3,2,1,0:T(8,128)(2,1)} custom-call(s32[32]{0:T(128)} %len_ref.3, bf16[32,2,16,128]{3,2,1,0:T(8,128)(2,1)} %pad_maximum_fusion.3.q_ref, bf16[32,2,1024,128]{3,2,1,0:T(8,128)(2,1)} %k_ref.3, bf16[32,2,1024,128]{3,2,1,0:T(8,128)(2,1)} %v_ref.3, bf16[32,2,2,128]{3,2,1,0:T(2,128)(2,1)} %get-tuple-element.25.kn_ref, ...), custom_call_target="tpu_custom_call" | custom-call | tf_op jit(solution)/shard_map/pallas_call | solution.py:100
  543.4 1.8 copy.91
  545.2 0.0 reduce-scatter.11.cloned.1.call-start
  545.3 56.4 %all-gather.11.cloned.1.call-done = bf16[256,4096]{1,0:T(8,128)(2,1)} async-done(((bf16[32,4096]{1,0:T(8,128)(2,1)}), bf16[256,4096]{1,0:T(8,128)(2,1)}) %all-gather.11.cloned.1.call-update) | async-done | bytes 2097168 | tf_op jit(solution)/shard_map/all_gather | solution.py:146
  601.7 12.2 %fusion.13 = f32[256,2048]{1,0:T(8,128)} fusion(bf16[256,4096]{1,0:T(8,128)(2,1)} %all-gather.11.cloned.1.call-done, bf16[4096,2048]{1,0:T(8,128)(2,1)} %param.10), kind=kOutput, calls=%fused_computation.42 | convolution fusion | flops 4294967296 | bytes 20971520 | tf_op jit(solution)/shard_map/dot_general | solution.py:145
  613.9 30.1 %reduce-scatter.11.cloned.1.call-done = f32[64,2048]{1,0:T(8,128)} async-done(((f32[256,2048]{1,0:T(8,128)}), f32[64,2048]{1,0:T(8,128)}) %reduce-scatter.11.cloned.1.call-update) | async-done | bytes 524304 | tf_op jit(solution)/shard_map/reduce_scatter | solution.py:171
  644.0 1.8 add_convert_fusion
  (37 shorter events, 0.5 us)
Async XLA Ops:
  6.5 21.8 %all-gather.5.cloned.1.call-start = ((), (), s32[]{:S(2)}) async-start(), calls=%async_computation.4 | async-start | bytes 1310720 | tf_op jit(solution)/shard_map/all_gather | solution.py:160
  7.3 130.6 %reduce-scatter.5.cloned.1.call-start = ((), (), s32[]{:S(2)}) async-start(), calls=%async_computation.5 | async-start | bytes 5308416 | tf_op jit(solution)/shard_map/reduce_scatter | solution.py:130
  7.3 17.5 %copy-start.1 = (bf16[2048,2,256]{2,1,0:T(2,128)(2,1)S(1)}, bf16[2048,2,256]{2,1,0:T(2,128)(2,1)}, u32[]{:S(2)}) copy-start(bf16[2048,2,256]{2,1,0:T(2,128)(2,1)} %param.9) | copy-start | bytes 6291460
  28.4 10.5 %copy-start.5 = (bf16[256,2048]{1,0:T(8,128)(2,1)S(1)}, bf16[256,2048]{1,0:T(8,128)(2,1)}, u32[]{:S(2)}) copy-start(bf16[256,2048]{1,0:T(8,128)(2,1)} %all-gather.5.cloned.1.call-done) | copy-start | bytes 3145732
  42.2 0.7 copy-start.4
  42.2 242.5 %all-gather.7.cloned.1.call-start = ((), (), s32[]{:S(2)}) async-start(), calls=%async_computation.6 | async-start | bytes 2359296 | tf_op jit(solution)/shard_map/all_gather | solution.py:146
  228.2 98.8 %copy-start.2 = (bf16[64,2048]{1,0:T(8,128)(2,1)S(1)}, bf16[64,2048]{1,0:T(8,128)(2,1)}, u32[]{:S(2)}) copy-start(bf16[64,2048]{1,0:T(8,128)(2,1)} %param.7) | copy-start | bytes 786436
  228.2 98.8 %reduce-scatter.7.cloned.1.call-start = ((), (), s32[]{:S(2)}) async-start(), calls=%async_computation.7 | async-start | bytes 2621440 | tf_op jit(solution)/shard_map/reduce_scatter | solution.py:171
  297.0 48.8 %all-gather.9.cloned.1.call-start = ((), (), s32[]{:S(2)}) async-start(), calls=%async_computation.8 | async-start | bytes 1310720 | tf_op jit(solution)/shard_map/all_gather | solution.py:160
  328.9 126.2 %reduce-scatter.9.cloned.1.call-start = ((), (), s32[]{:S(2)}) async-start(), calls=%async_computation.9 | async-start | bytes 5308416 | tf_op jit(solution)/shard_map/reduce_scatter | solution.py:130
  345.7 10.5 %copy-start.6 = (bf16[256,2048]{1,0:T(8,128)(2,1)S(1)}, bf16[256,2048]{1,0:T(8,128)(2,1)}, u32[]{:S(2)}) copy-start(bf16[256,2048]{1,0:T(8,128)(2,1)} %all-gather.9.cloned.1.call-done) | copy-start | bytes 3145732
  359.6 98.9 %copy-start.3 = (bf16[32,2,1,128]{3,2,1,0:T(2,128)(2,1)S(1)}, bf16[32,2,1,128]{3,2,1,0:T(2,128)(2,1)}, u32[]{:S(2)}) copy-start(bf16[32,2,1,128]{3,2,1,0:T(2,128)(2,1)} %copy.37.vn_ref) | copy-start | bytes 49156
  359.6 242.1 %all-gather.11.cloned.1.call-start = ((), (), s32[]{:S(2)}) async-start(), calls=%async_computation.10 | async-start | bytes 2359296 | tf_op jit(solution)/shard_map/all_gather | solution.py:146
  545.2 98.8 %copy-start = (bf16[64,2048]{1,0:T(8,128)(2,1)S(1)}, bf16[64,2048]{1,0:T(8,128)(2,1)}, u32[]{:S(2)}) copy-start(bf16[64,2048]{1,0:T(8,128)(2,1)} %add_convert_fusion.2) | copy-start | bytes 786436
  545.2 98.8 %reduce-scatter.11.cloned.1.call-start = ((), (), s32[]{:S(2)}) async-start(), calls=%async_computation.11 | async-start | bytes 2621440 | tf_op jit(solution)/shard_map/reduce_scatter | solution.py:171
Sparse Core Ops, SparseCore 0:
  8.9 19.4 all-gather.4
  42.4 95.4 reduce-scatter.4
  228.3 56.3 all-gather.6
  297.1 29.9 reduce-scatter.6
  329.0 16.6 all-gather.8
  359.7 95.2 reduce-scatter.8
  545.3 56.3 all-gather.10
  614.0 29.9 reduce-scatter.10

commit v8 on v1

--- a/solution.py
+++ b/solution.py
@@ -45,28 +45,40 @@
     keys_now = jnp.stack(new_keys, axis=2)
     vals_now = jnp.stack(new_vals, axis=2)
     scale = 1.0 / head_dim**0.5
-    live = (jnp.arange(slots, dtype=jnp.int32)[None, :] < lengths[:, None])[:, None, None, :]
-    cached = (
-        jnp.einsum("rgjd,rgcd->rgjc", query, key_cache, preferred_element_type=jnp.float32) * scale
-    )
-    cached = jnp.where(live, cached, -1e30)
-    fresh = (
-        jnp.einsum("rgjd,rgsd->rgjs", query, keys_now, preferred_element_type=jnp.float32) * scale
-    )
-    top = jnp.maximum(jnp.max(cached, axis=-1), jnp.max(fresh, axis=-1))
-    e_cached = jnp.where(live, jnp.exp(cached - top[..., None]), 0.0)
-    e_fresh = jnp.exp(fresh - top[..., None])
-    total = jnp.sum(e_cached, axis=-1) + jnp.sum(e_fresh, axis=-1)
-    p_cached = (e_cached / total[..., None]).astype(jnp.bfloat16)
-    p_fresh = (e_fresh / total[..., None]).astype(jnp.bfloat16)
-    out = jnp.einsum("rgjc,rgcd->rgjd", p_cached, value_cache, preferred_element_type=jnp.float32)
-    out = out + jnp.einsum("rgjs,rgsd->rgjd", p_fresh, vals_now, preferred_element_type=jnp.float32)
-    attended = out.astype(jnp.bfloat16).reshape(local_rows, groups * per_group * head_dim)
-    return jnp.dot(
-        lax.all_gather(attended, "wide", axis=0, tiled=True),
-        w_out,
-        preferred_element_type=jnp.float32,
-    )
+    live = (jnp.arange(slots, dtype=jnp.int32)[None, :] < lengths[:, None])[:, None, :]
+    width = per_group * head_dim
+    total_update = None
+    for g in range(groups):
+        q = query[:, g]
+        cached = (
+            jnp.einsum("rjd,rcd->rjc", q, key_cache[:, g], preferred_element_type=jnp.float32)
+            * scale
+        )
+        cached = jnp.where(live, cached, -1e30)
+        fresh = (
+            jnp.einsum("rjd,rsd->rjs", q, keys_now[:, g], preferred_element_type=jnp.float32)
+            * scale
+        )
+        top = jnp.maximum(jnp.max(cached, axis=-1), jnp.max(fresh, axis=-1))
+        e_cached = jnp.where(live, jnp.exp(cached - top[..., None]), 0.0)
+        e_fresh = jnp.exp(fresh - top[..., None])
+        total = jnp.sum(e_cached, axis=-1) + jnp.sum(e_fresh, axis=-1)
+        p_cached = (e_cached / total[..., None]).astype(jnp.bfloat16)
+        p_fresh = (e_fresh / total[..., None]).astype(jnp.bfloat16)
+        out = jnp.einsum(
+            "rjc,rcd->rjd", p_cached, value_cache[:, g], preferred_element_type=jnp.float32
+        )
+        out = out + jnp.einsum(
+            "rjs,rsd->rjd", p_fresh, vals_now[:, g], preferred_element_type=jnp.float32
+        )
+        attended = out.astype(jnp.bfloat16).reshape(local_rows, width)
+        update = jnp.dot(
+            lax.all_gather(attended, "wide", axis=0, tiled=True),
+            w_out[g * width : (g + 1) * width],
+            preferred_element_type=jnp.float32,
+        )
+        total_update = update if total_update is None else total_update + update
+    return total_update
 
 
 def on_device(hidden_in, w_query, w_keyval, w_out, key_cache, value_cache, lengths):

time: 513 us -> 552 us (1.076)
  waiting for transfers between devices: 369 us -> 408 us
  other arithmetic: 17.5 us -> 11.3 us
    all_gather x2 -> x4, waiting for transfers between devices: 98.1 us -> 137 us  [attend_step(): lax.all_gather(attended, 'wide', axis=0, tiled=True)]
    reduce_sum x3 -> x4, other arithmetic: 7.85 us -> 1.55 us  [attend_step(): total = jnp.sum(e_cached, axis=-1) + jnp.sum(e_fresh, axis=-1)]
    dot_general x9 -> x18, matrix products: 64.9 us -> 69 us  [the longest x4 28.8 us: attend_step(): jnp.dot(lax.all_gather(attended, 'wide', axis=0, tiled=True), w_out[g * w...]
    unnamed x25 -> x34, local copies, waits for them, and re-layouts: 22.6 us -> 23.7 us
  transfers between devices with their start and end apart: 8 -> 10, of which waited for: 8 -> 10; matrix products, arithmetic and copies ran while one was open for 4% -> 8% of each run, Pallas kernels for 0% -> 0%
where the time goes in v8:
time: 552 us; the launch traced here: 551 us
  waiting for transfers between devices  408 us (74%)
  matrix products  91.4 us (17%)
  local copies, waits for them, and re-layouts  25.5 us (5%)
  between operations  14 us (3%)
  other arithmetic  11.3 us (2%)
    reduce_scatter x2, waiting for transfers between devices, attend_step(): lax.psum_scatter(jnp.concatenate((part_q, part_kv), axis=1), 'wide', scat...  190 us
    all_gather x4, waiting for transfers between devices, attend_step(): lax.all_gather(attended, 'wide', axis=0, tiled=True)  137 us
    reduce_scatter x2, waiting for transfers between devices, on_device(): lax.psum_scatter(partial_value, 'narrow', scatter_dimension=0, tiled=True)  60.6 us
    dot_general x4, matrix products, attend_step(): jnp.dot(lax.all_gather(attended, 'wide', axis=0, tiled=True), w_out[g * w...  28.8 us
    unnamed x34, local copies, waits for them, and re-layouts  23.7 us
    dot_general x4, matrix products, attend_step(): jnp.einsum('rjd,rcd->rjc', q, key_cache[:, g], preferred_element_type=jnp...  22.9 us
    dot_general x2, matrix products, attend_step(): part_q = jnp.dot(every, w_q2, preferred_element_type=jnp.float32)  20.9 us
    all_gather x2, waiting for transfers between devices, on_device(): lax.all_gather(result, 'narrow', axis=0, tiled=True)  19.9 us
  transfers between devices with their start and end apart: 10, of which 10 were waited for; matrix products, arithmetic and copies ran while one was open for 8% of the time, Pallas kernels for 0%

profile of v8, /device:TPU:0, one launch (start us, length us, event | category | flops | bytes accessed | tf_op | source)
XLA Modules:
  0.0 551.1 jit_solution(122990783040698619)
XLA Ops:
  6.5 0.7 all-gather.7.cloned.1.call-update
  7.3 17.5 %copy.82 = bf16[256,8,2,2048]{3,1,2,0:T(8,128)(2,1)} copy(bf16[256,8,2,2048]{3,2,1,0:T(2,128)(2,1)} %bitcast.160) | data formatting | bytes 33554432
  24.8 0.5 copy.83
  25.3 3.1 all-gather.7.cloned.1.call-done
  28.4 10.5 %fusion.148 = f32[256,4096]{1,0:T(8,128)S(1)} fusion(bf16[256,2048]{1,0:T(8,128)(2,1)} %all-gather.7.cloned.1.call-done, bf16[2048,4096]{1,0:T(8,128)(2,1)} %bitcast.161), kind=kOutput, calls=%fused_computation.198 | convolution fusion | flops 4294967296 | bytes 22020096 | tf_op jit(solution)/shard_map/dot_general | solution.py:33
  38.9 0.7 fusion.149
  39.6 2.5 pad_maximum_fusion
  42.2 0.6 copy-done.4
  43.1 94.6 %reduce-scatter.5.cloned.1.call-done = f32[32,4608]{1,0:T(8,128)} async-done(((f32[256,4608]{1,0:T(8,128)}), f32[32,4608]{1,0:T(8,128)}) %reduce-scatter.5.cloned.1.call-update) | async-done | bytes 589840 | tf_op jit(solution)/shard_map/reduce_scatter | solution.py:35
  137.7 0.8 slice.147
  138.8 1.1 slice_bitcast_fusion.1
  140.5 0.2 fusion.108
  141.0 6.2 %fusion.38 = (f32[32,16]{1,0:T(8,128)S(1)}, f32[32,16,1024]{2,1,0:T(8,128)S(1)}) fusion(pred[32,1024]{1,0:T(8,128)(4,1)S(1)} %iota_compare_fusion, bf16[32,2,1024,128]{3,2,1,0:T(8,128)(2,1)} %param.11, bf16[32,2,16,64]{3,2,0,1:T(8,128)(2,1)S(1)} %get-tuple-element.11, bf16[32,2,16,64]{3,2,0,1:T(8,128)(2,1)S(1)} %get-tuple-element.12), kind=kOutput, calls=%fused_computation.48 | convolution fusion | flops 136052224 | bytes 10782720 | tf_op jit(solution)/shard_map/rjd,rcd->rjc/dot_general | solution.py:54
  147.2 5.9 %fusion.42 = (f32[32,16]{1,0:T(8,128)S(1)}, f32[32,16]{1,0:T(8,128)S(1)}, f32[32,16,1024]{2,1,0:T(8,128)S(1)}) fusion(f32[32,16,1024]{2,1,0:T(8,128)S(1)} %get-tuple-element.40, f32[32,16]{1,0:T(8,128)S(1)} %multiply_maximum_fusion.1, pred[32,1024]{1,0:T(8,128)(4,1)S(1)} %iota_compare_fusion, bf16[32,16,128]{2,1,0:T(8,128)(2,1)S(1)} %fusion.89, ...), kind=kOutput, calls=%fused_computation.52 | convolution fusion | flops 138411008 | bytes 12752896 | tf_op jit(solution)/shard_map/rjd,rcd->rjc/dot_general | solution.py:54
  153.1 0.7 fusion.43
  153.9 1.7 fusion.54
  155.6 0.7 copy.134
  156.4 5.6 %fusion.57 = bf16[32,16,128]{2,1,0:T(8,128)(2,1)S(1)} fusion(bf16[32,2,1024,128]{3,2,1,0:T(8,128)(2,1)} %param.12, f32[32,16,1024]{2,1,0:T(8,128)} %copy-done.2, f32[32,16]{1,0:T(8,128)S(1)} %get-tuple-element.26, f32[32,16]{1,0:T(8,128)S(1)} %multiply_maximum_fusion.1, pred[32,1024]{1,0:T(8,128)(4,1)S(1)} %iota_compare_fusion, ...), kind=kOutput, calls=%fused_computation.63 | convolution fusion | flops 137560064 | bytes 10672128 | tf_op jit(solution)/shard_map/rjc,rcd->rjd/dot_general | solution.py:68
  162.0 0.7 copy.135
  162.9 33.5 %all-gather.11.cloned.1.call-done = bf16[256,2048]{1,0:T(8,128)(2,1)} async-done(((bf16[32,2048]{1,0:T(8,128)(2,1)}), bf16[256,2048]{1,0:T(8,128)(2,1)}) %all-gather.11.cloned.1.call-update) | async-done | bytes 1048592 | tf_op jit(solution)/shard_map/all_gather | solution.py:76
  196.4 7.4 %fusion.18 = f32[256,2048]{1,0:T(8,128)} fusion(bf16[256,2048]{1,0:T(8,128)(2,1)} %all-gather.11.cloned.1.call-done, bf16[4096,2048]{1,0:T(8,128)(2,1)} %param.10), kind=kOutput, calls=%fused_computation.18 | convolution fusion | flops 2147483648 | bytes 11534336 | tf_op jit(solution)/shard_map/dot_general | solution.py:75
  203.8 33.5 %all-gather.9.cloned.1.call-done = bf16[256,2048]{1,0:T(8,128)(2,1)} async-done(((bf16[32,2048]{1,0:T(8,128)(2,1)}), bf16[256,2048]{1,0:T(8,128)(2,1)}) %all-gather.9.cloned.1.call-update) | async-done | bytes 1048592 | tf_op jit(solution)/shard_map/all_gather | solution.py:76
  237.3 8.0 %fusion.32 = f32[256,2048]{1,0:T(8,128)} fusion(f32[256,2048]{1,0:T(8,128)} %fusion.18, bf16[256,2048]{1,0:T(8,128)(2,1)} %all-gather.9.cloned.1.call-done, bf16[4096,2048]{1,0:T(8,128)(2,1)} %param.10), kind=kOutput, calls=%fused_computation.34 | convolution fusion | flops 2148007936 | bytes 13631488 | tf_op jit(solution)/shard_map/dot_general | solution.py:75
  245.4 30.3 %reduce-scatter.7.cloned.1.call-done = f32[64,2048]{1,0:T(8,128)} async-done(((f32[256,2048]{1,0:T(8,128)}), f32[64,2048]{1,0:T(8,128)}) %reduce-scatter.7.cloned.1.call-update) | async-done | bytes 524304 | tf_op jit(solution)/shard_map/reduce_scatter | solution.py:103
  275.7 1.8 add_convert_fusion.2
  277.5 16.8 %all-gather.13.cloned.1.call-done = bf16[256,2048]{1,0:T(8,128)(2,1)} async-done(((bf16[64,2048]{1,0:T(8,128)(2,1)}), bf16[256,2048]{1,0:T(8,128)(2,1)}) %all-gather.13.cloned.1.call-update) | async-done | bytes 1048592 | tf_op jit(solution)/shard_map/all_gather | solution.py:92
  294.4 10.5 %fusion.150 = f32[256,4096]{1,0:T(8,128)S(1)} fusion(bf16[256,2048]{1,0:T(8,128)(2,1)} %all-gather.13.cloned.1.call-done, bf16[2048,4096]{1,0:T(8,128)(2,1)} %bitcast.162), kind=kOutput, calls=%fused_computation.200 | convolution fusion | flops 4294967296 | bytes 22020096 | tf_op jit(solution)/shard_map/dot_general | solution.py:33
  304.8 0.7 fusion.151
  305.6 2.5 pad_maximum_fusion.1
  308.2 95.3 %reduce-scatter.9.cloned.1.call-done = f32[32,4608]{1,0:T(8,128)} async-done(((f32[256,4608]{1,0:T(8,128)}), f32[32,4608]{1,0:T(8,128)}) %reduce-scatter.9.cloned.1.call-update) | async-done | bytes 589840 | tf_op jit(solution)/shard_map/reduce_scatter | solution.py:35
  403.6 1.1 slice_bitcast_fusion
  405.1 5.8 %fusion.40 = (f32[32,16]{1,0:T(8,128)S(1)}, f32[32,16,1024]{2,1,0:T(8,128)S(1)}) fusion(pred[32,1024]{1,0:T(8,128)(4,1)S(1)} %iota_compare_fusion, bf16[32,2,1024,128]{3,2,1,0:T(8,128)(2,1)} %param.11, bf16[32,2,16,64]{3,2,0,1:T(8,128)(2,1)S(1)} %get-tuple-element.9, bf16[32,2,16,64]{3,2,0,1:T(8,128)(2,1)S(1)} %get-tuple-element.10), kind=kOutput, calls=%fused_computation.50 | convolution fusion | flops 136052224 | bytes 10782720 | tf_op jit(solution)/shard_map/rjd,rcd->rjc/dot_general | solution.py:54
  411.6 0.3 fusion.146
  412.1 5.1 fusion.44
  417.3 0.7 fusion.45
  418.0 4.3 fusion
  422.3 0.2 fusion.53
  422.6 0.7 copy.132
  423.3 0.3 all-gather.15.cloned.1.call-start
  423.6 4.3 fusion.8
  428.0 0.2 fusion.52
  428.2 0.7 copy.133
  429.0 34.5 %all-gather.17.cloned.1.call-done = bf16[256,2048]{1,0:T(8,128)(2,1)} async-done(((bf16[32,2048]{1,0:T(8,128)(2,1)}), bf16[256,2048]{1,0:T(8,128)(2,1)}) %all-gather.17.cloned.1.call-update) | async-done | bytes 1048592 | tf_op jit(solution)/shard_map/all_gather | solution.py:76
  463.4 6.0 %fusion.16 = f32[256,2048]{1,0:T(8,128)S(1)} fusion(bf16[256,2048]{1,0:T(8,128)(2,1)} %all-gather.17.cloned.1.call-done, bf16[4096,2048]{1,0:T(8,128)(2,1)} %param.10), kind=kOutput, calls=%fused_computation.16 | convolution fusion | flops 2147483648 | bytes 11534336 | tf_op jit(solution)/shard_map/dot_general | solution.py:75
  469.5 35.2 %all-gather.15.cloned.1.call-done = bf16[256,2048]{1,0:T(8,128)(2,1)} async-done(((bf16[32,2048]{1,0:T(8,128)(2,1)}), bf16[256,2048]{1,0:T(8,128)(2,1)}) %all-gather.15.cloned.1.call-update) | async-done | bytes 1048592 | tf_op jit(solution)/shard_map/all_gather | solution.py:76
  504.7 7.4 %fusion.35 = f32[256,2048]{1,0:T(8,128)} fusion(f32[256,2048]{1,0:T(8,128)S(1)} %fusion.16, bf16[256,2048]{1,0:T(8,128)(2,1)} %all-gather.15.cloned.1.call-done, bf16[4096,2048]{1,0:T(8,128)(2,1)} %param.10), kind=kOutput, calls=%fused_computation.35 | convolution fusion | flops 2148007936 | bytes 13631488 | tf_op jit(solution)/shard_map/dot_general | solution.py:75
  512.1 30.3 %reduce-scatter.11.cloned.1.call-done = f32[64,2048]{1,0:T(8,128)} async-done(((f32[256,2048]{1,0:T(8,128)}), f32[64,2048]{1,0:T(8,128)}) %reduce-scatter.11.cloned.1.call-update) | async-done | bytes 524304 | tf_op jit(solution)/shard_map/reduce_scatter | solution.py:103
  542.5 1.8 add_convert_fusion
  (83 shorter events, 3.5 us)
Async XLA Ops:
  6.5 21.8 %all-gather.7.cloned.1.call-start = ((), (), s32[]{:S(2)}) async-start(), calls=%async_computation.4 | async-start | bytes 1310720 | tf_op jit(solution)/shard_map/all_gather | solution.py:92
  7.3 130.4 %reduce-scatter.5.cloned.1.call-start = ((), (), s32[]{:S(2)}) async-start(), calls=%async_computation.5 | async-start | bytes 5308416 | tf_op jit(solution)/shard_map/reduce_scatter | solution.py:35
  7.3 17.5 %copy-start.1 = (bf16[2048,2,256]{2,1,0:T(2,128)(2,1)S(1)}, bf16[2048,2,256]{2,1,0:T(2,128)(2,1)}, u32[]{:S(2)}) copy-start(bf16[2048,2,256]{2,1,0:T(2,128)(2,1)} %param.9) | copy-start | bytes 6291460
  28.4 10.5 %copy-start.5 = (bf16[256,2048]{1,0:T(8,128)(2,1)S(1)}, bf16[256,2048]{1,0:T(8,128)(2,1)}, u32[]{:S(2)}) copy-start(bf16[256,2048]{1,0:T(8,128)(2,1)} %all-gather.7.cloned.1.call-done) | copy-start | bytes 3145732
  42.1 0.7 copy-start.4
  42.1 154.3 %all-gather.11.cloned.1.call-start = ((), (), s32[]{:S(2)}) async-start(), calls=%async_computation.7 | async-start | bytes 1179648 | tf_op jit(solution)/shard_map/all_gather | solution.py:76
  140.2 13.7 %slice-start.1 = ((s8[16777216]{0:T(1024)(128)(4,1)}), s8[4194304]{0:T(1024)(128)(4,1)S(1)}, s32[]{:S(2)}) async-start(s8[16777216]{0:T(1024)(128)(4,1)} %bitcast.183), calls=%async_computation.15 | async-start | bytes 8388608
  141.0 12.9 %slice-start.2 = ((s8[16777216]{0:T(1024)(128)(4,1)}), s8[4194304]{0:T(1024)(128)(4,1)S(1)}, s32[]{:S(2)}) async-start(s8[16777216]{0:T(1024)(128)(4,1)} %bitcast.183), calls=%async_computation.16 | async-start | bytes 8388608
  147.2 5.9 %copy-start.2 = (f32[32,16,1024]{2,1,0:T(8,128)}, f32[32,16,1024]{2,1,0:T(8,128)S(1)}, u32[]{:S(2)}) copy-start(f32[32,16,1024]{2,1,0:T(8,128)S(1)} %get-tuple-element.40) | copy-start | bytes 6291460
  147.2 6.7 %slice-start.3 = ((s8[16777216]{0:T(1024)(128)(4,1)}), s8[4194304]{0:T(1024)(128)(4,1)S(1)}, s32[]{:S(2)}) async-start(s8[16777216]{0:T(1024)(128)(4,1)} %bitcast.183), calls=%async_computation.17 | async-start | bytes 8388608
  147.2 6.7 %slice-start.4 = ((s8[16777216]{0:T(1024)(128)(4,1)}), s8[4194304]{0:T(1024)(128)(4,1)S(1)}, s32[]{:S(2)}) async-start(s8[16777216]{0:T(1024)(128)(4,1)} %bitcast.183), calls=%async_computation.18 | async-start | bytes 8388608
  156.3 81.0 %all-gather.9.cloned.1.call-start = ((), (), s32[]{:S(2)}) async-start(), calls=%async_computation.6 | async-start | bytes 1179648 | tf_op jit(solution)/shard_map/all_gather | solution.py:76
  162.7 113.0 %reduce-scatter.7.cloned.1.call-start = ((), (), s32[]{:S(2)}) async-start(), calls=%async_computation.8 | async-start | bytes 2621440 | tf_op jit(solution)/shard_map/reduce_scatter | solution.py:103
  245.3 30.4 %copy-start.3 = (bf16[64,2048]{1,0:T(8,128)(2,1)S(1)}, bf16[64,2048]{1,0:T(8,128)(2,1)}, u32[]{:S(2)}) copy-start(bf16[64,2048]{1,0:T(8,128)(2,1)} %param.7) | copy-start | bytes 786436
  245.3 49.0 %all-gather.13.cloned.1.call-start = ((), (), s32[]{:S(2)}) async-start(), calls=%async_computation.9 | async-start | bytes 1310720 | tf_op jit(solution)/shard_map/all_gather | solution.py:92
  277.5 126.1 %reduce-scatter.9.cloned.1.call-start = ((), (), s32[]{:S(2)}) async-start(), calls=%async_computation.10 | async-start | bytes 5308416 | tf_op jit(solution)/shard_map/reduce_scatter | solution.py:35
  294.4 10.5 %copy-start.6 = (bf16[256,2048]{1,0:T(8,128)(2,1)S(1)}, bf16[256,2048]{1,0:T(8,128)(2,1)}, u32[]{:S(2)}) copy-start(bf16[256,2048]{1,0:T(8,128)(2,1)} %all-gather.13.cloned.1.call-done) | copy-start | bytes 3145732
  308.1 155.3 %all-gather.17.cloned.1.call-start = ((), (), s32[]{:S(2)}) async-start(), calls=%async_computation.12 | async-start | bytes 1179648 | tf_op jit(solution)/shard_map/all_gather | solution.py:76
  405.1 6.0 %slice-start = ((f32[32,4608]{1,0:T(8,128)}), f32[32,512]{1,0:T(8,128)S(1)}, s32[]{:S(2)}) async-start(f32[32,4608]{1,0:T(8,128)} %reduce-scatter.9.cloned.1.call-done), calls=%async_computation.14 | async-start | bytes 131072 | tf_op jit(solution)/shard_map/slice | solution.py:42
  423.3 81.4 %all-gather.15.cloned.1.call-start = ((), (), s32[]{:S(2)}) async-start(), calls=%async_computation.11 | async-start | bytes 1179648 | tf_op jit(solution)/shard_map/all_gather | solution.py:76
  428.9 113.6 %reduce-scatter.11.cloned.1.call-start = ((), (), s32[]{:S(2)}) async-start(), calls=%async_computation.13 | async-start | bytes 2621440 | tf_op jit(solution)/shard_map/reduce_scatter | solution.py:103
  512.1 30.4 %copy-start = (bf16[64,2048]{1,0:T(8,128)(2,1)S(1)}, bf16[64,2048]{1,0:T(8,128)(2,1)}, u32[]{:S(2)}) copy-start(bf16[64,2048]{1,0:T(8,128)(2,1)} %add_convert_fusion.2) | copy-start | bytes 786436
Sparse Core Ops, SparseCore 0:
  8.9 19.4 all-gather.6
  42.3 95.3 reduce-scatter.4
  156.5 39.9 all-gather.10
  198.4 38.8 all-gather.8
  245.4 30.1 reduce-scatter.6
  277.6 16.7 all-gather.12
  308.3 95.2 reduce-scatter.8
  423.4 39.9 all-gather.16
  465.8 38.8 all-gather.14
  512.2 30.1 reduce-scatter.10

commit v9 on v1

--- a/solution.py
+++ b/solution.py
@@ -69,15 +69,41 @@
     )
 
 
+def narrow_gather(state, n_narrow):
+    rows, cols = state.shape
+    half = rows // 2
+    parts = [
+        lax.all_gather(state[h * half : (h + 1) * half], "narrow", axis=0, tiled=True).reshape(
+            n_narrow, 1, half, cols
+        )
+        for h in range(2)
+    ]
+    return jnp.concatenate(parts, axis=1).reshape(n_narrow * rows, cols)
+
+
+def narrow_scatter(value, n_narrow):
+    rows, cols = value.shape
+    half = rows // n_narrow // 2
+    blocks = value.reshape(n_narrow, 2, half, cols)
+    parts = [
+        lax.psum_scatter(
+            blocks[:, h].reshape(n_narrow * half, cols), "narrow", scatter_dimension=0, tiled=True
+        )
+        for h in range(2)
+    ]
+    return jnp.concatenate(parts, axis=0)
+
+
 def on_device(hidden_in, w_query, w_keyval, w_out, key_cache, value_cache, lengths):
     w_q2 = w_query.reshape(w_query.shape[0], -1)
     w_kv2 = w_keyval.reshape(w_keyval.shape[0], -1)
+    n_narrow = lax.axis_size("narrow")
     new_keys = []
     new_vals = []
     result = hidden_in
     for step in range(STEPS):
         partial_value = attend_step(
-            lax.all_gather(result, "narrow", axis=0, tiled=True),
+            narrow_gather(result, n_narrow),
             step,
             w_q2,
             w_kv2,
@@ -88,7 +114,7 @@
             new_keys,
             new_vals,
         )
-        update = lax.psum_scatter(partial_value, "narrow", scatter_dimension=0, tiled=True)
+        update = narrow_scatter(partial_value, n_narrow)
         result = (result.astype(jnp.float32) + update).astype(jnp.bfloat16)
     return result
 

time: 513 us -> 550 us (1.072)
  blocking collectives: 0 us -> 30.2 us
  waiting for transfers between devices: 369 us -> 391 us
  matrix products: 87.3 us -> 72.1 us
    reduce_scatter x2 -> x4, waiting for transfers between devices: 60.1 us -> 101 us  [narrow_scatter(): lax.psum_scatter(blocks[:, h].reshape(n_narrow * half, cols), 'narrow', s...]
    all_gather x0 -> x4, blocking collectives: none -> 30.2 us  [narrow_gather(): lax.all_gather(state[h * half:(h + 1) * half], 'narrow', axis=0, tiled=True)]
    all_gather x2 -> x0, waiting for transfers between devices: 19.9 us -> none  [on_device(): lax.all_gather(result, 'narrow', axis=0, tiled=True)]
    dot_general x2, matrix products: 21 us -> 12.8 us  [attend_step(): part_q = jnp.dot(every, w_q2, preferred_element_type=jnp.float32)]
    dot_general x2, matrix products: 24.4 us -> 17.4 us  [attend_step(): jnp.dot(lax.all_gather(attended, 'wide', axis=0, tiled=True), w_out, pref...]
    unnamed x25 -> x21, local copies, waits for them, and re-layouts: 22.6 us -> 17.7 us
  transfers between devices with their start and end apart: 8 -> 8, of which waited for: 8 -> 8; matrix products, arithmetic and copies ran while one was open for 4% -> 0% of each run, Pallas kernels for 0% -> 0%
where the time goes in v9:
time: 550 us; the launch traced here: 549 us
  waiting for transfers between devices  391 us (71%)
  matrix products  72.1 us (13%)
  blocking collectives  30.2 us (5%)
  local copies, waits for them, and re-layouts  24 us (4%)
  other arithmetic  17 us (3%)
  between operations  13.9 us (3%)
    reduce_scatter x2, waiting for transfers between devices, attend_step(): lax.psum_scatter(jnp.concatenate((part_q, part_kv), axis=1), 'wide', scat...  191 us
    reduce_scatter x4, waiting for transfers between devices, narrow_scatter(): lax.psum_scatter(blocks[:, h].reshape(n_narrow * half, cols), 'narrow', s...  101 us
    all_gather x2, waiting for transfers between devices, attend_step(): lax.all_gather(attended, 'wide', axis=0, tiled=True)  98.3 us
    all_gather x4, blocking collectives, narrow_gather(): lax.all_gather(state[h * half:(h + 1) * half], 'narrow', axis=0, tiled=True)  30.2 us
    dot_general x2, matrix products, attend_step(): jnp.einsum('rgjd,rgcd->rgjc', query, key_cache, preferred_element_type=jn...  24.5 us
    unnamed x21, local copies, waits for them, and re-layouts  17.7 us
    dot_general x2, matrix products, attend_step(): jnp.dot(lax.all_gather(attended, 'wide', axis=0, tiled=True), w_out, pref...  17.4 us
    dot_general x2, matrix products, attend_step(): jnp.einsum('rgjc,rgcd->rgjd', p_cached, value_cache, preferred_element_ty...  14.8 us
  transfers between devices with their start and end apart: 8, of which 8 were waited for; matrix products, arithmetic and copies ran while one was open for 0% of the time, Pallas kernels for 0%

profile of v9, /device:TPU:0, one launch (start us, length us, event | category | flops | bytes accessed | tf_op | source)
XLA Modules:
  0.0 548.9 jit_solution(18294584317028985907)
XLA Ops:
  6.5 1.0 fusion.61
  7.5 8.6 %all_gather.18 = bf16[128,2048]{1,0:T(8,128)(2,1)S(1)} all-gather(bf16[32,2048]{1,0:T(8,128)(2,1)S(1)} %get-tuple-element.15), channel_id=1, replica_groups=mesh['narrow'=4,'wide'=8] {'narrow'}, dimensions={0}, use_global_device_ids=true | all-gather | bytes 655360 | tf_op jit(solution)/shard_map/all_gather | solution.py:76
  16.2 7.3 %all_gather.19 = bf16[128,2048]{1,0:T(8,128)(2,1)S(1)} all-gather(bf16[32,2048]{1,0:T(8,128)(2,1)S(1)} %get-tuple-element.16), channel_id=1, replica_groups=mesh['narrow'=4,'wide'=8] {'narrow'}, dimensions={0}, use_global_device_ids=true | all-gather | bytes 655360 | tf_op jit(solution)/shard_map/all_gather | solution.py:76
  23.5 12.3 %copy.59 = bf16[256,8,2,2048]{3,1,2,0:T(8,128)(2,1)S(1)} copy(bf16[256,8,2,2048]{3,2,1,0:T(2,128)(2,1)} %bitcast.69) | data formatting | bytes 33554432
  35.8 0.5 copy.60
  36.5 4.6 fusion.65
  41.1 0.5 copy-done
  41.6 0.7 fusion.66
  42.3 2.5 pad_maximum_fusion
  45.1 0.4 copy-done.5
  45.8 95.4 %reduce-scatter.7.cloned.1.call-done = f32[32,4608]{1,0:T(8,128)} async-done(((f32[256,4608]{1,0:T(8,128)}), f32[32,4608]{1,0:T(8,128)}) %reduce-scatter.7.cloned.1.call-update) | async-done | bytes 589840 | tf_op jit(solution)/shard_map/reduce_scatter | solution.py:35
  141.1 0.8 slice.99
  142.2 1.1 slice_bitcast_fusion.1
  143.3 0.2 subtract_convert_fusion.1
  143.7 0.3 fusion.24
  144.0 12.2 %fusion = (f32[32,2,16]{2,1,0:T(2,128)S(1)}, f32[32,2,16,1024]{3,2,1,0:T(8,128)}) fusion(pred[32,1024]{1,0:T(8,128)(4,1)S(1)} %iota_compare_fusion, bf16[32,2,1024,128]{3,2,1,0:T(8,128)(2,1)} %param.11, bf16[32,2,16,64]{3,2,1,0:T(8,128)(2,1)S(1)} %get-tuple-element.12, bf16[32,2,16,64]{3,2,1,0:T(8,128)(2,1)S(1)} %get-tuple-element.11), kind=kOutput, calls=%fused_computation.8 | convolution fusion | flops 272104448 | bytes 21270528 | tf_op jit(solution)/shard_map/rgjd,rgcd->rgjc/dot_general | solution.py:50
  156.3 3.8 fusion.2
  160.2 7.5 %fusion.19 = bf16[32,2,16,128]{3,2,1,0:T(8,128)(2,1)S(1)} fusion(bf16[32,2,1024,128]{3,2,1,0:T(8,128)(2,1)} %param.12, f32[32,2,16,1024]{3,2,1,0:T(8,128)S(1)} %copy-done.2, f32[32,2,16]{2,1,0:T(2,128)S(1)} %get-tuple-element.20, f32[32,2,16]{2,1,0:T(2,128)S(1)} %multiply_maximum_fusion, pred[32,1024]{1,0:T(8,128)(4,1)S(1)} %iota_compare_fusion, ...), kind=kOutput, calls=%fused_computation.28 | convolution fusion | flops 275120128 | bytes 21311488 | tf_op jit(solution)/shard_map/rgjc,rgcd->rgjd/dot_general | solution.py:62
  167.7 0.8 copy.94
  168.6 49.2 %all-gather.3.cloned.1.call-done = bf16[256,4096]{1,0:T(8,128)(2,1)} async-done(((bf16[32,4096]{1,0:T(8,128)(2,1)}), bf16[256,4096]{1,0:T(8,128)(2,1)}) %all-gather.3.cloned.1.call-update) | async-done | bytes 2097168 | tf_op jit(solution)/shard_map/all_gather | solution.py:66
  217.7 8.7 %fusion.67 = f32[256,2048]{1,0:T(8,128)S(1)} fusion(bf16[256,4096]{1,0:T(8,128)(2,1)} %all-gather.3.cloned.1.call-done, bf16[4096,2048]{1,0:T(8,128)(2,1)} %param.10), kind=kOutput, calls=%fused_computation.110 | convolution fusion | flops 4294967296 | bytes 20971520 | tf_op jit(solution)/shard_map/dot_general | solution.py:65
  226.5 1.5 fusion.59
  228.1 0.5 reduce-scatter.9.cloned.1.call-update
  228.7 22.9 %reduce-scatter.11.cloned.1.call-done = f32[32,2048]{1,0:T(8,128)} async-done(((f32[128,2048]{1,0:T(8,128)}), f32[32,2048]{1,0:T(8,128)}) %reduce-scatter.11.cloned.1.call-update) | async-done | bytes 262160 | tf_op jit(solution)/shard_map/reduce_scatter | solution.py:89
  251.6 27.4 %reduce-scatter.9.cloned.1.call-done = f32[32,2048]{1,0:T(8,128)} async-done(((f32[128,2048]{1,0:T(8,128)}), f32[32,2048]{1,0:T(8,128)}) %reduce-scatter.9.cloned.1.call-update) | async-done | bytes 262160 | tf_op jit(solution)/shard_map/reduce_scatter | solution.py:89
  279.0 1.1 fusion.21
  280.1 6.8 %all_gather.22 = bf16[128,2048]{1,0:T(8,128)(2,1)S(1)} all-gather(bf16[32,2048]{1,0:T(8,128)(2,1)S(1)} %get-tuple-element.14), channel_id=1, replica_groups=mesh['narrow'=4,'wide'=8] {'narrow'}, dimensions={0}, use_global_device_ids=true | all-gather | bytes 655360 | tf_op jit(solution)/shard_map/all_gather | solution.py:76
  286.9 7.5 %all_gather.21 = bf16[128,2048]{1,0:T(8,128)(2,1)S(1)} all-gather(bf16[32,2048]{1,0:T(8,128)(2,1)S(1)} %get-tuple-element.13), channel_id=1, replica_groups=mesh['narrow'=4,'wide'=8] {'narrow'}, dimensions={0}, use_global_device_ids=true | all-gather | bytes 655360 | tf_op jit(solution)/shard_map/all_gather | solution.py:76
  294.5 8.2 %fusion.68 = f32[256,4096]{1,0:T(8,128)S(1)} fusion(bf16[256,2048]{1,0:T(8,128)(2,1)S(1)} %bitcast.87, bf16[2048,4096]{1,0:T(8,128)(2,1)} %bitcast.71), kind=kOutput, calls=%fused_computation.111 | convolution fusion | flops 4294967296 | bytes 22020096 | tf_op jit(solution)/shard_map/dot_general | solution.py:33
  302.7 0.7 fusion.69
  303.4 2.5 pad_maximum_fusion.1
  306.1 95.6 %reduce-scatter.13.cloned.1.call-done = f32[32,4608]{1,0:T(8,128)} async-done(((f32[256,4608]{1,0:T(8,128)}), f32[32,4608]{1,0:T(8,128)}) %reduce-scatter.13.cloned.1.call-update) | async-done | bytes 589840 | tf_op jit(solution)/shard_map/reduce_scatter | solution.py:35
  401.7 0.8 slice.110
  402.9 1.1 slice_bitcast_fusion
  404.0 0.2 subtract_convert_fusion
  404.3 12.3 %fusion.1 = (f32[32,2,16]{2,1,0:T(2,128)S(1)}, f32[32,2,16,1024]{3,2,1,0:T(8,128)}) fusion(pred[32,1024]{1,0:T(8,128)(4,1)S(1)} %iota_compare_fusion, bf16[32,2,1024,128]{3,2,1,0:T(8,128)(2,1)} %param.11, bf16[32,2,16,64]{3,2,1,0:T(8,128)(2,1)S(1)} %get-tuple-element.10, bf16[32,2,16,64]{3,2,1,0:T(8,128)(2,1)S(1)} %get-tuple-element.9), kind=kOutput, calls=%fused_computation.9 | convolution fusion | flops 272104448 | bytes 21270528 | tf_op jit(solution)/shard_map/rgjd,rgcd->rgjc/dot_general | solution.py:50
  416.5 0.5 fusion.64
  417.2 3.9 fusion.3
  421.2 7.3 %fusion.5 = f32[32,2,16,128]{3,2,1,0:T(8,128)S(1)} fusion(bf16[32,2,1024,128]{3,2,1,0:T(8,128)(2,1)} %param.12, f32[32,2,16,1024]{3,2,1,0:T(8,128)S(1)} %copy-done.1, f32[32,2,16]{2,1,0:T(2,128)S(1)} %add.63, f32[32,2,16]{2,1,0:T(2,128)S(1)} %max.13, pred[32,1024]{1,0:T(8,128)(4,1)S(1)} %iota_compare_fusion), kind=kOutput, calls=%fused_computation.13 | convolution fusion | flops 274726912 | bytes 21536768 | tf_op jit(solution)/shard_map/rgjc,rgcd->rgjd/dot_general | solution.py:62
  428.6 0.3 fusion.20
  428.9 0.8 copy.93
  429.8 49.1 %all-gather.5.cloned.1.call-done = bf16[256,4096]{1,0:T(8,128)(2,1)} async-done(((bf16[32,4096]{1,0:T(8,128)(2,1)}), bf16[256,4096]{1,0:T(8,128)(2,1)}) %all-gather.5.cloned.1.call-update) | async-done | bytes 2097168 | tf_op jit(solution)/shard_map/all_gather | solution.py:66
  478.9 8.7 %fusion.70 = f32[256,2048]{1,0:T(8,128)S(1)} fusion(bf16[256,4096]{1,0:T(8,128)(2,1)} %all-gather.5.cloned.1.call-done, bf16[4096,2048]{1,0:T(8,128)(2,1)} %param.10), kind=kOutput, calls=%fused_computation.113 | convolution fusion | flops 4294967296 | bytes 20971520 | tf_op jit(solution)/shard_map/dot_general | solution.py:65
  487.6 1.6 fusion.58
  489.2 0.7 reduce-scatter.17.cloned.1.call-update
  489.9 22.8 %reduce-scatter.15.cloned.1.call-done = f32[32,2048]{1,0:T(8,128)} async-done(((f32[128,2048]{1,0:T(8,128)}), f32[32,2048]{1,0:T(8,128)}) %reduce-scatter.15.cloned.1.call-update) | async-done | bytes 262160 | tf_op jit(solution)/shard_map/reduce_scatter | solution.py:89
  512.7 27.6 %reduce-scatter.17.cloned.1.call-done = f32[32,2048]{1,0:T(8,128)} async-done(((f32[128,2048]{1,0:T(8,128)}), f32[32,2048]{1,0:T(8,128)}) %reduce-scatter.17.cloned.1.call-update) | async-done | bytes 262160 | tf_op jit(solution)/shard_map/reduce_scatter | solution.py:89
  540.3 1.8 fusion.22
  (56 shorter events, 2.2 us)
Async XLA Ops:
  6.5 134.6 %reduce-scatter.7.cloned.1.call-start = ((), (), s32[]{:S(2)}) async-start(), calls=%async_computation.6 | async-start | bytes 5308416 | tf_op jit(solution)/shard_map/reduce_scatter | solution.py:35
  23.5 12.4 %copy-start.3 = (bf16[2048,2,256]{2,1,0:T(2,128)(2,1)S(1)}, bf16[2048,2,256]{2,1,0:T(2,128)(2,1)}, u32[]{:S(2)}) copy-start(bf16[2048,2,256]{2,1,0:T(2,128)(2,1)} %param.9) | copy-start | bytes 6291460
  35.8 5.7 %copy-start = (bf16[256,8,2,2048]{3,1,2,0:T(8,128)(2,1)}, bf16[256,8,2,2048]{3,1,2,0:T(8,128)(2,1)S(1)}, u32[]{:S(2)}) copy-start(bf16[256,8,2,2048]{3,1,2,0:T(8,128)(2,1)S(1)} %copy.59) | copy-start | bytes 50331652
  44.8 0.7 copy-start.5
  44.9 172.9 %all-gather.3.cloned.1.call-start = ((), (), s32[]{:S(2)}) async-start(), calls=%async_computation.7 | async-start | bytes 2359296 | tf_op jit(solution)/shard_map/all_gather | solution.py:66
  156.3 3.9 copy-start.2
  168.5 83.0 %reduce-scatter.11.cloned.1.call-start = ((), (), s32[]{:S(2)}) async-start(), calls=%async_computation.9 | async-start | bytes 1310720 | tf_op jit(solution)/shard_map/reduce_scatter | solution.py:89
  226.5 52.5 %copy-start.4 = (bf16[64,2048]{1,0:T(8,128)(2,1)S(1)}, bf16[64,2048]{1,0:T(8,128)(2,1)}, u32[]{:S(2)}) copy-start(bf16[64,2048]{1,0:T(8,128)(2,1)} %param.7) | copy-start | bytes 786436
  228.0 51.0 %reduce-scatter.9.cloned.1.call-start = ((), (), s32[]{:S(2)}) async-start(), calls=%async_computation.8 | async-start | bytes 1310720 | tf_op jit(solution)/shard_map/reduce_scatter | solution.py:89
  228.6 173.1 %reduce-scatter.13.cloned.1.call-start = ((), (), s32[]{:S(2)}) async-start(), calls=%async_computation.10 | async-start | bytes 5308416 | tf_op jit(solution)/shard_map/reduce_scatter | solution.py:35
  306.0 172.9 %all-gather.5.cloned.1.call-start = ((), (), s32[]{:S(2)}) async-start(), calls=%async_computation.11 | async-start | bytes 2359296 | tf_op jit(solution)/shard_map/all_gather | solution.py:66
  416.5 4.7 copy-start.1
  429.7 83.0 %reduce-scatter.15.cloned.1.call-start = ((), (), s32[]{:S(2)}) async-start(), calls=%async_computation.12 | async-start | bytes 1310720 | tf_op jit(solution)/shard_map/reduce_scatter | solution.py:89
  489.2 51.1 %reduce-scatter.17.cloned.1.call-start = ((), (), s32[]{:S(2)}) async-start(), calls=%async_computation.13 | async-start | bytes 1310720 | tf_op jit(solution)/shard_map/reduce_scatter | solution.py:89
Sparse Core Ops, SparseCore 0:
  45.0 96.1 reduce-scatter.6
  168.6 49.0 all-gather.2
  228.2 23.3 reduce-scatter.10
  254.1 24.8 reduce-scatter.8
  306.1 95.6 reduce-scatter.12
  429.8 49.0 all-gather.4
  489.3 23.3 reduce-scatter.14
  515.4 24.8 reduce-scatter.16

commit v10 on v1

--- a/solution.py
+++ b/solution.py
@@ -69,6 +69,18 @@
     )
 
 
+def narrow_gather(state, n_narrow):
+    rows, cols = state.shape
+    half = rows // 2
+    parts = [
+        lax.all_gather(state[h * half : (h + 1) * half], "narrow", axis=0, tiled=True).reshape(
+            n_narrow, 1, half, cols
+        )
+        for h in range(2)
+    ]
+    return jnp.concatenate(parts, axis=1).reshape(n_narrow * rows, cols)
+
+
 def on_device(hidden_in, w_query, w_keyval, w_out, key_cache, value_cache, lengths):
     w_q2 = w_query.reshape(w_query.shape[0], -1)
     w_kv2 = w_keyval.reshape(w_keyval.shape[0], -1)
@@ -77,7 +89,9 @@
     result = hidden_in
     for step in range(STEPS):
         partial_value = attend_step(
-            lax.all_gather(result, "narrow", axis=0, tiled=True),
+            lax.all_gather(result, "narrow", axis=0, tiled=True)
+            if step == 0
+            else narrow_gather(result, lax.axis_size("narrow")),
             step,
             w_q2,
             w_kv2,

time: 513 us -> 508 us (level)
  waiting for transfers between devices: 369 us -> 352 us
  blocking collectives: 0 us -> 14 us
    all_gather x2 -> x1, waiting for transfers between devices: 19.9 us -> 3.07 us  [on_device(): lax.all_gather(result, 'narrow', axis=0, tiled=True)]
    all_gather x0 -> x2, blocking collectives: none -> 14 us  [narrow_gather(): lax.all_gather(state[h * half:(h + 1) * half], 'narrow', axis=0, tiled=True)]
    unnamed x25 -> x21, local copies, waits for them, and re-layouts: 22.6 us -> 22.5 us
  transfers between devices with their start and end apart: 8 -> 7, of which waited for: 8 -> 7; matrix products, arithmetic and copies ran while one was open for 4% -> 4% of each run, Pallas kernels for 0% -> 0%
where the time goes in v10:
time: 508 us; the launch traced here: 507 us
  waiting for transfers between devices  352 us (69%)
  matrix products  85 us (17%)
  local copies, waits for them, and re-layouts  24.7 us (5%)
  other arithmetic  16.9 us (3%)
  blocking collectives  14 us (3%)
  between operations  13.8 us (3%)
    reduce_scatter x2, waiting for transfers between devices, attend_step(): lax.psum_scatter(jnp.concatenate((part_q, part_kv), axis=1), 'wide', scat...  190 us
    all_gather x2, waiting for transfers between devices, attend_step(): lax.all_gather(attended, 'wide', axis=0, tiled=True)  98.1 us
    reduce_scatter x2, waiting for transfers between devices, on_device(): lax.psum_scatter(partial_value, 'narrow', scatter_dimension=0, tiled=True)  60.1 us
    dot_general x2, matrix products, attend_step(): jnp.einsum('rgjd,rgcd->rgjc', query, key_cache, preferred_element_type=jn...  24.5 us
    dot_general x2, matrix products, attend_step(): jnp.dot(lax.all_gather(attended, 'wide', axis=0, tiled=True), w_out, pref...  24.4 us
    unnamed x21, local copies, waits for them, and re-layouts  22.5 us
    dot_general x2, matrix products, attend_step(): part_q = jnp.dot(every, w_q2, preferred_element_type=jnp.float32)  18.6 us
    dot_general x2, matrix products, attend_step(): jnp.einsum('rgjc,rgcd->rgjd', p_cached, value_cache, preferred_element_ty...  14.8 us
  transfers between devices with their start and end apart: 7, of which 7 were waited for; matrix products, arithmetic and copies ran while one was open for 4% of the time, Pallas kernels for 0%

profile of v10, /device:TPU:0, one launch (start us, length us, event | category | flops | bytes accessed | tf_op | source)
XLA Modules:
  0.0 507.4 jit_solution(4399895034537786279)
XLA Ops:
  6.5 0.7 all-gather.4.cloned.1.call-update
  7.3 17.5 %copy.69 = bf16[256,8,2,2048]{3,1,2,0:T(8,128)(2,1)} copy(bf16[256,8,2,2048]{3,2,1,0:T(2,128)(2,1)} %bitcast.64) | data formatting | bytes 33554432
  24.8 0.5 copy.70
  25.3 3.1 all-gather.4.cloned.1.call-done
  28.4 10.5 %fusion.60 = f32[256,4096]{1,0:T(8,128)S(1)} fusion(bf16[256,2048]{1,0:T(8,128)(2,1)} %all-gather.4.cloned.1.call-done, bf16[2048,4096]{1,0:T(8,128)(2,1)} %bitcast.65), kind=kOutput, calls=%fused_computation.102 | convolution fusion | flops 4294967296 | bytes 22020096 | tf_op jit(solution)/shard_map/dot_general | solution.py:33
  38.9 0.7 fusion.61
  39.6 2.5 pad_maximum_fusion
  42.2 0.6 copy-done.4
  42.9 0.2 multiply_cosine_fusion
  43.1 94.6 %reduce-scatter.5.cloned.1.call-done = f32[32,4608]{1,0:T(8,128)} async-done(((f32[256,4608]{1,0:T(8,128)}), f32[32,4608]{1,0:T(8,128)}) %reduce-scatter.5.cloned.1.call-update) | async-done | bytes 589840 | tf_op jit(solution)/shard_map/reduce_scatter | solution.py:35
  137.7 0.8 slice.75
  138.6 0.1 fusion.58
  138.7 1.1 slice_bitcast_fusion.1
  139.8 0.1 copy.71
  139.9 0.2 subtract_convert_fusion.1
  140.2 0.3 fusion.22
  140.5 12.2 %fusion = (f32[32,2,16]{2,1,0:T(2,128)S(1)}, f32[32,2,16,1024]{3,2,1,0:T(8,128)}) fusion(pred[32,1024]{1,0:T(8,128)(4,1)S(1)} %iota_compare_fusion, bf16[32,2,1024,128]{3,2,1,0:T(8,128)(2,1)} %param.11, bf16[32,2,16,64]{3,2,1,0:T(8,128)(2,1)S(1)} %get-tuple-element.8, bf16[32,2,16,64]{3,2,1,0:T(8,128)(2,1)S(1)} %get-tuple-element.7), kind=kOutput, calls=%fused_computation.8 | convolution fusion | flops 272104448 | bytes 21270528 | tf_op jit(solution)/shard_map/rgjd,rgcd->rgjc/dot_general | solution.py:50
  152.8 3.8 fusion.2
  156.7 7.5 %fusion.19 = bf16[32,2,16,128]{3,2,1,0:T(8,128)(2,1)S(1)} fusion(bf16[32,2,1024,128]{3,2,1,0:T(8,128)(2,1)} %param.12, f32[32,2,16,1024]{3,2,1,0:T(8,128)S(1)} %copy-done.1, f32[32,2,16]{2,1,0:T(2,128)S(1)} %get-tuple-element.14, f32[32,2,16]{2,1,0:T(2,128)S(1)} %multiply_maximum_fusion, pred[32,1024]{1,0:T(8,128)(4,1)S(1)} %iota_compare_fusion, ...), kind=kOutput, calls=%fused_computation.28 | convolution fusion | flops 275120128 | bytes 21311488 | tf_op jit(solution)/shard_map/rgjc,rgcd->rgjd/dot_general | solution.py:62
  164.2 0.8 copy.104
  165.1 0.2 reduce-scatter.7.cloned.1.call-start
  165.3 49.0 %all-gather.6.cloned.1.call-done = bf16[256,4096]{1,0:T(8,128)(2,1)} async-done(((bf16[32,4096]{1,0:T(8,128)(2,1)}), bf16[256,4096]{1,0:T(8,128)(2,1)}) %all-gather.6.cloned.1.call-update) | async-done | bytes 2097168 | tf_op jit(solution)/shard_map/all_gather | solution.py:66
  214.3 12.2 %fusion.62 = f32[256,2048]{1,0:T(8,128)} fusion(bf16[256,4096]{1,0:T(8,128)(2,1)} %all-gather.6.cloned.1.call-done, bf16[4096,2048]{1,0:T(8,128)(2,1)} %param.10), kind=kOutput, calls=%fused_computation.104 | convolution fusion | flops 4294967296 | bytes 20971520 | tf_op jit(solution)/shard_map/dot_general | solution.py:65
  226.6 30.0 %reduce-scatter.7.cloned.1.call-done = f32[64,2048]{1,0:T(8,128)} async-done(((f32[256,2048]{1,0:T(8,128)}), f32[64,2048]{1,0:T(8,128)}) %reduce-scatter.7.cloned.1.call-update) | async-done | bytes 524304 | tf_op jit(solution)/shard_map/reduce_scatter | solution.py:105
  256.6 1.1 add_convert_fusion.2
  257.7 6.8 %all_gather.17 = bf16[128,2048]{1,0:T(8,128)(2,1)S(1)} all-gather(bf16[32,2048]{1,0:T(8,128)(2,1)S(1)} %get-tuple-element.9), channel_id=1, replica_groups=mesh['narrow'=4,'wide'=8] {'narrow'}, dimensions={0}, use_global_device_ids=true | all-gather | bytes 655360 | tf_op jit(solution)/shard_map/all_gather | solution.py:76
  264.5 7.3 %all_gather.18 = bf16[128,2048]{1,0:T(8,128)(2,1)S(1)} all-gather(bf16[32,2048]{1,0:T(8,128)(2,1)S(1)} %get-tuple-element.10), channel_id=1, replica_groups=mesh['narrow'=4,'wide'=8] {'narrow'}, dimensions={0}, use_global_device_ids=true | all-gather | bytes 655360 | tf_op jit(solution)/shard_map/all_gather | solution.py:76
  271.8 0.1 pad_maximum_fusion.2
  271.9 8.2 %fusion.63 = f32[256,4096]{1,0:T(8,128)S(1)} fusion(bf16[256,2048]{1,0:T(8,128)(2,1)S(1)} %bitcast.74, bf16[2048,4096]{1,0:T(8,128)(2,1)} %bitcast.66), kind=kOutput, calls=%fused_computation.105 | convolution fusion | flops 4294967296 | bytes 22020096 | tf_op jit(solution)/shard_map/dot_general | solution.py:33
  280.0 0.7 fusion.64
  280.8 2.5 pad_maximum_fusion.1
  283.3 0.3 all-gather.8.cloned.1.call-start
  283.7 95.6 %reduce-scatter.9.cloned.1.call-done = f32[32,4608]{1,0:T(8,128)} async-done(((f32[256,4608]{1,0:T(8,128)}), f32[32,4608]{1,0:T(8,128)}) %reduce-scatter.9.cloned.1.call-update) | async-done | bytes 589840 | tf_op jit(solution)/shard_map/reduce_scatter | solution.py:35
  379.3 0.8 slice.84
  380.4 1.1 slice_bitcast_fusion
  381.5 0.1 copy.73
  381.6 0.2 subtract_convert_fusion
  381.8 12.3 %fusion.1 = (f32[32,2,16]{2,1,0:T(2,128)S(1)}, f32[32,2,16,1024]{3,2,1,0:T(8,128)}) fusion(pred[32,1024]{1,0:T(8,128)(4,1)S(1)} %iota_compare_fusion, bf16[32,2,1024,128]{3,2,1,0:T(8,128)(2,1)} %param.11, bf16[32,2,16,64]{3,2,1,0:T(8,128)(2,1)S(1)} %get-tuple-element.6, bf16[32,2,16,64]{3,2,1,0:T(8,128)(2,1)S(1)} %get-tuple-element.5), kind=kOutput, calls=%fused_computation.9 | convolution fusion | flops 272104448 | bytes 21270528 | tf_op jit(solution)/shard_map/rgjd,rgcd->rgjc/dot_general | solution.py:50
  394.1 0.5 fusion.59
  394.6 0.1 fusion.24
  394.8 3.9 fusion.3
  398.8 7.3 %fusion.5 = f32[32,2,16,128]{3,2,1,0:T(8,128)S(1)} fusion(bf16[32,2,1024,128]{3,2,1,0:T(8,128)(2,1)} %param.12, f32[32,2,16,1024]{3,2,1,0:T(8,128)S(1)} %copy-done, f32[32,2,16]{2,1,0:T(2,128)S(1)} %add.59, f32[32,2,16]{2,1,0:T(2,128)S(1)} %max.13, pred[32,1024]{1,0:T(8,128)(4,1)S(1)} %iota_compare_fusion), kind=kOutput, calls=%fused_computation.13 | convolution fusion | flops 274726912 | bytes 21536768 | tf_op jit(solution)/shard_map/rgjc,rgcd->rgjd/dot_general | solution.py:62
  406.1 0.3 fusion.20
  406.4 0.8 copy.103
  407.3 49.2 %all-gather.8.cloned.1.call-done = bf16[256,4096]{1,0:T(8,128)(2,1)} async-done(((bf16[32,4096]{1,0:T(8,128)(2,1)}), bf16[256,4096]{1,0:T(8,128)(2,1)}) %all-gather.8.cloned.1.call-update) | async-done | bytes 2097168 | tf_op jit(solution)/shard_map/all_gather | solution.py:66
  456.5 12.2 %fusion.65 = f32[256,2048]{1,0:T(8,128)} fusion(bf16[256,4096]{1,0:T(8,128)(2,1)} %all-gather.8.cloned.1.call-done, bf16[4096,2048]{1,0:T(8,128)(2,1)} %param.10), kind=kOutput, calls=%fused_computation.107 | convolution fusion | flops 4294967296 | bytes 20971520 | tf_op jit(solution)/shard_map/dot_general | solution.py:65
  468.7 30.1 %reduce-scatter.11.cloned.1.call-done = f32[64,2048]{1,0:T(8,128)} async-done(((f32[256,2048]{1,0:T(8,128)}), f32[64,2048]{1,0:T(8,128)}) %reduce-scatter.11.cloned.1.call-update) | async-done | bytes 524304 | tf_op jit(solution)/shard_map/reduce_scatter | solution.py:105
  498.8 1.8 add_convert_fusion
  (47 shorter events, 1.1 us)
Async XLA Ops:
  6.5 21.8 %all-gather.4.cloned.1.call-start = ((), (), s32[]{:S(2)}) async-start(), calls=%async_computation.4 | async-start | bytes 1310720 | tf_op jit(solution)/shard_map/all_gather | solution.py:92
  7.3 130.4 %reduce-scatter.5.cloned.1.call-start = ((), (), s32[]{:S(2)}) async-start(), calls=%async_computation.5 | async-start | bytes 5308416 | tf_op jit(solution)/shard_map/reduce_scatter | solution.py:35
  7.3 17.5 %copy-start.2 = (bf16[2048,2,256]{2,1,0:T(2,128)(2,1)S(1)}, bf16[2048,2,256]{2,1,0:T(2,128)(2,1)}, u32[]{:S(2)}) copy-start(bf16[2048,2,256]{2,1,0:T(2,128)(2,1)} %param.9) | copy-start | bytes 6291460
  28.4 10.5 %copy-start.5 = (bf16[256,2048]{1,0:T(8,128)(2,1)S(1)}, bf16[256,2048]{1,0:T(8,128)(2,1)}, u32[]{:S(2)}) copy-start(bf16[256,2048]{1,0:T(8,128)(2,1)} %all-gather.4.cloned.1.call-done) | copy-start | bytes 3145732
  42.1 0.7 copy-start.4
  42.2 172.1 %all-gather.6.cloned.1.call-start = ((), (), s32[]{:S(2)}) async-start(), calls=%async_computation.6 | async-start | bytes 2359296 | tf_op jit(solution)/shard_map/all_gather | solution.py:66
  152.8 3.9 copy-start.1
  165.1 91.5 %copy-start.3 = (bf16[64,2048]{1,0:T(8,128)(2,1)S(1)}, bf16[64,2048]{1,0:T(8,128)(2,1)}, u32[]{:S(2)}) copy-start(bf16[64,2048]{1,0:T(8,128)(2,1)} %param.7) | copy-start | bytes 786436
  165.1 91.5 %reduce-scatter.7.cloned.1.call-start = ((), (), s32[]{:S(2)}) async-start(), calls=%async_computation.7 | async-start | bytes 2621440 | tf_op jit(solution)/shard_map/reduce_scatter | solution.py:105
  226.5 152.8 %reduce-scatter.9.cloned.1.call-start = ((), (), s32[]{:S(2)}) async-start(), calls=%async_computation.8 | async-start | bytes 5308416 | tf_op jit(solution)/shard_map/reduce_scatter | solution.py:35
  283.3 173.1 %all-gather.8.cloned.1.call-start = ((), (), s32[]{:S(2)}) async-start(), calls=%async_computation.9 | async-start | bytes 2359296 | tf_op jit(solution)/shard_map/all_gather | solution.py:66
  394.1 4.7 copy-start
  407.3 91.5 %reduce-scatter.11.cloned.1.call-start = ((), (), s32[]{:S(2)}) async-start(), calls=%async_computation.10 | async-start | bytes 2621440 | tf_op jit(solution)/shard_map/reduce_scatter | solution.py:105
Sparse Core Ops, SparseCore 0:
  8.9 19.4 all-gather.3
  42.3 95.3 reduce-scatter.4
  165.2 49.0 all-gather.5
  226.6 29.9 reduce-scatter.6
  283.5 95.7 reduce-scatter.8
  407.4 49.0 all-gather.7
  468.8 29.9 reduce-scatter.10

commit v11 on v10

--- a/solution.py
+++ b/solution.py
@@ -63,7 +63,13 @@
     out = out + jnp.einsum("rgjs,rgsd->rgjd", p_fresh, vals_now, preferred_element_type=jnp.float32)
     attended = out.astype(jnp.bfloat16).reshape(local_rows, groups * per_group * head_dim)
     return jnp.dot(
-        lax.all_gather(attended, "wide", axis=0, tiled=True),
+        jnp.concatenate(
+            [
+                lax.all_gather(attended[:, i * 1024 : (i + 1) * 1024], "wide", axis=0, tiled=True)
+                for i in range(attended.shape[1] // 1024)
+            ],
+            axis=1,
+        ),
         w_out,
         preferred_element_type=jnp.float32,
     )

time: 508 us -> 657 us (1.29)
  blocking collectives: 14 us -> 265 us
  waiting for transfers between devices: 352 us -> 257 us
    all_gather x0 -> x8, blocking collectives: none -> 251 us  [attend_step(): lax.all_gather(attended[:, i * 1024:(i + 1) * 1024], 'wide', axis=0, tile...]
    all_gather x2 -> x0, waiting for transfers between devices: 98.1 us -> none  [attend_step(): lax.all_gather(attended, 'wide', axis=0, tiled=True)]
  transfers between devices with their start and end apart: 7 -> 5, of which waited for: 7 -> 5; matrix products, arithmetic and copies ran while one was open for 4% -> 3% of each run, Pallas kernels for 0% -> 0%
where the time goes in v11:
time: 657 us
  blocking collectives  265 us (40%)
  waiting for transfers between devices  257 us (39%)
  matrix products  80.9 us (12%)
  local copies, waits for them, and re-layouts  23.4 us (4%)
  other arithmetic  16.9 us (3%)
  between operations  13.5 us (2%)
    all_gather x8, blocking collectives, attend_step(): lax.all_gather(attended[:, i * 1024:(i + 1) * 1024], 'wide', axis=0, tile...  251 us
    reduce_scatter x2, waiting for transfers between devices, attend_step(): lax.psum_scatter(jnp.concatenate((part_q, part_kv), axis=1), 'wide', scat...  190 us
    reduce_scatter x2, waiting for transfers between devices, on_device(): lax.psum_scatter(partial_value, 'narrow', scatter_dimension=0, tiled=True)  62.4 us
    dot_general x2, matrix products, attend_step(): jnp.einsum('rgjd,rgcd->rgjc', query, key_cache, preferred_element_type=jn...  24.5 us
    unnamed x21, local copies, waits for them, and re-layouts  21.2 us
    dot_general x2, matrix products, attend_step(): jnp.dot(jnp.concatenate([lax.all_gather(attended[:, i * 1024:(i + 1) * 10...  20.4 us
    dot_general x2, matrix products, attend_step(): part_q = jnp.dot(every, w_q2, preferred_element_type=jnp.float32)  18.6 us
    dot_general x2, matrix products, attend_step(): jnp.einsum('rgjc,rgcd->rgjd', p_cached, value_cache, preferred_element_ty...  14.8 us
  transfers between devices with their start and end apart: 5, of which 5 were waited for; matrix products, arithmetic and copies ran while one was open for 3% of the time, Pallas kernels for 0%

profile of v11, /device:TPU:0, one launch (start us, length us, event | category | flops | bytes accessed | tf_op | source)
XLA Modules:
  0.0 656.7 jit_solution(6499864838221455631)
XLA Ops:
  6.5 0.7 all-gather.2.cloned.1.call-update
  7.3 17.5 %copy.69 = bf16[256,8,2,2048]{3,1,2,0:T(8,128)(2,1)} copy(bf16[256,8,2,2048]{3,2,1,0:T(2,128)(2,1)} %bitcast.62) | data formatting | bytes 33554432
  24.8 0.5 copy.70
  25.3 3.1 all-gather.2.cloned.1.call-done
  28.4 10.5 %fusion.80 = f32[256,4096]{1,0:T(8,128)S(1)} fusion(bf16[256,2048]{1,0:T(8,128)(2,1)} %all-gather.2.cloned.1.call-done, bf16[2048,4096]{1,0:T(8,128)(2,1)} %bitcast.63), kind=kOutput, calls=%fused_computation.122 | convolution fusion | flops 4294967296 | bytes 22020096 | tf_op jit(solution)/shard_map/dot_general | solution.py:33
  38.9 0.7 fusion.81
  39.6 2.5 pad_maximum_fusion
  42.2 0.6 copy-done.4
  42.9 0.2 multiply_cosine_fusion
  43.1 94.6 %reduce-scatter.5.cloned.1.call-done = f32[32,4608]{1,0:T(8,128)} async-done(((f32[256,4608]{1,0:T(8,128)}), f32[32,4608]{1,0:T(8,128)}) %reduce-scatter.5.cloned.1.call-update) | async-done | bytes 589840 | tf_op jit(solution)/shard_map/reduce_scatter | solution.py:35
  137.7 0.8 slice.107
  138.7 1.1 slice_bitcast_fusion.1
  139.9 0.2 subtract_convert_fusion.1
  140.2 0.3 fusion.38
  140.5 12.2 %fusion = (f32[32,2,16]{2,1,0:T(2,128)S(1)}, f32[32,2,16,1024]{3,2,1,0:T(8,128)}) fusion(pred[32,1024]{1,0:T(8,128)(4,1)S(1)} %iota_compare_fusion, bf16[32,2,1024,128]{3,2,1,0:T(8,128)(2,1)} %param.11, bf16[32,2,16,64]{3,2,1,0:T(8,128)(2,1)S(1)} %get-tuple-element.8, bf16[32,2,16,64]{3,2,1,0:T(8,128)(2,1)S(1)} %get-tuple-element.7), kind=kOutput, calls=%fused_computation.8 | convolution fusion | flops 272104448 | bytes 21270528 | tf_op jit(solution)/shard_map/rgjd,rgcd->rgjc/dot_general | solution.py:50
  152.8 3.8 fusion.2
  156.7 7.5 %fusion.35 = bf16[32,2,16,128]{3,2,1,0:T(8,128)(2,1)S(1)} fusion(bf16[32,2,1024,128]{3,2,1,0:T(8,128)(2,1)} %param.12, f32[32,2,16,1024]{3,2,1,0:T(8,128)S(1)} %copy-done.1, f32[32,2,16]{2,1,0:T(2,128)S(1)} %get-tuple-element.22, f32[32,2,16]{2,1,0:T(2,128)S(1)} %multiply_maximum_fusion, pred[32,1024]{1,0:T(8,128)(4,1)S(1)} %iota_compare_fusion, ...), kind=kOutput, calls=%fused_computation.44 | convolution fusion | flops 275120128 | bytes 21311488 | tf_op jit(solution)/shard_map/rgjc,rgcd->rgjd/dot_general | solution.py:62
  164.2 0.1 copy.104
  164.4 31.5 %all_gather.34 = bf16[256,1024]{1,0:T(8,128)(2,1)S(1)} all-gather(bf16[32,1024]{1,0:T(8,128)(2,1)S(1)} %get-tuple-element.15), channel_id=1, replica_groups=mesh['narrow'=4,'wide'=8] {'wide'}, dimensions={0}, use_global_device_ids=true | all-gather | bytes 589824 | tf_op jit(solution)/shard_map/all_gather | solution.py:68
  195.9 31.4 %all_gather.35 = bf16[256,1024]{1,0:T(8,128)(2,1)S(1)} all-gather(bf16[32,1024]{1,0:T(8,128)(2,1)S(1)} %get-tuple-element.18), channel_id=1, replica_groups=mesh['narrow'=4,'wide'=8] {'wide'}, dimensions={0}, use_global_device_ids=true | all-gather | bytes 589824 | tf_op jit(solution)/shard_map/all_gather | solution.py:68
  227.2 31.5 %all_gather.36 = bf16[256,1024]{1,0:T(8,128)(2,1)S(1)} all-gather(bf16[32,1024]{1,0:T(8,128)(2,1)S(1)} %get-tuple-element.17), channel_id=1, replica_groups=mesh['narrow'=4,'wide'=8] {'wide'}, dimensions={0}, use_global_device_ids=true | all-gather | bytes 589824 | tf_op jit(solution)/shard_map/all_gather | solution.py:68
  258.7 31.2 %all_gather.37 = bf16[256,1024]{1,0:T(8,128)(2,1)S(1)} all-gather(bf16[32,1024]{1,0:T(8,128)(2,1)S(1)} %get-tuple-element.16), channel_id=1, replica_groups=mesh['narrow'=4,'wide'=8] {'wide'}, dimensions={0}, use_global_device_ids=true | all-gather | bytes 589824 | tf_op jit(solution)/shard_map/all_gather | solution.py:68
  289.9 10.2 %fusion.6 = f32[256,2048]{1,0:T(8,128)} fusion(bf16[4096,2048]{1,0:T(8,128)(2,1)} %param.10, bf16[256,1024]{1,0:T(8,128)(2,1)S(1)} %all_gather.37, bf16[256,1024]{1,0:T(8,128)(2,1)S(1)} %all_gather.36, bf16[256,1024]{1,0:T(8,128)(2,1)S(1)} %all_gather.35, bf16[256,1024]{1,0:T(8,128)(2,1)S(1)} %all_gather.34), kind=kOutput, calls=%fused_computation.14 | convolution fusion | flops 4303355904 | bytes 20971520 | tf_op jit(solution)/shard_map/dot_general | solution.py:65
  300.2 31.1 %reduce-scatter.7.cloned.1.call-done = f32[64,2048]{1,0:T(8,128)} async-done(((f32[256,2048]{1,0:T(8,128)}), f32[64,2048]{1,0:T(8,128)}) %reduce-scatter.7.cloned.1.call-update) | async-done | bytes 524304 | tf_op jit(solution)/shard_map/reduce_scatter | solution.py:111
  331.3 1.1 add_convert_fusion.2
  332.4 6.8 %all_gather.38 = bf16[128,2048]{1,0:T(8,128)(2,1)S(1)} all-gather(bf16[32,2048]{1,0:T(8,128)(2,1)S(1)} %get-tuple-element.13), channel_id=1, replica_groups=mesh['narrow'=4,'wide'=8] {'narrow'}, dimensions={0}, use_global_device_ids=true | all-gather | bytes 655360 | tf_op jit(solution)/shard_map/all_gather | solution.py:82
  339.2 7.3 %all_gather.39 = bf16[128,2048]{1,0:T(8,128)(2,1)S(1)} all-gather(bf16[32,2048]{1,0:T(8,128)(2,1)S(1)} %get-tuple-element.14), channel_id=1, replica_groups=mesh['narrow'=4,'wide'=8] {'narrow'}, dimensions={0}, use_global_device_ids=true | all-gather | bytes 655360 | tf_op jit(solution)/shard_map/all_gather | solution.py:82
  346.6 8.2 %fusion.82 = f32[256,4096]{1,0:T(8,128)S(1)} fusion(bf16[256,2048]{1,0:T(8,128)(2,1)S(1)} %bitcast.72, bf16[2048,4096]{1,0:T(8,128)(2,1)} %bitcast.64), kind=kOutput, calls=%fused_computation.124 | convolution fusion | flops 4294967296 | bytes 22020096 | tf_op jit(solution)/shard_map/dot_general | solution.py:33
  354.7 0.7 fusion.83
  355.5 2.5 pad_maximum_fusion.1
  358.2 95.8 %reduce-scatter.9.cloned.1.call-done = f32[32,4608]{1,0:T(8,128)} async-done(((f32[256,4608]{1,0:T(8,128)}), f32[32,4608]{1,0:T(8,128)}) %reduce-scatter.9.cloned.1.call-update) | async-done | bytes 589840 | tf_op jit(solution)/shard_map/reduce_scatter | solution.py:35
  454.0 0.8 slice.120
  455.1 1.1 slice_bitcast_fusion
  456.3 0.2 subtract_convert_fusion
  456.5 12.2 %fusion.1 = (f32[32,2,16]{2,1,0:T(2,128)S(1)}, f32[32,2,16,1024]{3,2,1,0:T(8,128)}) fusion(pred[32,1024]{1,0:T(8,128)(4,1)S(1)} %iota_compare_fusion, bf16[32,2,1024,128]{3,2,1,0:T(8,128)(2,1)} %param.11, bf16[32,2,16,64]{3,2,1,0:T(8,128)(2,1)S(1)} %get-tuple-element.6, bf16[32,2,16,64]{3,2,1,0:T(8,128)(2,1)S(1)} %get-tuple-element.5), kind=kOutput, calls=%fused_computation.9 | convolution fusion | flops 272104448 | bytes 21270528 | tf_op jit(solution)/shard_map/rgjd,rgcd->rgjc/dot_general | solution.py:50
  468.7 0.5 fusion.79
  469.3 0.1 fusion.40
  469.4 3.9 fusion.3
  473.4 7.3 %fusion.5 = f32[32,2,16,128]{3,2,1,0:T(8,128)S(1)} fusion(bf16[32,2,1024,128]{3,2,1,0:T(8,128)(2,1)} %param.12, f32[32,2,16,1024]{3,2,1,0:T(8,128)S(1)} %copy-done, f32[32,2,16]{2,1,0:T(2,128)S(1)} %add.59, f32[32,2,16]{2,1,0:T(2,128)S(1)} %max.13, pred[32,1024]{1,0:T(8,128)(4,1)S(1)} %iota_compare_fusion), kind=kOutput, calls=%fused_computation.13 | convolution fusion | flops 274726912 | bytes 21536768 | tf_op jit(solution)/shard_map/rgjc,rgcd->rgjd/dot_general | solution.py:62
  480.8 0.3 fusion.36
  481.1 0.1 copy.103
  481.2 31.5 %all_gather.40 = bf16[256,1024]{1,0:T(8,128)(2,1)S(1)} all-gather(bf16[32,1024]{1,0:T(8,128)(2,1)S(1)} %get-tuple-element.9), channel_id=1, replica_groups=mesh['narrow'=4,'wide'=8] {'wide'}, dimensions={0}, use_global_device_ids=true | all-gather | bytes 589824 | tf_op jit(solution)/shard_map/all_gather | solution.py:68
  512.7 31.3 %all_gather.41 = bf16[256,1024]{1,0:T(8,128)(2,1)S(1)} all-gather(bf16[32,1024]{1,0:T(8,128)(2,1)S(1)} %get-tuple-element.12), channel_id=1, replica_groups=mesh['narrow'=4,'wide'=8] {'wide'}, dimensions={0}, use_global_device_ids=true | all-gather | bytes 589824 | tf_op jit(solution)/shard_map/all_gather | solution.py:68
  544.1 31.6 %all_gather.42 = bf16[256,1024]{1,0:T(8,128)(2,1)S(1)} all-gather(bf16[32,1024]{1,0:T(8,128)(2,1)S(1)} %get-tuple-element.11), channel_id=1, replica_groups=mesh['narrow'=4,'wide'=8] {'wide'}, dimensions={0}, use_global_device_ids=true | all-gather | bytes 589824 | tf_op jit(solution)/shard_map/all_gather | solution.py:68
  575.7 31.2 %all_gather.43 = bf16[256,1024]{1,0:T(8,128)(2,1)S(1)} all-gather(bf16[32,1024]{1,0:T(8,128)(2,1)S(1)} %get-tuple-element.10), channel_id=1, replica_groups=mesh['narrow'=4,'wide'=8] {'wide'}, dimensions={0}, use_global_device_ids=true | all-gather | bytes 589824 | tf_op jit(solution)/shard_map/all_gather | solution.py:68
  606.8 10.2 %fusion.14 = f32[256,2048]{1,0:T(8,128)} fusion(bf16[4096,2048]{1,0:T(8,128)(2,1)} %param.10, bf16[256,1024]{1,0:T(8,128)(2,1)S(1)} %all_gather.43, bf16[256,1024]{1,0:T(8,128)(2,1)S(1)} %all_gather.42, bf16[256,1024]{1,0:T(8,128)(2,1)S(1)} %all_gather.41, bf16[256,1024]{1,0:T(8,128)(2,1)S(1)} %all_gather.40), kind=kOutput, calls=%fused_computation.22 | convolution fusion | flops 4303355904 | bytes 20971520 | tf_op jit(solution)/shard_map/dot_general | solution.py:65
  617.0 31.4 %reduce-scatter.11.cloned.1.call-done = f32[64,2048]{1,0:T(8,128)} async-done(((f32[256,2048]{1,0:T(8,128)}), f32[64,2048]{1,0:T(8,128)}) %reduce-scatter.11.cloned.1.call-update) | async-done | bytes 524304 | tf_op jit(solution)/shard_map/reduce_scatter | solution.py:111
  648.4 1.8 add_convert_fusion
  (51 shorter events, 1.4 us)
Async XLA Ops:
  6.5 21.8 %all-gather.2.cloned.1.call-start = ((), (), s32[]{:S(2)}) async-start(), calls=%async_computation.4 | async-start | bytes 1310720 | tf_op jit(solution)/shard_map/all_gather | solution.py:98
  7.3 130.4 %reduce-scatter.5.cloned.1.call-start = ((), (), s32[]{:S(2)}) async-start(), calls=%async_computation.5 | async-start | bytes 5308416 | tf_op jit(solution)/shard_map/reduce_scatter | solution.py:35
  7.3 17.5 %copy-start.2 = (bf16[2048,2,256]{2,1,0:T(2,128)(2,1)S(1)}, bf16[2048,2,256]{2,1,0:T(2,128)(2,1)}, u32[]{:S(2)}) copy-start(bf16[2048,2,256]{2,1,0:T(2,128)(2,1)} %param.9) | copy-start | bytes 6291460
  28.4 10.5 %copy-start.5 = (bf16[256,2048]{1,0:T(8,128)(2,1)S(1)}, bf16[256,2048]{1,0:T(8,128)(2,1)}, u32[]{:S(2)}) copy-start(bf16[256,2048]{1,0:T(8,128)(2,1)} %all-gather.2.cloned.1.call-done) | copy-start | bytes 3145732
  42.1 0.7 copy-start.4
  42.2 289.1 %reduce-scatter.7.cloned.1.call-start = ((), (), s32[]{:S(2)}) async-start(), calls=%async_computation.6 | async-start | bytes 2621440 | tf_op jit(solution)/shard_map/reduce_scatter | solution.py:111
  152.8 3.9 copy-start.1
  289.9 41.4 %copy-start.3 = (bf16[64,2048]{1,0:T(8,128)(2,1)S(1)}, bf16[64,2048]{1,0:T(8,128)(2,1)}, u32[]{:S(2)}) copy-start(bf16[64,2048]{1,0:T(8,128)(2,1)} %param.7) | copy-start | bytes 786436
  300.1 153.8 %reduce-scatter.9.cloned.1.call-start = ((), (), s32[]{:S(2)}) async-start(), calls=%async_computation.7 | async-start | bytes 5308416 | tf_op jit(solution)/shard_map/reduce_scatter | solution.py:35
  358.0 290.4 %reduce-scatter.11.cloned.1.call-start = ((), (), s32[]{:S(2)}) async-start(), calls=%async_computation.8 | async-start | bytes 2621440 | tf_op jit(solution)/shard_map/reduce_scatter | solution.py:111
  468.7 4.7 copy-start
Sparse Core Ops, SparseCore 0:
  8.9 19.4 all-gather.1
  42.3 95.3 reduce-scatter.4
  300.3 30.9 reduce-scatter.6
  358.1 95.7 reduce-scatter.8
  617.2 31.1 reduce-scatter.10

commit v12 on v10

--- a/solution.py
+++ b/solution.py
@@ -71,12 +71,13 @@
 
 def narrow_gather(state, n_narrow):
     rows, cols = state.shape
-    half = rows // 2
+    pieces = 4
+    half = rows // pieces
     parts = [
         lax.all_gather(state[h * half : (h + 1) * half], "narrow", axis=0, tiled=True).reshape(
             n_narrow, 1, half, cols
         )
-        for h in range(2)
+        for h in range(pieces)
     ]
     return jnp.concatenate(parts, axis=1).reshape(n_narrow * rows, cols)
 

time: 508 us -> 517 us (1.018)
  blocking collectives: 14 us -> 23.3 us
    all_gather x2 -> x4, blocking collectives: 14 us -> 23.3 us  [narrow_gather(): lax.all_gather(state[h * half:(h + 1) * half], 'narrow', axis=0, tiled=True)]
where the time goes in v12:
time: 517 us; the launch traced here: 516 us
  waiting for transfers between devices  352 us (68%)
  matrix products  85 us (16%)
  local copies, waits for them, and re-layouts  24.7 us (5%)
  blocking collectives  23.3 us (5%)
  other arithmetic  16.9 us (3%)
  between operations  13.8 us (3%)
    reduce_scatter x2, waiting for transfers between devices, attend_step(): lax.psum_scatter(jnp.concatenate((part_q, part_kv), axis=1), 'wide', scat...  190 us
    all_gather x2, waiting for transfers between devices, attend_step(): lax.all_gather(attended, 'wide', axis=0, tiled=True)  98.1 us
    reduce_scatter x2, waiting for transfers between devices, on_device(): lax.psum_scatter(partial_value, 'narrow', scatter_dimension=0, tiled=True)  60.1 us
    dot_general x2, matrix products, attend_step(): jnp.einsum('rgjd,rgcd->rgjc', query, key_cache, preferred_element_type=jn...  24.5 us
    dot_general x2, matrix products, attend_step(): jnp.dot(lax.all_gather(attended, 'wide', axis=0, tiled=True), w_out, pref...  24.4 us
    all_gather x4, blocking collectives, narrow_gather(): lax.all_gather(state[h * half:(h + 1) * half], 'narrow', axis=0, tiled=True)  23.3 us
    unnamed x21, local copies, waits for them, and re-layouts  22.5 us
    dot_general x2, matrix products, attend_step(): part_q = jnp.dot(every, w_q2, preferred_element_type=jnp.float32)  18.6 us
  transfers between devices with their start and end apart: 7, of which 7 were waited for; matrix products, arithmetic and copies ran while one was open for 4% of the time, Pallas kernels for 0%

profile of v12, /device:TPU:0, one launch (start us, length us, event | category | flops | bytes accessed | tf_op | source)
XLA Modules:
  0.0 516.2 jit_solution(14633697596700805299)
XLA Ops:
  6.5 0.7 all-gather.4.cloned.1.call-update
  7.3 17.5 %copy.79 = bf16[256,8,2,2048]{3,1,2,0:T(8,128)(2,1)} copy(bf16[256,8,2,2048]{3,2,1,0:T(2,128)(2,1)} %bitcast.70) | data formatting | bytes 33554432
  24.8 0.5 copy.80
  25.3 3.1 all-gather.4.cloned.1.call-done
  28.4 10.5 %fusion.60 = f32[256,4096]{1,0:T(8,128)S(1)} fusion(bf16[256,2048]{1,0:T(8,128)(2,1)} %all-gather.4.cloned.1.call-done, bf16[2048,4096]{1,0:T(8,128)(2,1)} %bitcast.71), kind=kOutput, calls=%fused_computation.102 | convolution fusion | flops 4294967296 | bytes 22020096 | tf_op jit(solution)/shard_map/dot_general | solution.py:33
  38.9 0.7 fusion.61
  39.6 2.5 pad_maximum_fusion
  42.2 0.6 copy-done.4
  42.9 0.2 multiply_cosine_fusion
  43.1 94.6 %reduce-scatter.5.cloned.1.call-done = f32[32,4608]{1,0:T(8,128)} async-done(((f32[256,4608]{1,0:T(8,128)}), f32[32,4608]{1,0:T(8,128)}) %reduce-scatter.5.cloned.1.call-update) | async-done | bytes 589840 | tf_op jit(solution)/shard_map/reduce_scatter | solution.py:35
  137.7 0.8 slice.83
  138.7 1.1 slice_bitcast_fusion.1
  139.9 0.2 subtract_convert_fusion.1
  140.2 0.3 fusion.22
  140.5 12.2 %fusion = (f32[32,2,16]{2,1,0:T(2,128)S(1)}, f32[32,2,16,1024]{3,2,1,0:T(8,128)}) fusion(pred[32,1024]{1,0:T(8,128)(4,1)S(1)} %iota_compare_fusion, bf16[32,2,1024,128]{3,2,1,0:T(8,128)(2,1)} %param.11, bf16[32,2,16,64]{3,2,1,0:T(8,128)(2,1)S(1)} %get-tuple-element.8, bf16[32,2,16,64]{3,2,1,0:T(8,128)(2,1)S(1)} %get-tuple-element.7), kind=kOutput, calls=%fused_computation.8 | convolution fusion | flops 272104448 | bytes 21270528 | tf_op jit(solution)/shard_map/rgjd,rgcd->rgjc/dot_general | solution.py:50
  152.8 3.8 fusion.2
  156.7 7.5 %fusion.19 = bf16[32,2,16,128]{3,2,1,0:T(8,128)(2,1)S(1)} fusion(bf16[32,2,1024,128]{3,2,1,0:T(8,128)(2,1)} %param.12, f32[32,2,16,1024]{3,2,1,0:T(8,128)S(1)} %copy-done.1, f32[32,2,16]{2,1,0:T(2,128)S(1)} %get-tuple-element.16, f32[32,2,16]{2,1,0:T(2,128)S(1)} %multiply_maximum_fusion, pred[32,1024]{1,0:T(8,128)(4,1)S(1)} %iota_compare_fusion, ...), kind=kOutput, calls=%fused_computation.28 | convolution fusion | flops 275120128 | bytes 21311488 | tf_op jit(solution)/shard_map/rgjc,rgcd->rgjd/dot_general | solution.py:62
  164.2 0.8 copy.114
  165.1 0.2 reduce-scatter.7.cloned.1.call-start
  165.3 49.0 %all-gather.6.cloned.1.call-done = bf16[256,4096]{1,0:T(8,128)(2,1)} async-done(((bf16[32,4096]{1,0:T(8,128)(2,1)}), bf16[256,4096]{1,0:T(8,128)(2,1)}) %all-gather.6.cloned.1.call-update) | async-done | bytes 2097168 | tf_op jit(solution)/shard_map/all_gather | solution.py:66
  214.3 12.2 %fusion.62 = f32[256,2048]{1,0:T(8,128)} fusion(bf16[256,4096]{1,0:T(8,128)(2,1)} %all-gather.6.cloned.1.call-done, bf16[4096,2048]{1,0:T(8,128)(2,1)} %param.10), kind=kOutput, calls=%fused_computation.104 | convolution fusion | flops 4294967296 | bytes 20971520 | tf_op jit(solution)/shard_map/dot_general | solution.py:65
  226.6 30.0 %reduce-scatter.7.cloned.1.call-done = f32[64,2048]{1,0:T(8,128)} async-done(((f32[256,2048]{1,0:T(8,128)}), f32[64,2048]{1,0:T(8,128)}) %reduce-scatter.7.cloned.1.call-update) | async-done | bytes 524304 | tf_op jit(solution)/shard_map/reduce_scatter | solution.py:106
  256.6 1.1 add_convert_fusion.2
  257.7 5.8 %all_gather.26 = bf16[64,2048]{1,0:T(8,128)(2,1)S(1)} all-gather(bf16[16,2048]{1,0:T(8,128)(2,1)S(1)} %get-tuple-element.10), channel_id=1, replica_groups=mesh['narrow'=4,'wide'=8] {'narrow'}, dimensions={0}, use_global_device_ids=true | all-gather | bytes 327680 | tf_op jit(solution)/shard_map/all_gather | solution.py:77
  263.5 5.8 %all_gather.23 = bf16[64,2048]{1,0:T(8,128)(2,1)S(1)} all-gather(bf16[16,2048]{1,0:T(8,128)(2,1)S(1)} %get-tuple-element.9), channel_id=1, replica_groups=mesh['narrow'=4,'wide'=8] {'narrow'}, dimensions={0}, use_global_device_ids=true | all-gather | bytes 327680 | tf_op jit(solution)/shard_map/all_gather | solution.py:77
  269.4 5.8 %all_gather.24 = bf16[64,2048]{1,0:T(8,128)(2,1)S(1)} all-gather(bf16[16,2048]{1,0:T(8,128)(2,1)S(1)} %get-tuple-element.12), channel_id=1, replica_groups=mesh['narrow'=4,'wide'=8] {'narrow'}, dimensions={0}, use_global_device_ids=true | all-gather | bytes 327680 | tf_op jit(solution)/shard_map/all_gather | solution.py:77
  275.2 5.8 %all_gather.25 = bf16[64,2048]{1,0:T(8,128)(2,1)S(1)} all-gather(bf16[16,2048]{1,0:T(8,128)(2,1)S(1)} %get-tuple-element.11), channel_id=1, replica_groups=mesh['narrow'=4,'wide'=8] {'narrow'}, dimensions={0}, use_global_device_ids=true | all-gather | bytes 327680 | tf_op jit(solution)/shard_map/all_gather | solution.py:77
  281.1 0.1 pad_maximum_fusion.2
  281.2 8.2 %fusion.63 = f32[256,4096]{1,0:T(8,128)S(1)} fusion(bf16[256,2048]{1,0:T(8,128)(2,1)S(1)} %bitcast.78, bf16[2048,4096]{1,0:T(8,128)(2,1)} %bitcast.72), kind=kOutput, calls=%fused_computation.105 | convolution fusion | flops 4294967296 | bytes 22020096 | tf_op jit(solution)/shard_map/dot_general | solution.py:33
  289.4 0.7 fusion.64
  290.1 2.5 pad_maximum_fusion.1
  292.7 0.3 all-gather.8.cloned.1.call-start
  293.0 95.0 %reduce-scatter.9.cloned.1.call-done = f32[32,4608]{1,0:T(8,128)} async-done(((f32[256,4608]{1,0:T(8,128)}), f32[32,4608]{1,0:T(8,128)}) %reduce-scatter.9.cloned.1.call-update) | async-done | bytes 589840 | tf_op jit(solution)/shard_map/reduce_scatter | solution.py:35
  388.1 0.8 slice.94
  389.2 1.1 slice_bitcast_fusion
  390.3 0.1 copy.83
  390.4 0.2 subtract_convert_fusion
  390.6 12.3 %fusion.1 = (f32[32,2,16]{2,1,0:T(2,128)S(1)}, f32[32,2,16,1024]{3,2,1,0:T(8,128)}) fusion(pred[32,1024]{1,0:T(8,128)(4,1)S(1)} %iota_compare_fusion, bf16[32,2,1024,128]{3,2,1,0:T(8,128)(2,1)} %param.11, bf16[32,2,16,64]{3,2,1,0:T(8,128)(2,1)S(1)} %get-tuple-element.6, bf16[32,2,16,64]{3,2,1,0:T(8,128)(2,1)S(1)} %get-tuple-element.5), kind=kOutput, calls=%fused_computation.9 | convolution fusion | flops 272104448 | bytes 21270528 | tf_op jit(solution)/shard_map/rgjd,rgcd->rgjc/dot_general | solution.py:50
  402.9 0.5 fusion.59
  403.4 0.1 fusion.24
  403.6 3.9 fusion.3
  407.6 7.3 %fusion.5 = f32[32,2,16,128]{3,2,1,0:T(8,128)S(1)} fusion(bf16[32,2,1024,128]{3,2,1,0:T(8,128)(2,1)} %param.12, f32[32,2,16,1024]{3,2,1,0:T(8,128)S(1)} %copy-done, f32[32,2,16]{2,1,0:T(2,128)S(1)} %add.59, f32[32,2,16]{2,1,0:T(2,128)S(1)} %max.13, pred[32,1024]{1,0:T(8,128)(4,1)S(1)} %iota_compare_fusion), kind=kOutput, calls=%fused_computation.13 | convolution fusion | flops 274726912 | bytes 21536768 | tf_op jit(solution)/shard_map/rgjc,rgcd->rgjd/dot_general | solution.py:62
  414.9 0.3 fusion.20
  415.2 0.8 copy.113
  416.1 49.2 %all-gather.8.cloned.1.call-done = bf16[256,4096]{1,0:T(8,128)(2,1)} async-done(((bf16[32,4096]{1,0:T(8,128)(2,1)}), bf16[256,4096]{1,0:T(8,128)(2,1)}) %all-gather.8.cloned.1.call-update) | async-done | bytes 2097168 | tf_op jit(solution)/shard_map/all_gather | solution.py:66
  465.3 12.2 %fusion.65 = f32[256,2048]{1,0:T(8,128)} fusion(bf16[256,4096]{1,0:T(8,128)(2,1)} %all-gather.8.cloned.1.call-done, bf16[4096,2048]{1,0:T(8,128)(2,1)} %param.10), kind=kOutput, calls=%fused_computation.107 | convolution fusion | flops 4294967296 | bytes 20971520 | tf_op jit(solution)/shard_map/dot_general | solution.py:65
  477.5 30.1 %reduce-scatter.11.cloned.1.call-done = f32[64,2048]{1,0:T(8,128)} async-done(((f32[256,2048]{1,0:T(8,128)}), f32[64,2048]{1,0:T(8,128)}) %reduce-scatter.11.cloned.1.call-update) | async-done | bytes 524304 | tf_op jit(solution)/shard_map/reduce_scatter | solution.py:106
  507.6 1.8 add_convert_fusion
  (49 shorter events, 1.2 us)
Async XLA Ops:
  6.5 21.8 %all-gather.4.cloned.1.call-start = ((), (), s32[]{:S(2)}) async-start(), calls=%async_computation.4 | async-start | bytes 1310720 | tf_op jit(solution)/shard_map/all_gather | solution.py:93
  7.3 130.4 %reduce-scatter.5.cloned.1.call-start = ((), (), s32[]{:S(2)}) async-start(), calls=%async_computation.5 | async-start | bytes 5308416 | tf_op jit(solution)/shard_map/reduce_scatter | solution.py:35
  7.3 17.5 %copy-start.2 = (bf16[2048,2,256]{2,1,0:T(2,128)(2,1)S(1)}, bf16[2048,2,256]{2,1,0:T(2,128)(2,1)}, u32[]{:S(2)}) copy-start(bf16[2048,2,256]{2,1,0:T(2,128)(2,1)} %param.9) | copy-start | bytes 6291460
  28.4 10.5 %copy-start.5 = (bf16[256,2048]{1,0:T(8,128)(2,1)S(1)}, bf16[256,2048]{1,0:T(8,128)(2,1)}, u32[]{:S(2)}) copy-start(bf16[256,2048]{1,0:T(8,128)(2,1)} %all-gather.4.cloned.1.call-done) | copy-start | bytes 3145732
  42.1 0.7 copy-start.4
  42.2 172.1 %all-gather.6.cloned.1.call-start = ((), (), s32[]{:S(2)}) async-start(), calls=%async_computation.6 | async-start | bytes 2359296 | tf_op jit(solution)/shard_map/all_gather | solution.py:66
  152.8 3.9 copy-start.1
  165.1 91.5 %copy-start.3 = (bf16[64,2048]{1,0:T(8,128)(2,1)S(1)}, bf16[64,2048]{1,0:T(8,128)(2,1)}, u32[]{:S(2)}) copy-start(bf16[64,2048]{1,0:T(8,128)(2,1)} %param.7) | copy-start | bytes 786436
  165.1 91.5 %reduce-scatter.7.cloned.1.call-start = ((), (), s32[]{:S(2)}) async-start(), calls=%async_computation.7 | async-start | bytes 2621440 | tf_op jit(solution)/shard_map/reduce_scatter | solution.py:106
  226.5 161.6 %reduce-scatter.9.cloned.1.call-start = ((), (), s32[]{:S(2)}) async-start(), calls=%async_computation.8 | async-start | bytes 5308416 | tf_op jit(solution)/shard_map/reduce_scatter | solution.py:35
  292.7 172.6 %all-gather.8.cloned.1.call-start = ((), (), s32[]{:S(2)}) async-start(), calls=%async_computation.9 | async-start | bytes 2359296 | tf_op jit(solution)/shard_map/all_gather | solution.py:66
  402.9 4.7 copy-start
  416.1 91.5 %reduce-scatter.11.cloned.1.call-start = ((), (), s32[]{:S(2)}) async-start(), calls=%async_computation.10 | async-start | bytes 2621440 | tf_op jit(solution)/shard_map/reduce_scatter | solution.py:106
Sparse Core Ops, SparseCore 0:
  8.9 19.4 all-gather.3
  42.3 95.3 reduce-scatter.4
  165.2 49.0 all-gather.5
  226.6 29.9 reduce-scatter.6
  292.8 95.2 reduce-scatter.8
  416.2 49.0 all-gather.7
  477.6 29.9 reduce-scatter.10
